TPU v7x, 256 devices: a whole 4x4x8 slice. The times are simulated.
256 devices in a mesh: seq: 16 (over z_hi, y), head: 16 (over x, z_lo, core).
Axes of the slice: x: 4, y: 4, z: 8 (z_hi: 4, z_lo: 2; z = z_hi * 2 + z_lo), core: 2. Of those that a mesh axis runs over, the one named last changes fastest.
Arguments:
- queries: bfloat16 [8192, 4096], P('seq', 'head'), may hold values from -40 to 40
- stretch_keys: bfloat16 [8192, 4096], P('seq', 'head'), may hold values from -6 to 6
- stretch_values: bfloat16 [8192, 4096], P('seq', 'head'), may hold values from -6 to 6
- segment_ids: int32 [8192], replicated, may hold values from 0 to 7, never falling along the last dimension, each value on 1 to 6144 neighbouring positions
- block_live: int32 [16, 16], replicated, may hold values 0 or 1
- out_weight: bfloat16 [4096, 7168], P('head'), may hold values from -0.09375 to 0.09375
- cache_keys: bfloat16 [4, 8192, 4096], P(None, 'seq', 'head'), may hold values from -6 to 6
- cache_values: bfloat16 [4, 8192, 4096], P(None, 'seq', 'head'), may hold values from -6 to 6
- page_table: int32 [512], replicated, may hold values from 0 to 511, as said below
Outputs:
- attn_out: bfloat16 [8192, 4096], P('seq', 'head')
- proj_out: bfloat16 [8192, 7168], P(('seq', 'head'))
- decode_keys: bfloat16 [4, 512, 16, 4096], P(None, 'seq', None, 'head')
- decode_values: bfloat16 [4, 512, 16, 4096], P(None, 'seq', None, 'head')
Inputs may be any that keep to these rules, and one draw needn't show every extreme that they name: page_table holds each of 0 to 511 once; the slot s belongs to request group s // 32; each aligned run of 2 pages of one token block goes to one group, and the 16 runs of one token block go to 16 different groups.
All inputs are finite; a program needn't handle non-finite values.
Results may differ from a plain program's by a relative error of at most 0.018.
Values may be sent and summed in bfloat16 or wider, within the bound.
No kernel may reach another device: no remote copies, remote signals or barrier semaphores. Data moves between devices by JAX's collectives and lax.ppermute only.
A program may use at most 128 MiB of HBM per device.

v0:
```python
import math

import jax
import jax.numpy as jnp
from jax import lax
from jax.sharding import PartitionSpec as P

HD = 128


def relayout(cache_keys, cache_values, page_table):
    position = lax.axis_index("seq")
    groups = lax.axis_size("seq")
    layers, block_rows, feat_width = cache_keys.shape
    page_count = page_table.shape[0] // groups
    page_len = block_rows // page_count
    per_group = page_count // groups
    slot_table = page_table.reshape(groups, page_count)
    own_slots = lax.dynamic_index_in_dim(slot_table, position, 0, keepdims=False)
    ordering = jnp.argsort(own_slots // page_count, stable=True)

    def outgoing(cache):
        paged = cache.reshape(layers, page_count, page_len, feat_width)[:, ordering]
        return paged.reshape(layers, groups, per_group, page_len, feat_width)

    moved_keys, moved_values = (
        lax.all_to_all(outgoing(cache_keys), "seq", split_axis=1, concat_axis=1, tiled=True),
        lax.all_to_all(outgoing(cache_values), "seq", split_axis=1, concat_axis=1, tiled=True),
    )
    to_here = jnp.where(slot_table // page_count == position, 0, 1)
    picked = jnp.argsort(to_here, axis=1, stable=True)[:, :per_group]
    slot_ids = jnp.take_along_axis(slot_table, picked, axis=1) % page_count
    inverse = jnp.argsort(slot_ids.reshape(-1))

    def placed(moved):
        return moved.reshape(layers, page_count, page_len, feat_width)[:, inverse]

    return (placed(moved_keys), placed(moved_values))


def attention(queries, stretch_keys, stretch_values, segment_ids, block_live):
    position = lax.axis_index("seq")
    block_count = lax.axis_size("seq")
    block_rows, feat_width = queries.shape
    head_count = feat_width // HD
    score_scale = 1.0 / math.sqrt(HD)
    query_start = position * block_rows
    live_row = lax.dynamic_index_in_dim(block_live, position, 0, keepdims=False)
    query_seg = lax.dynamic_slice_in_dim(segment_ids, query_start, block_rows)
    query_pos = query_start + jnp.arange(block_rows, dtype=jnp.int32)
    query_heads = queries.reshape(block_rows, head_count, HD)
    block_ids = jnp.arange(block_count, dtype=jnp.int32)
    initial = (
        jnp.zeros((head_count, block_rows, HD), jnp.float32),
        jnp.full((head_count, block_rows), -jnp.inf, jnp.float32),
        jnp.zeros((head_count, block_rows), jnp.float32),
    )
    key_piece = lax.all_gather(stretch_keys, "seq", axis=0, tiled=True)
    value_piece = lax.all_gather(stretch_values, "seq", axis=0, tiled=True)
    piece_rows = key_piece.shape[0]
    key_pos = jnp.arange(piece_rows, dtype=jnp.int32)
    key_block = key_pos // block_rows
    earlier_live = jnp.any(
        (key_block[:, None] == block_ids[None, :]) & (live_row[None, :] == 1), axis=1
    )
    column_live = (key_block == position) | (key_block < position) & (key_pos >= 0) & earlier_live
    allowed = (
        (query_seg[:, None] == segment_ids[None, :])
        & (key_pos[None, :] <= query_pos[:, None])
        & column_live[None, :]
    )

    def compute(state_now):
        numerator, row_best, weight_sum = state_now
        key_heads = key_piece.reshape(piece_rows, head_count, HD)
        value_heads = value_piece.reshape(piece_rows, head_count, HD)
        scores = (
            jnp.einsum("qhd,khd->hqk", query_heads, key_heads, preferred_element_type=jnp.float32)
            * score_scale
        )
        scores = jnp.where(allowed[None], scores, -jnp.inf)
        new_max = jnp.max(scores, axis=-1)
        safe_max = jnp.where(jnp.isfinite(new_max), new_max, 0.0)
        rescale = jnp.exp(row_best - safe_max)
        weights = jnp.exp(scores - safe_max[..., None])
        weight_sum = weight_sum * rescale + jnp.sum(weights, axis=-1)
        added = jnp.einsum(
            "hqk,khd->hqd",
            weights.astype(jnp.bfloat16),
            value_heads,
            preferred_element_type=jnp.float32,
        )
        numerator = numerator * rescale[..., None] + added
        return (numerator, new_max, weight_sum)

    numerator, row_best, weight_sum = lax.cond(
        jnp.any(allowed), compute, lambda unchanged: unchanged, initial
    )
    attended = numerator / weight_sum[..., None]
    return jnp.transpose(attended, (1, 0, 2)).reshape(block_rows, feat_width).astype(jnp.bfloat16)


def local(
    queries,
    stretch_keys,
    stretch_values,
    segment_ids,
    block_live,
    out_weight,
    cache_keys,
    cache_values,
    page_table,
):
    decode_keys, decode_values = relayout(cache_keys, cache_values, page_table)
    attended = attention(queries, stretch_keys, stretch_values, segment_ids, block_live)
    projected = lax.psum_scatter(
        jnp.dot(attended, out_weight, preferred_element_type=jnp.float32).astype(jnp.bfloat16),
        "head",
        scatter_dimension=0,
        tiled=True,
    )
    return (attended, projected, decode_keys, decode_values)


def solution(mesh):
    placed = (
        P("seq", "head"),
        P("seq", "head"),
        P("seq", "head"),
        P(),
        P(),
        P("head", None),
        P(None, "seq", "head"),
        P(None, "seq", "head"),
        P(),
    )
    return jax.shard_map(
        local,
        mesh=mesh,
        in_specs=placed,
        out_specs=(
            P("seq", "head"),
            P(("seq", "head"), None),
            P(None, "seq", None, "head"),
            P(None, "seq", None, "head"),
        ),
        check_vma=False,
    )
```

profile of v0, /device:TPU:8, one launch (start us, length us, event | category | flops | bytes accessed | tf_op | source)
XLA Modules:
  0.0 364.7 jit_solution(11860897653675955476)
XLA Ops:
  7.2 0.0 copy-start
  7.2 0.0 all-gather.3.cloned.1.call-start
  7.2 0.7 all-gather.3.cloned.1.call-update
  7.9 0.0 all-gather.5.cloned.1.call-start
  8.0 0.7 all-gather.5.cloned.1.call-update
  8.7 0.0 reduce-scatter.2.cloned.1.call-start
  8.7 0.8 dynamic_slice.11
  9.5 0.7 compare_bitcast_fusion
  10.2 0.2 fusion.24
  10.4 8.4 %fusion.34 = (pred[]{:T(512)}, pred[512,8192]{1,0:T(8,128)(4,1)}) fusion(pred[8192]{0:T(1024)(128)(4,1)S(1)} %and_or_fusion, s32[512]{0:T(512)S(1)} %iota_add_fusion, s32[8192]{0:T(1024)} %param.14, s32[512]{0:T(512)S(1)} %dynamic_slice.11), kind=kLoop, calls=%fused_computation.70 | loop fusion | flops 20971520 | bytes 4239361 | tf_op jit(solution)/shard_map/reduce_or | solution.py:97
  19.4 69.8 %all-gather.3.cloned.1.call-done = bf16[8192,256]{1,0:T(8,128)(2,1)} async-done(((bf16[512,256]{1,0:T(8,128)(2,1)}), bf16[8192,256]{1,0:T(8,128)(2,1)}) %all-gather.3.cloned.1.call-update) | async-done | bytes 4194320 | tf_op jit(solution)/shard_map/all_gather | solution.py:58
  89.3 78.2 %all-gather.5.cloned.1.call-done = bf16[8192,256]{1,0:T(8,128)(2,1)} async-done(((bf16[512,256]{1,0:T(8,128)(2,1)}), bf16[8192,256]{1,0:T(8,128)(2,1)}) %all-gather.5.cloned.1.call-update) | async-done | bytes 4194320 | tf_op jit(solution)/shard_map/all_gather | solution.py:59
  167.5 48.5 %conditional.1 = (f32[2,512,128]{2,1,0:T(8,128)S(1)}, f32[2,512]{1,0:T(2,128)S(1)}) conditional(s32[]{:T(128)} %convert_element_type.18, () %tuple.16, (pred[512,8192]{1,0:T(8,128)(4,1)}, bf16[512,256]{1,0:T(8,128)(2,1)}, bf16[8192,256]{1,0:T(8,128)(2,1)}, bf16[8192,256]{1,0:T(8,128)(2,1)}) %tuple.17), branch_computations={%region_2.3_spmd, %region_3.6_spmd} | conditional | flops 4387378176 | bytes 139243568 | solution.py:96
  167.5 16.6 %fusion = (f32[2,512]{1,0:T(2,128)S(1)}, f32[2,512,8192]{2,1,0:T(8,128)}) fusion(pred[512,8192]{1,0:T(8,128)(4,1)} %get-tuple-element.9, bf16[8192,256]{1,0:T(8,128)(2,1)} %get-tuple-element.11, bf16[512,256]{1,0:T(8,128)(2,1)} %get-tuple-element.28), kind=kOutput, calls=%fused_computation.7 | convolution fusion | flops 2172648448 | bytes 42209280 | tf_op jit(solution)/shard_map/cond/branch_1_fun/qhd,khd->hqk/dot_general | solution.py:78
  184.1 16.0 %fusion.1 = f32[2,512]{1,0:T(2,128)S(1)} fusion(f32[2,512,8192]{2,1,0:T(8,128)} %get-tuple-element.54, f32[2,512]{1,0:T(2,128)S(1)} %is-finite_select_fusion, pred[512,8192]{1,0:T(8,128)(4,1)} %get-tuple-element.9), kind=kLoop, calls=%fused_computation.8 | loop fusion | flops 33553408 | bytes 37756928 | tf_op jit(solution)/shard_map/cond/branch_1_fun/reduce_sum | solution.py:86
  200.1 15.7 %fusion.11 = f32[2,512,128]{2,1,0:T(8,128)S(1)} fusion(f32[2,512,8192]{2,1,0:T(8,128)} %get-tuple-element.54, f32[2,512]{1,0:T(2,128)S(1)} %is-finite_select_fusion, pred[512,8192]{1,0:T(8,128)(4,1)S(1)} %copy-done.1, f32[2,512]{1,0:T(2,128)S(1)} %get-tuple-element.52, bf16[8192,256]{1,0:T(8,128)(2,1)} %get-tuple-element.12), kind=kOutput, calls=%fused_computation.17 | convolution fusion | flops 2181169152 | bytes 42475520 | tf_op jit(solution)/shard_map/cond/branch_1_fun/hqk,khd->hqd/dot_general | solution.py:87
  216.0 0.2 copy_bitcast_fusion
  216.2 0.0 copy-start.2
  216.2 0.0 copy-start.3
  216.2 7.2 %convolution_convert_fusion = bf16[512,7168]{1,0:T(8,128)(2,1)} fusion(bf16[512,256]{1,0:T(8,128)(2,1)S(1)} %copy_bitcast_fusion, bf16[256,7168]{1,0:T(8,128)(2,1)} %param.16), kind=kOutput, calls=%fused_computation.28 | convolution fusion | flops 1882718208 | bytes 11272192 | tf_op jit(solution)/shard_map/dot_general | solution.py:117
  223.4 0.0 reduce-scatter.2.cloned.1.call-update
  223.5 0.1 reshape.104
  223.6 0.1 copy.81
  223.7 0.8 sort.52
  224.5 0.1 copy.82
  224.6 0.1 reshape.143
  224.6 0.7 gather_fusion.4
  225.4 0.1 reshape.146
  225.4 0.1 copy.83
  225.5 0.1 copy.84
  225.6 0.1 select_n.92
  225.8 1.6 sort.51
  227.4 0.6 gather_fusion
  228.0 1.1 copy.79
  229.1 8.5 %all-to-all-start = ((bf16[4,16,2,16,256]{4,3,2,0,1:T(8,128)(2,1)}), bf16[4,16,2,16,256]{4,3,2,0,1:T(8,128)(2,1)S(1)}, u32[]{:S(2)}, u32[]{:S(2)}) async-start(bf16[4,16,2,16,256]{4,3,2,0,1:T(8,128)(2,1)} %copy.79), calls=%async_computation.1 | async-start | bytes 2097152 | tf_op jit(solution)/shard_map/all_to_all | solution.py:27
  237.7 1.8 gather_fusion.2
  239.5 1.2 copy.86
  240.7 36.9 %all-to-all-done = bf16[4,16,2,16,256]{4,3,2,0,1:T(8,128)(2,1)S(1)} async-done(((bf16[4,16,2,16,256]{4,3,2,0,1:T(8,128)(2,1)}), bf16[4,16,2,16,256]{4,3,2,0,1:T(8,128)(2,1)S(1)}, u32[]{:S(2)}, u32[]{:S(2)}) %all-to-all-start) | async-done | bytes 1048608 | tf_op jit(solution)/shard_map/all_to_all | solution.py:27
  277.6 5.5 %all-to-all-start.1 = ((bf16[4,16,2,16,256]{4,3,2,0,1:T(8,128)(2,1)}), bf16[4,16,2,16,256]{4,3,2,0,1:T(8,128)(2,1)}, u32[]{:S(2)}, u32[]{:S(2)}) async-start(bf16[4,16,2,16,256]{4,3,2,0,1:T(8,128)(2,1)} %copy.86), calls=%async_computation.2 | async-start | bytes 2097152 | tf_op jit(solution)/shard_map/all_to_all | solution.py:28
  283.1 1.6 sort.53
  284.7 0.1 copy.80
  284.8 0.6 gather_fusion.1
  285.5 1.1 copy.88
  286.5 36.3 %all-to-all-done.1 = bf16[4,16,2,16,256]{4,3,2,0,1:T(8,128)(2,1)} async-done(((bf16[4,16,2,16,256]{4,3,2,0,1:T(8,128)(2,1)}), bf16[4,16,2,16,256]{4,3,2,0,1:T(8,128)(2,1)}, u32[]{:S(2)}, u32[]{:S(2)}) %all-to-all-start.1) | async-done | bytes 1048608 | tf_op jit(solution)/shard_map/all_to_all | solution.py:28
  322.8 1.3 copy.87
  324.1 0.6 gather_fusion.3
  324.7 1.1 copy.89
  325.8 32.4 %reduce-scatter.2.cloned.1.call-done = bf16[32,7168]{1,0:T(8,128)(2,1)} async-done(((bf16[512,7168]{1,0:T(8,128)(2,1)}), bf16[32,7168]{1,0:T(8,128)(2,1)}) %reduce-scatter.2.cloned.1.call-update) | async-done | bytes 458768 | tf_op jit(solution)/shard_map/reduce_scatter | solution.py:116
  (21 shorter events, 0.1 us)
Async XLA Ops:
  7.2 220.2 %copy-start = (bf16[4,512,256]{2,1,0:T(8,128)(2,1)S(1)}, bf16[4,512,256]{2,1,0:T(8,128)(2,1)}, u32[]{:S(2)}) copy-start(bf16[4,512,256]{2,1,0:T(8,128)(2,1)} %param.17) | copy-start | bytes 3145732
  7.2 82.1 %all-gather.3.cloned.1.call-start = ((), (), s32[]{:S(2)}) async-start(), calls=%async_computation.3 | async-start | bytes 4456448 | tf_op jit(solution)/shard_map/all_gather | solution.py:58
  7.9 159.6 %all-gather.5.cloned.1.call-start = ((), (), s32[]{:S(2)}) async-start(), calls=%async_computation.4 | async-start | bytes 4456448 | tf_op jit(solution)/shard_map/all_gather | solution.py:59
  8.7 349.5 %reduce-scatter.2.cloned.1.call-start = ((), (), s32[]{:S(2)}) async-start(), calls=%async_computation.5 | async-start | bytes 7798784 | tf_op jit(solution)/shard_map/reduce_scatter | solution.py:116
  184.1 16.0 %copy-start.1 = (pred[512,8192]{1,0:T(8,128)(4,1)S(1)}, pred[512,8192]{1,0:T(8,128)(4,1)}, u32[]{:S(2)}) copy-start(pred[512,8192]{1,0:T(8,128)(4,1)} %get-tuple-element.9) | copy-start | bytes 12582916 | tf_op jit(solution)/shard_map/cond
  216.2 7.2 %copy-start.2 = (bf16[512,256]{1,0:T(8,128)(2,1)}, bf16[512,256]{1,0:T(8,128)(2,1)S(1)}, u32[]{:S(2)}) copy-start(bf16[512,256]{1,0:T(8,128)(2,1)S(1)} %copy_bitcast_fusion) | copy-start | bytes 786436
  216.2 7.2 %copy-start.3 = (s32[512]{0:T(512)S(1)}, s32[512]{0:T(512)}, u32[]{:S(2)}) copy-start(s32[512]{0:T(512)} %param.19) | copy-start | bytes 6148
  229.1 48.5 %all-to-all-start = ((bf16[4,16,2,16,256]{4,3,2,0,1:T(8,128)(2,1)}), bf16[4,16,2,16,256]{4,3,2,0,1:T(8,128)(2,1)S(1)}, u32[]{:S(2)}, u32[]{:S(2)}) async-start(bf16[4,16,2,16,256]{4,3,2,0,1:T(8,128)(2,1)} %copy.79), calls=%async_computation.1 | async-start | bytes 2097152 | tf_op jit(solution)/shard_map/all_to_all | solution.py:27
  277.6 45.2 %all-to-all-start.1 = ((bf16[4,16,2,16,256]{4,3,2,0,1:T(8,128)(2,1)}), bf16[4,16,2,16,256]{4,3,2,0,1:T(8,128)(2,1)}, u32[]{:S(2)}, u32[]{:S(2)}) async-start(bf16[4,16,2,16,256]{4,3,2,0,1:T(8,128)(2,1)} %copy.86), calls=%async_computation.2 | async-start | bytes 2097152 | tf_op jit(solution)/shard_map/all_to_all | solution.py:28
Sparse Core Ops, SparseCore 0:
  10.4 78.7 all-gather.2
  91.7 75.7 all-gather.4
  223.6 134.5 reduce-scatter.1
where the time goes:
time: 365 us
  waiting for transfers between devices  255 us (70%)
  matrix products  39.5 us (11%)
  other arithmetic  29.6 us (8%)
  between operations  14.6 us (4%)
  starting transfers between devices  14.2 us (4%)
  local copies, waits for them, and re-layouts  11.7 us (3%)
    all_gather x1, waiting for transfers between devices, attention(): value_piece = lax.all_gather(stretch_values, 'seq', axis=0, tiled=True)  78.2 us
    all_gather x1, waiting for transfers between devices, attention(): key_piece = lax.all_gather(stretch_keys, 'seq', axis=0, tiled=True)  69.8 us
    all_to_all x1, waiting for transfers between devices, relayout(): lax.all_to_all(outgoing(cache_keys), 'seq', split_axis=1, concat_axis=1,...  36.9 us
    all_to_all x1, waiting for transfers between devices, relayout(): lax.all_to_all(outgoing(cache_values), 'seq', split_axis=1, concat_axis=1...  36.3 us
    reduce_scatter x1, waiting for transfers between devices, local(): lax.psum_scatter(jnp.dot(attended, out_weight, preferred_element_type=jnp...  32.4 us
    dot_general x1, matrix products, compute(): jnp.einsum('qhd,khd->hqk', query_heads, key_heads, preferred_element_type...  16.6 us
    reduce_sum x1, other arithmetic, compute(): weight_sum = weight_sum * rescale + jnp.sum(weights, axis=-1)  16 us
    dot_general x1, matrix products, compute(): jnp.einsum('hqk,khd->hqd', weights.astype(jnp.bfloat16), value_heads, pre...  15.7 us
  transfers between devices with their start and end apart: 5, of which 5 were waited for; matrix products, arithmetic and copies ran while one was open for 7% of the time, Pallas kernels for 0%

commit v1 on v0

v1 whole, which is shorter than its diff:
```python
import functools
import math

import jax
import jax.numpy as jnp
from jax import lax
from jax.experimental import pallas as pl
from jax.experimental.pallas import tpu as pltpu
from jax.sharding import PartitionSpec as P

HD = 128
Q_ROWS = 256


def relayout(cache_keys, cache_values, page_table):
    position = lax.axis_index("seq")
    groups = lax.axis_size("seq")
    layers, block_rows, feat_width = cache_keys.shape
    page_count = page_table.shape[0] // groups
    page_len = block_rows // page_count
    per_group = page_count // groups
    table = page_table.reshape(groups, groups, per_group)
    own = lax.dynamic_index_in_dim(table, position, 0, keepdims=False)
    run_ids = jnp.arange(groups, dtype=jnp.int32)
    goes = (own[:, 0] // page_count)[None, :] == run_ids[:, None]
    run_of = jnp.sum(jnp.where(goes, run_ids[None, :], 0), axis=1)
    send_pages = (run_of[:, None] * per_group + jnp.arange(per_group, dtype=jnp.int32)[None, :]).reshape(-1)
    both = jnp.stack([cache_keys, cache_values]).reshape(2, layers, page_count, page_len, feat_width)
    outgoing = jnp.take(both, send_pages, axis=2).reshape(2, layers, groups, per_group, page_len, feat_width)
    moved = lax.all_to_all(outgoing, "seq", split_axis=2, concat_axis=2, tiled=True)
    hit = (table[:, :, 0] // page_count) == position
    slot_of = (jnp.sum(jnp.where(hit[:, :, None], table, 0), axis=1) % page_count).reshape(-1)
    arrivals = jnp.arange(page_count, dtype=jnp.int32)
    inverse = jnp.sum(jnp.where(slot_of[None, :] == arrivals[:, None], arrivals[None, :], 0), axis=1)
    placed = jnp.take(moved.reshape(2, layers, page_count, page_len, feat_width), inverse, axis=2)
    return (placed[0], placed[1])


def attention_kernel(meta_ref, q_ref, qseg_ref, kseg_ref, k_ref, v_ref, o_ref, *, block_count, block_rows, scale):
    chunk = pl.program_id(0)
    query_block = meta_ref[block_count]
    q = q_ref[...]
    qseg = qseg_ref[...]
    rows = q.shape[0]
    qpos = query_block * block_rows + chunk * rows + lax.broadcasted_iota(jnp.int32, (rows, 1), 0)
    kiota = lax.broadcasted_iota(jnp.int32, (1, block_rows), 1)

    def scores(c):
        s = lax.dot_general(
            q, k_ref[c], (((1,), (1,)), ((), ())), preferred_element_type=jnp.float32
        ) * scale
        allowed = (qseg == kseg_ref[c]) & (c * block_rows + kiota <= qpos)
        return s, allowed

    def max_body(c, m):
        def live(m):
            s, allowed = scores(c)
            return jnp.maximum(m, jnp.max(jnp.where(allowed, s, -jnp.inf), axis=1, keepdims=True))

        return lax.cond(meta_ref[c] != 0, live, lambda m: m, m)

    m = lax.fori_loop(0, block_count, max_body, jnp.full((rows, 1), -jnp.inf, jnp.float32))

    def sum_body(c, carry):
        def live(carry):
            l, acc = carry
            s, allowed = scores(c)
            w = jnp.where(allowed, jnp.exp(s - m), 0.0)
            l = l + jnp.sum(w, axis=1, keepdims=True)
            acc = acc + jnp.dot(w.astype(jnp.bfloat16), v_ref[c], preferred_element_type=jnp.float32)
            return (l, acc)

        return lax.cond(meta_ref[c] != 0, live, lambda x: x, carry)

    initial = (jnp.zeros((rows, 1), jnp.float32), jnp.zeros((rows, q.shape[1]), jnp.float32))
    l, acc = lax.fori_loop(0, block_count, sum_body, initial)
    o_ref[...] = (acc / l).astype(o_ref.dtype)


def attend_head(meta, queries, qseg, kseg, kv, head):
    block_count, _, block_rows, width = kv.shape
    rows = queries.shape[0]
    kernel = functools.partial(
        attention_kernel, block_count=block_count, block_rows=block_rows, scale=1.0 / math.sqrt(HD)
    )
    return pl.pallas_call(
        kernel,
        grid_spec=pltpu.PrefetchScalarGridSpec(
            num_scalar_prefetch=1,
            grid=(rows // Q_ROWS,),
            in_specs=[
                pl.BlockSpec((Q_ROWS, width), lambda i, meta: (i, head)),
                pl.BlockSpec((Q_ROWS, 1), lambda i, meta: (i, 0)),
                pl.BlockSpec((block_count, 1, block_rows), lambda i, meta: (0, 0, 0)),
                pl.BlockSpec((block_count, None, block_rows, width), lambda i, meta: (0, 0, 0, 0)),
                pl.BlockSpec((block_count, None, block_rows, width), lambda i, meta: (0, 1, 0, 0)),
            ],
            out_specs=pl.BlockSpec((Q_ROWS, width), lambda i, meta: (i, 0)),
        ),
        out_shape=jax.ShapeDtypeStruct((rows, width), queries.dtype),
    )(meta, queries, qseg, kseg, kv, kv)


def attention(queries, stretch_keys, stretch_values, segment_ids, block_live):
    position = lax.axis_index("seq")
    block_count = lax.axis_size("seq")
    block_rows, feat_width = queries.shape
    head_count = feat_width // HD
    seg_blocks = segment_ids.reshape(block_count, block_rows)
    query_seg = lax.dynamic_index_in_dim(seg_blocks, position, 0, keepdims=False)
    live_row = lax.dynamic_index_in_dim(block_live, position, 0, keepdims=False)
    block_ids = jnp.arange(block_count, dtype=jnp.int32)
    live = (block_ids == position) | (
        (block_ids < position) & (live_row == 1) & (seg_blocks[:, -1] >= query_seg[0])
    )
    meta = jnp.concatenate([live.astype(jnp.int32), position.astype(jnp.int32)[None]])
    qseg = query_seg[:, None]
    kseg = seg_blocks[:, None, :]
    outs = []
    for head in range(head_count):
        columns = slice(head * HD, (head + 1) * HD)
        kv = jnp.stack([stretch_keys[:, columns], stretch_values[:, columns]])
        kv_all = lax.all_gather(kv, "seq", axis=0, tiled=False)
        outs.append(attend_head(meta, queries, qseg, kseg, kv_all, head))
    return jnp.concatenate(outs, axis=1)


def local(
    queries,
    stretch_keys,
    stretch_values,
    segment_ids,
    block_live,
    out_weight,
    cache_keys,
    cache_values,
    page_table,
):
    decode_keys, decode_values = relayout(cache_keys, cache_values, page_table)
    attended = attention(queries, stretch_keys, stretch_values, segment_ids, block_live)
    projected = lax.psum_scatter(
        jnp.dot(attended, out_weight, preferred_element_type=jnp.float32).astype(jnp.bfloat16),
        "head",
        scatter_dimension=0,
        tiled=True,
    )
    return (attended, projected, decode_keys, decode_values)


def solution(mesh):
    placed = (
        P("seq", "head"),
        P("seq", "head"),
        P("seq", "head"),
        P(),
        P(),
        P("head", None),
        P(None, "seq", "head"),
        P(None, "seq", "head"),
        P(),
    )
    return jax.shard_map(
        local,
        mesh=mesh,
        in_specs=placed,
        out_specs=(
            P("seq", "head"),
            P(("seq", "head"), None),
            P(None, "seq", None, "head"),
            P(None, "seq", None, "head"),
        ),
        check_vma=False,
    )
```

time: 365 us -> 341 us (0.934)
  matrix products: 39.5 us -> 7.17 us
  other arithmetic: 29.6 us -> 7.44 us
  Pallas kernels: 0 us -> 18.6 us
  starting transfers between devices: 14.2 us -> 20.4 us
    dot_general x2 -> x0, matrix products: 32.3 us -> none  [the longest x1 16.6 us: compute(): jnp.einsum('qhd,khd->hqk', query_heads, key_heads, preferred_element_type...]
    pallas_call x0 -> x2, Pallas kernels: none -> 18.6 us  [attend_head(): pl.pallas_call(kernel, grid_spec=pltpu.PrefetchScalarGridSpec(num_scalar_...]
    reduce_sum x1 -> x3, other arithmetic: 16 us -> 0.35 us  [the longest x1 0.12 us: relayout(): jnp.sum(jnp.where(hit[:, :, None], table, 0), axis=1) % page_count]
    reduce_or x2 -> x0, other arithmetic: 8.58 us -> none  [the longest x1 8.41 us: attention(): jnp.any(allowed)]
    reduce_scatter x1, waiting for transfers between devices: 32.4 us -> 38.9 us  [local(): lax.psum_scatter(jnp.dot(attended, out_weight, preferred_element_type=jnp...]
    all_to_all x2 -> x1, starting transfers between devices: 14.1 us -> 20.3 us  [relayout(): lax.all_to_all(outgoing, 'seq', split_axis=2, concat_axis=2, tiled=True)]
    sort x3 -> x0, other arithmetic: 4.02 us -> none  [the longest x1 1.61 us: relayout(): ordering = jnp.argsort(own_slots // page_count, stable=True)]
    all_to_all x2 -> x1, waiting for transfers between devices: 73.2 us -> 73 us  [relayout(): lax.all_to_all(outgoing, 'seq', split_axis=2, concat_axis=2, tiled=True)]
  transfers between devices with their start and end apart: 5 -> 4, of which waited for: 5 -> 4; matrix products, arithmetic and copies ran while one was open for 7% -> 5% of each run, Pallas kernels for 0% -> 3%
where the time goes in v1:
time: 341 us; the launch traced here: 339 us
  waiting for transfers between devices  258 us (76%)
  starting transfers between devices  20.4 us (6%)
  Pallas kernels  18.6 us (5%)
  between operations  13.9 us (4%)
  local copies, waits for them, and re-layouts  13.7 us (4%)
  other arithmetic  7.44 us (2%)
  matrix products  7.17 us (2%)
    all_gather x2, waiting for transfers between devices, attention(): kv_all = lax.all_gather(kv, 'seq', axis=0, tiled=False)  146 us
    all_to_all x1, waiting for transfers between devices, relayout(): lax.all_to_all(outgoing, 'seq', split_axis=2, concat_axis=2, tiled=True)  73 us
    reduce_scatter x1, waiting for transfers between devices, local(): lax.psum_scatter(jnp.dot(attended, out_weight, preferred_element_type=jnp...  38.9 us
    all_to_all x1, starting transfers between devices, relayout(): lax.all_to_all(outgoing, 'seq', split_axis=2, concat_axis=2, tiled=True)  20.3 us
    pallas_call x2, Pallas kernels, attend_head(): pl.pallas_call(kernel, grid_spec=pltpu.PrefetchScalarGridSpec(num_scalar_...  18.6 us
    dot_general x1, matrix products, local(): jnp.dot(attended, out_weight, preferred_element_type=jnp.float32)  7.17 us
  transfers between devices with their start and end apart: 4, of which 4 were waited for; matrix products, arithmetic and copies ran while one was open for 5% of the time, Pallas kernels for 3%

profile of v1, /device:TPU:8, one launch (start us, length us, event | category | flops | bytes accessed | tf_op | source)
XLA Modules:
  0.0 339.2 jit_solution(12336941731509857547)
XLA Ops:
  7.2 0.0 copy-start.4
  7.2 0.0 all-gather.7.cloned.1.call-start
  7.2 1.1 slice_bitcast_fusion.4
  8.4 0.7 pad_maximum_fusion.2
  9.1 0.0 all-gather.7.cloned.1.call-update
  9.1 0.0 all-gather.5.cloned.1.call-start
  9.2 0.7 pad_maximum_fusion.1
  9.9 0.0 all-gather.5.cloned.1.call-update
  9.9 0.0 reduce-scatter.2.cloned.1.call-start
  10.0 0.5 constant_dynamic-slice_fusion
  10.5 0.9 copy.44.qseg_ref
  11.4 0.8 fusion.4
  12.2 0.7 fusion.7
  12.9 0.6 pad_add_fusion.meta_ref
  13.5 76.4 %all-gather.7.cloned.1.call-done = bf16[32,512,128]{2,1,0:T(8,128)(2,1)} async-done(((bf16[2,512,128]{2,1,0:T(8,128)(2,1)}), bf16[32,512,128]{2,1,0:T(8,128)(2,1)}) %all-gather.7.cloned.1.call-update) | async-done | bytes 4194320 | tf_op jit(solution)/shard_map/all_gather | solution.py:123
  89.9 9.2 %shard_map.121 = bf16[512,128]{1,0:T(8,128)(2,1)} custom-call(s32[17]{0:T(128)} %pad_add_fusion.meta_ref, bf16[512,256]{1,0:T(8,128)(2,1)} %q_ref.3, s32[512,1]{1,0:T(8,128)} %copy.44.qseg_ref, s32[16,1,512]{2,1,0:T(1,128)} %bitcast.54, bf16[16,2,512,128]{3,2,1,0:T(8,128)(2,1)} %bitcast.46, bf16[16,2,512,128]{3,2,1,0:T(8,128)(2,1)} %bitcast.47), custom_call_target="tpu_custom_call" | custom-call | tf_op jit(solution)/shard_map/pallas_call | solution.py:86
  99.1 69.5 %all-gather.5.cloned.1.call-done = bf16[32,512,128]{2,1,0:T(8,128)(2,1)} async-done(((bf16[2,512,128]{2,1,0:T(8,128)(2,1)}), bf16[32,512,128]{2,1,0:T(8,128)(2,1)}) %all-gather.5.cloned.1.call-update) | async-done | bytes 4194320 | tf_op jit(solution)/shard_map/all_gather | solution.py:123
  168.6 9.4 %shard_map.120 = bf16[512,128]{1,0:T(8,128)(2,1)} custom-call(s32[17]{0:T(128)} %pad_add_fusion.meta_ref, bf16[512,256]{1,0:T(8,128)(2,1)} %q_ref.3, s32[512,1]{1,0:T(8,128)} %copy.44.qseg_ref, s32[16,1,512]{2,1,0:T(1,128)} %bitcast.55, bf16[16,2,512,128]{3,2,1,0:T(8,128)(2,1)} %bitcast.48, bf16[16,2,512,128]{3,2,1,0:T(8,128)(2,1)} %bitcast.49), custom_call_target="tpu_custom_call" | custom-call | tf_op jit(solution)/shard_map/pallas_call | solution.py:86
  178.0 0.0 copy-done.3
  178.0 0.9 pad_maximum_fusion.3
  178.9 0.0 copy-start
  178.9 7.2 %convolution_convert_fusion = bf16[512,7168]{1,0:T(8,128)(2,1)} fusion(bf16[512,256]{1,0:T(8,128)(2,1)S(1)} %pad_maximum_fusion.3, bf16[256,7168]{1,0:T(8,128)(2,1)} %param.16), kind=kOutput, calls=%fused_computation.2 | convolution fusion | flops 1882718208 | bytes 11272192 | tf_op jit(solution)/shard_map/dot_general | solution.py:142
  186.1 0.0 reduce-scatter.2.cloned.1.call-update
  186.2 0.6 copy-done.5
  186.8 0.1 reshape.95
  187.0 0.1 copy.46
  187.1 0.1 select_reduce_fusion.2
  187.2 0.1 iota_add_fusion
  187.3 0.1 add.54
  187.3 0.4 fusion.3
  187.7 0.1 select_reduce_fusion
  187.8 0.1 reduce_sum.31
  188.0 0.0 copy-done.1
  188.0 0.0 copy-done.2
  188.0 1.6 pad_maximum_fusion
  189.6 2.3 gather_fusion
  191.8 0.3 broadcast_select_fusion
  192.1 1.7 copy.48
  193.8 20.3 %all-to-all-start = ((bf16[2,4,16,2,16,256]{5,4,3,1,0,2:T(8,128)(2,1)}), bf16[2,4,16,2,16,256]{5,4,3,1,0,2:T(8,128)(2,1)S(1)}, u32[]{:S(2)}, u32[]{:S(2)}) async-start(bf16[2,4,16,2,16,256]{5,4,3,1,0,2:T(8,128)(2,1)} %copy.48), calls=%async_computation.1 | async-start | bytes 4194304 | tf_op jit(solution)/shard_map/all_to_all | solution.py:30
  214.0 0.1 select_reduce_fusion.1
  214.2 73.0 %all-to-all-done = bf16[2,4,16,2,16,256]{5,4,3,1,0,2:T(8,128)(2,1)S(1)} async-done(((bf16[2,4,16,2,16,256]{5,4,3,1,0,2:T(8,128)(2,1)}), bf16[2,4,16,2,16,256]{5,4,3,1,0,2:T(8,128)(2,1)S(1)}, u32[]{:S(2)}, u32[]{:S(2)}) %all-to-all-start) | async-done | bytes 2097184 | tf_op jit(solution)/shard_map/all_to_all | solution.py:30
  287.2 1.6 copy.49
  288.8 2.3 gather_fusion.1
  291.1 0.3 select_bitcast_fusion
  291.4 0.1 slice_bitcast_fusion
  291.6 1.1 copy.50
  292.6 1.1 copy.51
  293.7 38.9 %reduce-scatter.2.cloned.1.call-done = bf16[32,7168]{1,0:T(8,128)(2,1)} async-done(((bf16[512,7168]{1,0:T(8,128)(2,1)}), bf16[32,7168]{1,0:T(8,128)(2,1)}) %reduce-scatter.2.cloned.1.call-update) | async-done | bytes 458768 | tf_op jit(solution)/shard_map/reduce_scatter | solution.py:141
  (17 shorter events, 0.1 us)
Async XLA Ops:
  7.2 2.8 copy-start.4
  7.2 82.7 %all-gather.7.cloned.1.call-start = ((), (), s32[]{:S(2)}) async-start(), calls=%async_computation.4 | async-start | bytes 4456448 | tf_op jit(solution)/shard_map/all_gather | solution.py:123
  9.1 159.5 %all-gather.5.cloned.1.call-start = ((), (), s32[]{:S(2)}) async-start(), calls=%async_computation.3 | async-start | bytes 4456448 | tf_op jit(solution)/shard_map/all_gather | solution.py:123
  9.9 322.7 %reduce-scatter.2.cloned.1.call-start = ((), (), s32[]{:S(2)}) async-start(), calls=%async_computation.2 | async-start | bytes 7798784 | tf_op jit(solution)/shard_map/reduce_scatter | solution.py:141
  168.6 9.4 %copy-start.3 = (bf16[512,128]{1,0:T(8,128)(2,1)S(1)}, bf16[512,128]{1,0:T(8,128)(2,1)}, u32[]{:S(2)}) copy-start(bf16[512,128]{1,0:T(8,128)(2,1)} %shard_map.121) | copy-start | bytes 393220
  178.9 7.2 %copy-start = (bf16[512,256]{1,0:T(8,128)(2,1)}, bf16[512,256]{1,0:T(8,128)(2,1)S(1)}, u32[]{:S(2)}) copy-start(bf16[512,256]{1,0:T(8,128)(2,1)S(1)} %pad_maximum_fusion.3) | copy-start | bytes 786436
  186.1 0.7 copy-start.5
  186.1 1.8 copy-start.1
  186.1 1.9 copy-start.2
  193.8 93.4 %all-to-all-start = ((bf16[2,4,16,2,16,256]{5,4,3,1,0,2:T(8,128)(2,1)}), bf16[2,4,16,2,16,256]{5,4,3,1,0,2:T(8,128)(2,1)S(1)}, u32[]{:S(2)}, u32[]{:S(2)}) async-start(bf16[2,4,16,2,16,256]{5,4,3,1,0,2:T(8,128)(2,1)} %copy.48), calls=%async_computation.1 | async-start | bytes 4194304 | tf_op jit(solution)/shard_map/all_to_all | solution.py:30
Sparse Core Ops, SparseCore 0:
  11.0 78.7 all-gather.6
  92.9 75.7 all-gather.4
  186.3 146.3 reduce-scatter.1

commit v2 on v1

--- a/solution.py
+++ b/solution.py
@@ -6,15 +6,18 @@
 from jax import lax
 from jax.experimental import pallas as pl
 from jax.experimental.pallas import tpu as pltpu
+from jax.sharding import Mesh
 from jax.sharding import PartitionSpec as P
 
 HD = 128
+SEQ = ("zh", "y")
+HEAD = ("x", "zl", "c")
 Q_ROWS = 256
 
 
 def relayout(cache_keys, cache_values, page_table):
-    position = lax.axis_index("seq")
-    groups = lax.axis_size("seq")
+    position = lax.axis_index(SEQ)
+    groups = lax.axis_size(SEQ)
     layers, block_rows, feat_width = cache_keys.shape
     page_count = page_table.shape[0] // groups
     page_len = block_rows // page_count
@@ -27,12 +30,16 @@
     send_pages = (run_of[:, None] * per_group + jnp.arange(per_group, dtype=jnp.int32)[None, :]).reshape(-1)
     both = jnp.stack([cache_keys, cache_values]).reshape(2, layers, page_count, page_len, feat_width)
     outgoing = jnp.take(both, send_pages, axis=2).reshape(2, layers, groups, per_group, page_len, feat_width)
-    moved = lax.all_to_all(outgoing, "seq", split_axis=2, concat_axis=2, tiled=True)
+    moved = lax.all_to_all(outgoing, SEQ, split_axis=2, concat_axis=2, tiled=True)
     hit = (table[:, :, 0] // page_count) == position
     slot_of = (jnp.sum(jnp.where(hit[:, :, None], table, 0), axis=1) % page_count).reshape(-1)
     arrivals = jnp.arange(page_count, dtype=jnp.int32)
     inverse = jnp.sum(jnp.where(slot_of[None, :] == arrivals[:, None], arrivals[None, :], 0), axis=1)
-    placed = jnp.take(moved.reshape(2, layers, page_count, page_len, feat_width), inverse, axis=2)
+    return (moved.reshape(2, layers, page_count, page_len, feat_width), inverse)
+
+
+def place_pages(moved, inverse):
+    placed = jnp.take(moved, inverse, axis=2)
     return (placed[0], placed[1])
 
 
@@ -101,9 +108,9 @@
     )(meta, queries, qseg, kseg, kv, kv)
 
 
-def attention(queries, stretch_keys, stretch_values, segment_ids, block_live):
-    position = lax.axis_index("seq")
-    block_count = lax.axis_size("seq")
+def attention(queries, stretch_keys, stretch_values, segment_ids, block_live, moved):
+    position = lax.axis_index(SEQ)
+    block_count = lax.axis_size(SEQ)
     block_rows, feat_width = queries.shape
     head_count = feat_width // HD
     seg_blocks = segment_ids.reshape(block_count, block_rows)
@@ -120,9 +127,11 @@
     for head in range(head_count):
         columns = slice(head * HD, (head + 1) * HD)
         kv = jnp.stack([stretch_keys[:, columns], stretch_values[:, columns]])
-        kv_all = lax.all_gather(kv, "seq", axis=0, tiled=False)
+        kv_all = lax.all_gather(kv, SEQ, axis=0, tiled=False)
+        if outs:
+            moved, kv_all, outs = lax.optimization_barrier((moved, kv_all, outs))
         outs.append(attend_head(meta, queries, qseg, kseg, kv_all, head))
-    return jnp.concatenate(outs, axis=1)
+    return (jnp.concatenate(outs, axis=1), moved)
 
 
 def local(
@@ -136,38 +145,42 @@
     cache_values,
     page_table,
 ):
-    decode_keys, decode_values = relayout(cache_keys, cache_values, page_table)
-    attended = attention(queries, stretch_keys, stretch_values, segment_ids, block_live)
-    projected = lax.psum_scatter(
-        jnp.dot(attended, out_weight, preferred_element_type=jnp.float32).astype(jnp.bfloat16),
-        "head",
-        scatter_dimension=0,
-        tiled=True,
-    )
+    moved, inverse = relayout(cache_keys, cache_values, page_table)
+    attended, moved = attention(queries, stretch_keys, stretch_values, segment_ids, block_live, moved)
+    decode_keys, decode_values = place_pages(moved, inverse)
+    sizes = [lax.axis_size(name) for name in HEAD]
+    rows, width = attended.shape
+    share = rows // math.prod(sizes)
+    order = attended.reshape(*sizes, share, width).transpose(2, 1, 0, 3, 4).reshape(rows, width)
+    projected = jnp.dot(order, out_weight, preferred_element_type=jnp.float32).astype(jnp.bfloat16)
+    for name in reversed(HEAD):
+        projected = lax.psum_scatter(projected, name, scatter_dimension=0, tiled=True)
     return (attended, projected, decode_keys, decode_values)
 
 
 def solution(mesh):
+    seq_size, head_size = mesh.shape["seq"], mesh.shape["head"]
+    fine = Mesh(mesh.devices.reshape(seq_size // 4, 4, head_size // 4, 2, 2), SEQ + HEAD)
     placed = (
-        P("seq", "head"),
-        P("seq", "head"),
-        P("seq", "head"),
+        P(SEQ, HEAD),
+        P(SEQ, HEAD),
+        P(SEQ, HEAD),
         P(),
         P(),
-        P("head", None),
-        P(None, "seq", "head"),
-        P(None, "seq", "head"),
+        P(HEAD, None),
+        P(None, SEQ, HEAD),
+        P(None, SEQ, HEAD),
         P(),
     )
     return jax.shard_map(
         local,
-        mesh=mesh,
+        mesh=fine,
         in_specs=placed,
         out_specs=(
-            P("seq", "head"),
-            P(("seq", "head"), None),
-            P(None, "seq", None, "head"),
-            P(None, "seq", None, "head"),
+            P(SEQ, HEAD),
+            P(SEQ + HEAD, None),
+            P(None, SEQ, None, HEAD),
+            P(None, SEQ, None, HEAD),
         ),
         check_vma=False,
     )

time: 341 us -> 344 us (level)
  waiting for transfers between devices: 258 us -> 272 us
  starting transfers between devices: 20.4 us -> 11.9 us
    reduce_scatter x1 -> x3, waiting for transfers between devices: 38.9 us -> 117 us  [local(): lax.psum_scatter(projected, name, scatter_dimension=0, tiled=True)]
    all_gather x2, waiting for transfers between devices: 146 us -> 80.4 us  [attention(): kv_all = lax.all_gather(kv, SEQ, axis=0, tiled=False)]
    all_to_all x1, starting transfers between devices: 20.3 us -> 11.7 us  [relayout(): lax.all_to_all(outgoing, SEQ, split_axis=2, concat_axis=2, tiled=True)]
  transfers between devices with their start and end apart: 4 -> 6, of which waited for: 4 -> 6; matrix products, arithmetic and copies ran while one was open for 5% -> 6% of each run, Pallas kernels for 3% -> 2%
where the time goes in v2:
time: 344 us; the launch traced here: 342 us
  waiting for transfers between devices  272 us (79%)
  Pallas kernels  15.6 us (5%)
  between operations  14 us (4%)
  local copies, waits for them, and re-layouts  13.1 us (4%)
  starting transfers between devices  11.9 us (3%)
  other arithmetic  9 us (3%)
  matrix products  7.15 us (2%)
    reduce_scatter x3, waiting for transfers between devices, local(): lax.psum_scatter(projected, name, scatter_dimension=0, tiled=True)  117 us
    all_gather x2, waiting for transfers between devices, attention(): kv_all = lax.all_gather(kv, SEQ, axis=0, tiled=False)  80.4 us
    all_to_all x1, waiting for transfers between devices, relayout(): lax.all_to_all(outgoing, SEQ, split_axis=2, concat_axis=2, tiled=True)  74.1 us
    pallas_call x2, Pallas kernels, attend_head(): pl.pallas_call(kernel, grid_spec=pltpu.PrefetchScalarGridSpec(num_scalar_...  15.6 us
    all_to_all x1, starting transfers between devices, relayout(): lax.all_to_all(outgoing, SEQ, split_axis=2, concat_axis=2, tiled=True)  11.7 us
    dot_general x1, matrix products, local(): jnp.dot(order, out_weight, preferred_element_type=jnp.float32)  7.15 us
  transfers between devices with their start and end apart: 6, of which 6 were waited for; matrix products, arithmetic and copies ran while one was open for 6% of the time, Pallas kernels for 2%

profile of v2, /device:TPU:8, one launch (start us, length us, event | category | flops | bytes accessed | tf_op | source)
XLA Modules:
  0.0 342.3 jit_solution(9464763095664452149)
XLA Ops:
  7.2 0.0 all-gather.7.cloned.1.call-start
  7.2 1.3 slice_bitcast_fusion.2
  8.5 0.7 pad_maximum_fusion.2
  9.2 0.0 all-gather.7.cloned.1.call-update
  9.3 0.0 all-gather.5.cloned.1.call-start
  9.3 0.7 pad_maximum_fusion.1
  10.0 0.0 all-gather.5.cloned.1.call-update
  10.1 0.1 reshape.100
  10.2 0.4 fusion.3
  10.6 0.1 select_reduce_fusion
  10.7 0.1 reduce_sum.31
  10.8 0.1 copy.49
  10.9 0.1 select_reduce_fusion.2
  11.0 0.1 iota_add_fusion
  11.1 0.1 add.63
  11.2 0.1 select_reduce_fusion.1
  11.4 1.5 pad_maximum_fusion
  12.9 2.3 gather_fusion
  15.2 0.3 broadcast_select_fusion
  15.5 1.6 copy.51
  17.1 11.7 %all-to-all-start = ((bf16[2,4,16,2,16,256]{5,4,3,1,0,2:T(8,128)(2,1)}), bf16[2,4,16,2,16,256]{5,4,3,1,0,2:T(8,128)(2,1)}, u32[]{:S(2)}, u32[]{:S(2)}) async-start(bf16[2,4,16,2,16,256]{5,4,3,1,0,2:T(8,128)(2,1)} %copy.51), calls=%async_computation | async-start | bytes 4194304 | tf_op jit(solution)/shard_map/all_to_all | solution.py:33
  28.8 0.0 reduce-scatter.4.cloned.1.call-start
  28.8 0.6 constant_dynamic-slice_fusion
  29.4 0.9 copy.53.qseg_ref
  30.3 0.8 fusion.4
  31.1 0.7 fusion.7
  31.8 0.6 pad_add_fusion.meta_ref
  32.4 74.1 %all-to-all-done = bf16[2,4,16,2,16,256]{5,4,3,1,0,2:T(8,128)(2,1)} async-done(((bf16[2,4,16,2,16,256]{5,4,3,1,0,2:T(8,128)(2,1)}), bf16[2,4,16,2,16,256]{5,4,3,1,0,2:T(8,128)(2,1)}, u32[]{:S(2)}, u32[]{:S(2)}) %all-to-all-start) | async-done | bytes 2097184 | tf_op jit(solution)/shard_map/all_to_all | solution.py:33
  106.5 1.8 copy.52
  108.3 9.7 %all-gather.7.cloned.1.call-done = bf16[32,512,128]{2,1,0:T(8,128)(2,1)} async-done(((bf16[2,512,128]{2,1,0:T(8,128)(2,1)}), bf16[32,512,128]{2,1,0:T(8,128)(2,1)}) %all-gather.7.cloned.1.call-update) | async-done | bytes 4194320 | tf_op jit(solution)/shard_map/all_gather | solution.py:130
  118.0 7.7 %shard_map.120 = bf16[512,128]{1,0:T(8,128)(2,1)} custom-call(s32[17]{0:T(128)} %pad_add_fusion.meta_ref, bf16[512,256]{1,0:T(8,128)(2,1)} %q_ref.3, s32[512,1]{1,0:T(8,128)} %copy.53.qseg_ref, s32[16,1,512]{2,1,0:T(1,128)} %bitcast.60, bf16[16,2,512,128]{3,2,1,0:T(8,128)(2,1)} %bitcast.50, bf16[16,2,512,128]{3,2,1,0:T(8,128)(2,1)} %bitcast.51), custom_call_target="tpu_custom_call" | custom-call | tf_op jit(solution)/shard_map/pallas_call | solution.py:93
  125.8 70.7 %all-gather.5.cloned.1.call-done = bf16[32,512,128]{2,1,0:T(8,128)(2,1)} async-done(((bf16[2,512,128]{2,1,0:T(8,128)(2,1)}), bf16[32,512,128]{2,1,0:T(8,128)(2,1)}) %all-gather.5.cloned.1.call-update) | async-done | bytes 4194320 | tf_op jit(solution)/shard_map/all_gather | solution.py:130
  196.4 7.9 %shard_map.121 = bf16[512,128]{1,0:T(8,128)(2,1)} custom-call(s32[17]{0:T(128)} %pad_add_fusion.meta_ref, bf16[512,256]{1,0:T(8,128)(2,1)} %q_ref.3, s32[512,1]{1,0:T(8,128)} %copy.53.qseg_ref, s32[16,1,512]{2,1,0:T(1,128)} %bitcast.61, bf16[16,2,512,128]{3,2,1,0:T(8,128)(2,1)} %bitcast.52, bf16[16,2,512,128]{3,2,1,0:T(8,128)(2,1)} %bitcast.53), custom_call_target="tpu_custom_call" | custom-call | tf_op jit(solution)/shard_map/pallas_call | solution.py:93
  204.3 0.9 pad_maximum_fusion.3
  205.3 7.2 %convolution_convert_fusion = bf16[512,7168]{1,0:T(8,128)(2,1)} fusion(bf16[512,256]{1,0:T(8,128)(2,1)S(1)} %bitcast.56, bf16[256,7168]{1,0:T(8,128)(2,1)} %param.16), kind=kOutput, calls=%fused_computation.2 | convolution fusion | flops 1882718208 | bytes 11272192 | tf_op jit(solution)/shard_map/dot_general | solution.py:155
  212.4 0.0 reduce-scatter.4.cloned.1.call-update
  212.4 0.0 reduce-scatter.6.cloned.1.call-start
  212.5 31.7 %reduce-scatter.4.cloned.1.call-done = bf16[256,7168]{1,0:T(8,128)(2,1)} async-done(((bf16[512,7168]{1,0:T(8,128)(2,1)}), bf16[256,7168]{1,0:T(8,128)(2,1)}) %reduce-scatter.4.cloned.1.call-update) | async-done | bytes 3670032 | tf_op jit(solution)/shard_map/reduce_scatter | solution.py:157
  244.2 0.0 reduce-scatter.6.cloned.1.call-update
  244.2 0.0 reduce-scatter.8.cloned.1.call-start
  244.3 58.0 %reduce-scatter.6.cloned.1.call-done = bf16[128,7168]{1,0:T(8,128)(2,1)} async-done(((bf16[256,7168]{1,0:T(8,128)(2,1)}), bf16[128,7168]{1,0:T(8,128)(2,1)}) %reduce-scatter.6.cloned.1.call-update) | async-done | bytes 1835024 | tf_op jit(solution)/shard_map/reduce_scatter | solution.py:157
  302.3 0.0 reduce-scatter.8.cloned.1.call-update
  302.3 2.0 gather_fusion.1
  304.4 1.8 select_bitcast_fusion
  306.2 0.1 slice_bitcast_fusion
  306.4 1.1 copy.57
  307.4 1.1 copy.56
  308.5 27.3 %reduce-scatter.8.cloned.1.call-done = bf16[32,7168]{1,0:T(8,128)(2,1)} async-done(((bf16[128,7168]{1,0:T(8,128)(2,1)}), bf16[32,7168]{1,0:T(8,128)(2,1)}) %reduce-scatter.8.cloned.1.call-update) | async-done | bytes 458768 | tf_op jit(solution)/shard_map/reduce_scatter | solution.py:157
  (23 shorter events, 0.1 us)
Async XLA Ops:
  7.2 2.9 copy-start.5
  7.2 4.2 %copy-start.1 = (bf16[4,512,256]{2,1,0:T(8,128)(2,1)S(1)}, bf16[4,512,256]{2,1,0:T(8,128)(2,1)}, u32[]{:S(2)}) copy-start(bf16[4,512,256]{2,1,0:T(8,128)(2,1)} %param.18) | copy-start | bytes 3145732
  7.2 4.2 %copy-start.2 = (bf16[4,512,256]{2,1,0:T(8,128)(2,1)S(1)}, bf16[4,512,256]{2,1,0:T(8,128)(2,1)}, u32[]{:S(2)}) copy-start(bf16[4,512,256]{2,1,0:T(8,128)(2,1)} %param.17) | copy-start | bytes 3145732
  7.2 110.8 %all-gather.7.cloned.1.call-start = ((), (), s32[]{:S(2)}) async-start(), calls=%async_computation.8 | async-start | bytes 4456448 | tf_op jit(solution)/shard_map/all_gather | solution.py:130
  9.3 187.2 %all-gather.5.cloned.1.call-start = ((), (), s32[]{:S(2)}) async-start(), calls=%async_computation.7 | async-start | bytes 4456448 | tf_op jit(solution)/shard_map/all_gather | solution.py:130
  17.1 11.7 %copy-start.4 = (s32[8192]{0:T(1024)S(1)}, s32[8192]{0:T(1024)}, u32[]{:S(2)}) copy-start(s32[8192]{0:T(1024)} %param.14) | copy-start | bytes 98308
  17.1 89.4 %all-to-all-start = ((bf16[2,4,16,2,16,256]{5,4,3,1,0,2:T(8,128)(2,1)}), bf16[2,4,16,2,16,256]{5,4,3,1,0,2:T(8,128)(2,1)}, u32[]{:S(2)}, u32[]{:S(2)}) async-start(bf16[2,4,16,2,16,256]{5,4,3,1,0,2:T(8,128)(2,1)} %copy.51), calls=%async_computation | async-start | bytes 4194304 | tf_op jit(solution)/shard_map/all_to_all | solution.py:33
  28.8 215.4 %reduce-scatter.4.cloned.1.call-start = ((), (), s32[]{:S(2)}) async-start(), calls=%async_computation.4 | async-start | bytes 11010048 | tf_op jit(solution)/shard_map/reduce_scatter | solution.py:157
  196.4 7.9 %copy-start.3 = (bf16[512,128]{1,0:T(8,128)(2,1)S(1)}, bf16[512,128]{1,0:T(8,128)(2,1)}, u32[]{:S(2)}) copy-start(bf16[512,128]{1,0:T(8,128)(2,1)} %shard_map.120) | copy-start | bytes 393220
  205.2 7.2 %copy-start = (bf16[512,256]{1,0:T(8,128)(2,1)}, bf16[512,256]{1,0:T(8,128)(2,1)S(1)}, u32[]{:S(2)}) copy-start(bf16[512,256]{1,0:T(8,128)(2,1)S(1)} %pad_maximum_fusion.3) | copy-start | bytes 786436
  212.4 89.9 %reduce-scatter.6.cloned.1.call-start = ((), (), s32[]{:S(2)}) async-start(), calls=%async_computation.5 | async-start | bytes 5505024 | tf_op jit(solution)/shard_map/reduce_scatter | solution.py:157
  244.2 91.6 %reduce-scatter.8.cloned.1.call-start = ((), (), s32[]{:S(2)}) async-start(), calls=%async_computation.6 | async-start | bytes 2293760 | tf_op jit(solution)/shard_map/reduce_scatter | solution.py:157
Sparse Core Ops, SparseCore 0:
  11.0 106.9 all-gather.6
  121.0 75.3 all-gather.4
  212.6 31.5 reduce-scatter.3
  246.7 55.5 reduce-scatter.5
  305.3 30.4 reduce-scatter.7

commit v3 on v2

--- a/solution.py
+++ b/solution.py
@@ -30,7 +30,9 @@
     send_pages = (run_of[:, None] * per_group + jnp.arange(per_group, dtype=jnp.int32)[None, :]).reshape(-1)
     both = jnp.stack([cache_keys, cache_values]).reshape(2, layers, page_count, page_len, feat_width)
     outgoing = jnp.take(both, send_pages, axis=2).reshape(2, layers, groups, per_group, page_len, feat_width)
-    moved = lax.all_to_all(outgoing, SEQ, split_axis=2, concat_axis=2, tiled=True)
+    outgoing = outgoing.transpose(2, 0, 1, 3, 4, 5)
+    moved = lax.all_to_all(outgoing, SEQ, split_axis=0, concat_axis=0, tiled=True)
+    moved = moved.transpose(1, 2, 0, 3, 4, 5)
     hit = (table[:, :, 0] // page_count) == position
     slot_of = (jnp.sum(jnp.where(hit[:, :, None], table, 0), axis=1) % page_count).reshape(-1)
     arrivals = jnp.arange(page_count, dtype=jnp.int32)
@@ -148,14 +150,33 @@
     moved, inverse = relayout(cache_keys, cache_values, page_table)
     attended, moved = attention(queries, stretch_keys, stretch_values, segment_ids, block_live, moved)
     decode_keys, decode_values = place_pages(moved, inverse)
-    sizes = [lax.axis_size(name) for name in HEAD]
+    projected = reduce_rows(attended, out_weight)
+    return (attended, projected, decode_keys, decode_values)
+
+
+def exchange(pieces, name):
+    size = pieces.shape[0]
+    me = lax.axis_index(name)
+    total = lax.dynamic_index_in_dim(pieces, me, 0, keepdims=False).astype(jnp.float32)
+    for shift in range(1, size):
+        target = (me + shift) % size
+        sent = lax.dynamic_index_in_dim(pieces, target, 0, keepdims=False).astype(jnp.bfloat16)
+        pairs = [(i, (i + shift) % size) for i in range(size)]
+        total = total + lax.ppermute(sent, name, pairs).astype(jnp.float32)
+    return total
+
+
+def reduce_rows(attended, out_weight):
+    x_size, zl_size, c_size = [lax.axis_size(name) for name in HEAD]
     rows, width = attended.shape
-    share = rows // math.prod(sizes)
-    order = attended.reshape(*sizes, share, width).transpose(2, 1, 0, 3, 4).reshape(rows, width)
-    projected = jnp.dot(order, out_weight, preferred_element_type=jnp.float32).astype(jnp.bfloat16)
-    for name in reversed(HEAD):
-        projected = lax.psum_scatter(projected, name, scatter_dimension=0, tiled=True)
-    return (attended, projected, decode_keys, decode_values)
+    share = rows // (x_size * zl_size * c_size)
+    order = attended.reshape(x_size, zl_size, c_size, share, width).transpose(2, 0, 1, 3, 4).reshape(rows, width)
+    partial = jnp.dot(order, out_weight, preferred_element_type=jnp.float32).astype(jnp.bfloat16)
+    columns = partial.shape[1]
+    total = exchange(partial.reshape(c_size, x_size, zl_size, share, columns), "c")
+    total = exchange(total.reshape(x_size, zl_size, share, columns), "x")
+    total = exchange(total.reshape(zl_size, share, columns), "zl")
+    return total.astype(jnp.bfloat16)
 
 
 def solution(mesh):

time: 344 us -> 307 us (0.89)
  the two profiles are of different devices: /device:TPU:8 before, /device:TPU:198 now
where the time goes in v3:
time: 307 us; the launch traced here: 306 us
  waiting for transfers between devices  197 us (64%)
  Pallas kernels  39.8 us (13%)
  local copies, waits for them, and re-layouts  23.1 us (8%)
  other arithmetic  15.2 us (5%)
  between operations  14.3 us (5%)
  starting transfers between devices  12.5 us (4%)
  matrix products  4.2 us (1%)
    all_to_all x1, waiting for transfers between devices, relayout(): lax.all_to_all(outgoing, SEQ, split_axis=0, concat_axis=0, tiled=True)  73.4 us
    all_gather x2, waiting for transfers between devices, attention(): kv_all = lax.all_gather(kv, SEQ, axis=0, tiled=False)  68.3 us
    ppermute x5, waiting for transfers between devices, exchange(): total = total + lax.ppermute(sent, name, pairs).astype(jnp.float32)  55.4 us
    pallas_call x2, Pallas kernels, attend_head(): pl.pallas_call(kernel, grid_spec=pltpu.PrefetchScalarGridSpec(num_scalar_...  39.8 us
    all_to_all x1, starting transfers between devices, relayout(): lax.all_to_all(outgoing, SEQ, split_axis=0, concat_axis=0, tiled=True)  9.08 us
    unnamed x22, local copies, waits for them, and re-layouts  8.1 us
    add x2, other arithmetic, exchange(): total = total + lax.ppermute(sent, name, pairs).astype(jnp.float32)  7.08 us
  transfers between devices with their start and end apart: 8, of which 8 were waited for; matrix products, arithmetic and copies ran while one was open for 6% of the time, Pallas kernels for 6%

profile of v3, /device:TPU:198, one launch (start us, length us, event | category | flops | bytes accessed | tf_op | source)
XLA Modules:
  0.0 306.3 jit_solution(5935085742283425493)
XLA Ops:
  7.2 1.3 slice_bitcast_fusion.2
  8.5 0.7 pad_maximum_fusion.2
  9.3 0.7 pad_maximum_fusion.1
  10.1 0.1 reshape.109
  10.3 0.1 select_reduce_fusion.2
  10.5 0.1 add.130
  10.6 0.4 fusion.10
  11.0 0.1 select_reduce_fusion
  11.2 0.1 select_reduce_fusion.1
  11.4 1.5 pad_maximum_fusion
  12.9 2.3 gather_fusion
  15.2 0.3 broadcast_select_fusion
  15.5 1.6 copy.51
  17.1 9.1 %all-to-all-start = ((bf16[16,2,4,2,16,256]{5,4,3,2,1,0:T(8,128)(2,1)}), bf16[16,2,4,2,16,256]{5,4,3,2,1,0:T(8,128)(2,1)S(1)}, u32[]{:S(2)}, u32[]{:S(2)}) async-start(bf16[16,2,4,2,16,256]{5,4,3,2,1,0:T(8,128)(2,1)} %copy.51), calls=%async_computation | async-start | bytes 4194304 | tf_op jit(solution)/shard_map/all_to_all | solution.py:34
  26.2 0.5 constant_dynamic-slice_fusion
  26.8 0.9 copy.53.qseg_ref
  27.6 0.7 fusion.11
  28.4 0.7 fusion.15
  29.1 0.6 pad_add_fusion.meta_ref
  29.6 73.4 %all-to-all-done = bf16[16,2,4,2,16,256]{5,4,3,2,1,0:T(8,128)(2,1)S(1)} async-done(((bf16[16,2,4,2,16,256]{5,4,3,2,1,0:T(8,128)(2,1)}), bf16[16,2,4,2,16,256]{5,4,3,2,1,0:T(8,128)(2,1)S(1)}, u32[]{:S(2)}, u32[]{:S(2)}) %all-to-all-start) | async-done | bytes 2097184 | tf_op jit(solution)/shard_map/all_to_all | solution.py:34
  103.1 1.4 copy-done.2
  104.5 1.8 copy.52
  106.3 9.2 %all-gather.7.cloned.1.call-done = bf16[32,512,128]{2,1,0:T(8,128)(2,1)} async-done(((bf16[2,512,128]{2,1,0:T(8,128)(2,1)}), bf16[32,512,128]{2,1,0:T(8,128)(2,1)}) %all-gather.7.cloned.1.call-update) | async-done | bytes 4194320 | tf_op jit(solution)/shard_map/all_gather | solution.py:132
  115.5 19.8 %shard_map.120 = bf16[512,128]{1,0:T(8,128)(2,1)} custom-call(s32[17]{0:T(128)} %pad_add_fusion.meta_ref, bf16[512,256]{1,0:T(8,128)(2,1)} %q_ref.3, s32[512,1]{1,0:T(8,128)} %copy.53.qseg_ref, s32[16,1,512]{2,1,0:T(1,128)} %bitcast.90, bf16[16,2,512,128]{3,2,1,0:T(8,128)(2,1)} %bitcast.79, bf16[16,2,512,128]{3,2,1,0:T(8,128)(2,1)} %bitcast.80), custom_call_target="tpu_custom_call" | custom-call | tf_op jit(solution)/shard_map/pallas_call | solution.py:95
  135.3 59.1 %all-gather.5.cloned.1.call-done = bf16[32,512,128]{2,1,0:T(8,128)(2,1)} async-done(((bf16[2,512,128]{2,1,0:T(8,128)(2,1)}), bf16[32,512,128]{2,1,0:T(8,128)(2,1)}) %all-gather.5.cloned.1.call-update) | async-done | bytes 4194320 | tf_op jit(solution)/shard_map/all_gather | solution.py:132
  194.4 20.0 %shard_map.121 = bf16[512,128]{1,0:T(8,128)(2,1)} custom-call(s32[17]{0:T(128)} %pad_add_fusion.meta_ref, bf16[512,256]{1,0:T(8,128)(2,1)} %q_ref.3, s32[512,1]{1,0:T(8,128)} %copy.53.qseg_ref, s32[16,1,512]{2,1,0:T(1,128)} %bitcast.91, bf16[16,2,512,128]{3,2,1,0:T(8,128)(2,1)} %bitcast.81, bf16[16,2,512,128]{3,2,1,0:T(8,128)(2,1)} %bitcast.82), custom_call_target="tpu_custom_call" | custom-call | tf_op jit(solution)/shard_map/pallas_call | solution.py:95
  214.4 0.9 pad_maximum_fusion.3
  215.3 4.2 %convolution_convert_fusion = bf16[512,7168]{1,0:T(8,128)(2,1)S(1)} fusion(bf16[512,256]{1,0:T(8,128)(2,1)S(1)} %bitcast.86, bf16[256,7168]{1,0:T(8,128)(2,1)} %param.16), kind=kOutput, calls=%fused_computation.2 | convolution fusion | flops 1882718208 | bytes 11272192 | tf_op jit(solution)/shard_map/dot_general | solution.py:174
  219.6 2.4 dynamic-slice_bitcast_fusion
  222.0 1.6 copy-done
  223.6 6.7 %collective-permute-done = bf16[4,2,32,7168]{3,2,1,0:T(8,128)(2,1)} collective-permute-done((bf16[4,2,32,7168]{3,2,1,0:T(8,128)(2,1)}, bf16[4,2,32,7168]{3,2,1,0:T(8,128)(2,1)}, u32[]{:S(2)}, u32[]{:S(2)}) %collective-permute-start) | collective-permute-done | bytes 3670048 | tf_op jit(solution)/shard_map/ppermute | solution.py:165
  230.3 4.4 %convert_add_fusion = f32[4,2,32,7168]{3,2,1,0:T(8,128)S(1)} fusion(bf16[4,2,32,7168]{3,2,1,0:T(8,128)(2,1)} %collective-permute-done, bf16[2,4,2,32,7168]{4,3,2,1,0:T(8,128)(2,1)} %bitcast.78, s32[]{:T(128)S(6)} %select_n.105), kind=kLoop, calls=%fused_computation.3 | loop fusion | flops 5505024 | bytes 14680068 | tf_op jit(solution)/shard_map/add | solution.py:165
  234.7 2.9 copy-done.1
  237.7 1.6 fusion.2
  239.3 0.5 collective-permute-start.1
  239.8 2.4 collective-permute-start.2
  242.2 2.1 gather_fusion.1
  244.3 18.5 %collective-permute-done.1 = bf16[2,32,7168]{2,1,0:T(8,128)(2,1)} collective-permute-done((bf16[2,32,7168]{2,1,0:T(8,128)(2,1)}, bf16[2,32,7168]{2,1,0:T(8,128)(2,1)}, u32[]{:S(2)}, u32[]{:S(2)}) %collective-permute-start.1) | collective-permute-done | bytes 917536 | tf_op jit(solution)/shard_map/ppermute | solution.py:165
  262.8 2.1 collective-permute-done.2
  264.9 18.5 %collective-permute-done.3 = bf16[2,32,7168]{2,1,0:T(8,128)(2,1)} collective-permute-done((bf16[2,32,7168]{2,1,0:T(8,128)(2,1)S(1)}, bf16[2,32,7168]{2,1,0:T(8,128)(2,1)}, u32[]{:S(2)}, u32[]{:S(2)}) %collective-permute-start.3) | collective-permute-done | bytes 917536 | tf_op jit(solution)/shard_map/ppermute | solution.py:165
  283.4 2.7 fusion.1
  286.1 0.4 collective-permute-start.4
  286.5 0.3 select_bitcast_fusion
  286.8 0.1 slice_bitcast_fusion
  286.9 1.1 copy.56
  288.0 1.1 copy.57
  289.1 9.6 %collective-permute-done.4 = bf16[32,7168]{1,0:T(8,128)(2,1)S(1)} collective-permute-done((bf16[32,7168]{1,0:T(8,128)(2,1)S(1)}, bf16[32,7168]{1,0:T(8,128)(2,1)S(1)}, u32[]{:S(2)}, u32[]{:S(2)}) %collective-permute-start.4) | collective-permute-done | bytes 458784 | tf_op jit(solution)/shard_map/ppermute | solution.py:165
  298.6 0.8 fusion.5
  (38 shorter events, 0.5 us)
Async XLA Ops:
  7.2 2.9 copy-start.9
  7.2 4.2 %copy-start.6 = (bf16[4,512,256]{2,1,0:T(8,128)(2,1)S(1)}, bf16[4,512,256]{2,1,0:T(8,128)(2,1)}, u32[]{:S(2)}) copy-start(bf16[4,512,256]{2,1,0:T(8,128)(2,1)} %param.17) | copy-start | bytes 3145732
  7.2 4.2 %copy-start.5 = (bf16[4,512,256]{2,1,0:T(8,128)(2,1)S(1)}, bf16[4,512,256]{2,1,0:T(8,128)(2,1)}, u32[]{:S(2)}) copy-start(bf16[4,512,256]{2,1,0:T(8,128)(2,1)} %param.18) | copy-start | bytes 3145732
  7.2 108.3 %all-gather.7.cloned.1.call-start = ((), (), s32[]{:S(2)}) async-start(), calls=%async_computation.2 | async-start | bytes 4456448 | tf_op jit(solution)/shard_map/all_gather | solution.py:132
  9.3 185.1 %all-gather.5.cloned.1.call-start = ((), (), s32[]{:S(2)}) async-start(), calls=%async_computation.1 | async-start | bytes 4456448 | tf_op jit(solution)/shard_map/all_gather | solution.py:132
  17.1 9.1 %copy-start.8 = (s32[8192]{0:T(1024)S(1)}, s32[8192]{0:T(1024)}, u32[]{:S(2)}) copy-start(s32[8192]{0:T(1024)} %param.14) | copy-start | bytes 98308
  17.1 86.0 %all-to-all-start = ((bf16[16,2,4,2,16,256]{5,4,3,2,1,0:T(8,128)(2,1)}), bf16[16,2,4,2,16,256]{5,4,3,2,1,0:T(8,128)(2,1)S(1)}, u32[]{:S(2)}, u32[]{:S(2)}) async-start(bf16[16,2,4,2,16,256]{5,4,3,2,1,0:T(8,128)(2,1)} %copy.51), calls=%async_computation | async-start | bytes 4194304 | tf_op jit(solution)/shard_map/all_to_all | solution.py:34
  103.1 1.4 copy-start.2
  194.4 20.0 %copy-start.7 = (bf16[512,128]{1,0:T(8,128)(2,1)S(1)}, bf16[512,128]{1,0:T(8,128)(2,1)}, u32[]{:S(2)}) copy-start(bf16[512,128]{1,0:T(8,128)(2,1)} %shard_map.120) | copy-start | bytes 393220
  215.3 4.2 %copy-start.4 = (bf16[512,256]{1,0:T(8,128)(2,1)}, bf16[512,256]{1,0:T(8,128)(2,1)S(1)}, u32[]{:S(2)}) copy-start(bf16[512,256]{1,0:T(8,128)(2,1)S(1)} %pad_maximum_fusion.3) | copy-start | bytes 786436
  219.6 4.0 %copy-start = (bf16[512,7168]{1,0:T(8,128)(2,1)}, bf16[512,7168]{1,0:T(8,128)(2,1)S(1)}, u32[]{:S(2)}) copy-start(bf16[512,7168]{1,0:T(8,128)(2,1)S(1)} %convolution_convert_fusion) | copy-start | bytes 22020100
  223.6 6.8 %collective-permute-start = (bf16[4,2,32,7168]{3,2,1,0:T(8,128)(2,1)}, bf16[4,2,32,7168]{3,2,1,0:T(8,128)(2,1)}, u32[]{:S(2)}, u32[]{:S(2)}) collective-permute-start(bf16[4,2,32,7168]{3,2,1,0:T(8,128)(2,1)} %dynamic-slice_bitcast_fusion), channel_id=1, source_target_pairs={{0,1},{1,0},{2,3},{3,2},{4,5},{5,4},{6,7},{7,6},{8,9},{9,8},{10,11... | collective-permute-start | bytes 11010056 | tf_op jit(solution)/shard_map/ppermute | solution.py:165
  234.7 2.9 copy-start.1
  239.3 23.5 %collective-permute-start.1 = (bf16[2,32,7168]{2,1,0:T(8,128)(2,1)}, bf16[2,32,7168]{2,1,0:T(8,128)(2,1)}, u32[]{:S(2)}, u32[]{:S(2)}) collective-permute-start(bf16[2,32,7168]{2,1,0:T(8,128)(2,1)} %get-tuple-element.35), channel_id=1, source_target_pairs={{0,4},{4,8},{8,12},{12,0},{1,5},{5,9},{9,13},{13,1},{2,6},{6,10},{... | collective-permute-start | bytes 2752520 | tf_op jit(solution)/shard_map/ppermute | solution.py:165
  239.8 25.1 %collective-permute-start.2 = (bf16[2,32,7168]{2,1,0:T(8,128)(2,1)}, bf16[2,32,7168]{2,1,0:T(8,128)(2,1)}, u32[]{:S(2)}, u32[]{:S(2)}) collective-permute-start(bf16[2,32,7168]{2,1,0:T(8,128)(2,1)} %get-tuple-element.37), channel_id=1, source_target_pairs={{0,8},{4,12},{8,0},{12,4},{1,9},{5,13},{9,1},{13,5},{2,10},{6,14},... | collective-permute-start | bytes 2752520 | tf_op jit(solution)/shard_map/ppermute | solution.py:165
  242.2 41.2 %collective-permute-start.3 = (bf16[2,32,7168]{2,1,0:T(8,128)(2,1)S(1)}, bf16[2,32,7168]{2,1,0:T(8,128)(2,1)}, u32[]{:S(2)}, u32[]{:S(2)}) collective-permute-start(bf16[2,32,7168]{2,1,0:T(8,128)(2,1)S(1)} %get-tuple-element.36), channel_id=1, source_target_pairs={{0,12},{4,0},{8,4},{12,8},{1,13},{5,1},{9,5},{13,9},{2,14},{6,2},{... | collective-permute-start | bytes 2752520 | tf_op jit(solution)/shard_map/ppermute | solution.py:165
  244.3 42.3 %copy-start.3 = (bf16[32,2,4,16,256]{4,3,2,1,0:T(8,128)(2,1)S(1)}, bf16[32,2,4,16,256]{4,3,2,1,0:T(8,128)(2,1)}, u32[]{:S(2)}) copy-start(bf16[32,2,4,16,256]{4,3,2,1,0:T(8,128)(2,1)} %gather_fusion.1) | copy-start | bytes 6291460
  286.1 12.5 %collective-permute-start.4 = (bf16[32,7168]{1,0:T(8,128)(2,1)S(1)}, bf16[32,7168]{1,0:T(8,128)(2,1)S(1)}, u32[]{:S(2)}, u32[]{:S(2)}) collective-permute-start(bf16[32,7168]{1,0:T(8,128)(2,1)S(1)} %fusion.6), channel_id=1, source_target_pairs={{0,2},{2,0},{1,3},{3,1},{4,6},{6,4},{5,7},{7,5},{8,10},{10,8},{9,1... | collective-permute-start | bytes 1376264 | tf_op jit(solution)/shard_map/ppermute | solution.py:165
Sparse Core Ops, SparseCore 0:
  11.0 104.3 all-gather.6
  118.5 75.8 all-gather.4

commit v4 on v3

--- a/solution.py
+++ b/solution.py
@@ -31,16 +31,17 @@
     both = jnp.stack([cache_keys, cache_values]).reshape(2, layers, page_count, page_len, feat_width)
     outgoing = jnp.take(both, send_pages, axis=2).reshape(2, layers, groups, per_group, page_len, feat_width)
     outgoing = outgoing.transpose(2, 0, 1, 3, 4, 5)
-    moved = lax.all_to_all(outgoing, SEQ, split_axis=0, concat_axis=0, tiled=True)
-    moved = moved.transpose(1, 2, 0, 3, 4, 5)
     hit = (table[:, :, 0] // page_count) == position
     slot_of = (jnp.sum(jnp.where(hit[:, :, None], table, 0), axis=1) % page_count).reshape(-1)
     arrivals = jnp.arange(page_count, dtype=jnp.int32)
     inverse = jnp.sum(jnp.where(slot_of[None, :] == arrivals[:, None], arrivals[None, :], 0), axis=1)
-    return (moved.reshape(2, layers, page_count, page_len, feat_width), inverse)
-
-
-def place_pages(moved, inverse):
+    return (outgoing, inverse)
+
+
+def place_pages(outgoing, inverse):
+    moved = lax.all_to_all(outgoing, SEQ, split_axis=0, concat_axis=0, tiled=True)
+    _, kinds, layers, per_group, page_len, feat_width = moved.shape
+    moved = moved.transpose(1, 2, 0, 3, 4, 5).reshape(kinds, layers, -1, page_len, feat_width)
     placed = jnp.take(moved, inverse, axis=2)
     return (placed[0], placed[1])
 

time: 307 us -> 290 us (0.945)
  the two profiles are of different devices: /device:TPU:198 before, /device:TPU:8 now
where the time goes in v4:
time: 290 us; the launch traced here: 289 us
  waiting for transfers between devices  189 us (65%)
  starting transfers between devices  29.1 us (10%)
  local copies, waits for them, and re-layouts  21.9 us (8%)
  Pallas kernels  15.6 us (5%)
  other arithmetic  15.4 us (5%)
  between operations  14.4 us (5%)
  matrix products  4.2 us (1%)
    all_gather x2, waiting for transfers between devices, attention(): kv_all = lax.all_gather(kv, SEQ, axis=0, tiled=False)  142 us
    all_to_all x1, waiting for transfers between devices, place_pages(): lax.all_to_all(outgoing, SEQ, split_axis=0, concat_axis=0, tiled=True)  38.2 us
    all_to_all x1, starting transfers between devices, place_pages(): lax.all_to_all(outgoing, SEQ, split_axis=0, concat_axis=0, tiled=True)  23.3 us
    pallas_call x2, Pallas kernels, attend_head(): pl.pallas_call(kernel, grid_spec=pltpu.PrefetchScalarGridSpec(num_scalar_...  15.6 us
    ppermute x5, waiting for transfers between devices, exchange(): total = total + lax.ppermute(sent, name, pairs).astype(jnp.float32)  9.05 us
    add x2, other arithmetic, exchange(): total = total + lax.ppermute(sent, name, pairs).astype(jnp.float32)  7.09 us
    unnamed x18, local copies, waits for them, and re-layouts  6.74 us
  transfers between devices with their start and end apart: 8, of which 4 were waited for; matrix products, arithmetic and copies ran while one was open for 8% of the time, Pallas kernels for 3%

profile of v4, /device:TPU:8, one launch (start us, length us, event | category | flops | bytes accessed | tf_op | source)
XLA Modules:
  0.0 289.5 jit_solution(18289914595565738662)
XLA Ops:
  7.3 1.3 slice_bitcast_fusion.2
  8.5 0.7 pad_maximum_fusion.2
  9.3 0.7 pad_maximum_fusion.1
  10.1 0.5 constant_dynamic-slice_fusion
  10.7 0.9 copy.51.qseg_ref
  11.5 0.1 reshape.109
  11.7 0.1 copy.49
  11.8 0.1 select_reduce_fusion.2
  11.9 0.1 iota_add_fusion
  12.0 0.1 add.130
  12.1 0.4 fusion.10
  12.5 0.1 select_reduce_fusion
  12.6 0.1 reduce_sum.31
  12.7 1.5 pad_maximum_fusion
  14.3 2.3 gather_fusion
  16.6 0.3 select_bitcast_fusion.1
  16.8 0.2 copy.50
  17.0 0.8 fusion.11
  17.8 0.7 fusion.15
  18.5 0.6 pad_add_fusion.meta_ref
  19.2 70.7 %all-gather.7.cloned.1.call-done = bf16[32,512,128]{2,1,0:T(8,128)(2,1)} async-done(((bf16[2,512,128]{2,1,0:T(8,128)(2,1)}), bf16[32,512,128]{2,1,0:T(8,128)(2,1)}) %all-gather.7.cloned.1.call-update) | async-done | bytes 4194320 | tf_op jit(solution)/shard_map/all_gather | solution.py:133
  89.9 7.7 %shard_map.120 = bf16[512,128]{1,0:T(8,128)(2,1)} custom-call(s32[17]{0:T(128)} %pad_add_fusion.meta_ref, bf16[512,256]{1,0:T(8,128)(2,1)} %q_ref.3, s32[512,1]{1,0:T(8,128)} %copy.51.qseg_ref, s32[16,1,512]{2,1,0:T(1,128)} %bitcast.90, bf16[16,2,512,128]{3,2,1,0:T(8,128)(2,1)} %bitcast.79, bf16[16,2,512,128]{3,2,1,0:T(8,128)(2,1)} %bitcast.80), custom_call_target="tpu_custom_call" | custom-call | tf_op jit(solution)/shard_map/pallas_call | solution.py:96
  97.6 70.9 %all-gather.5.cloned.1.call-done = bf16[32,512,128]{2,1,0:T(8,128)(2,1)} async-done(((bf16[2,512,128]{2,1,0:T(8,128)(2,1)}), bf16[32,512,128]{2,1,0:T(8,128)(2,1)}) %all-gather.5.cloned.1.call-update) | async-done | bytes 4194320 | tf_op jit(solution)/shard_map/all_gather | solution.py:133
  168.5 7.9 %shard_map.121 = bf16[512,128]{1,0:T(8,128)(2,1)} custom-call(s32[17]{0:T(128)} %pad_add_fusion.meta_ref, bf16[512,256]{1,0:T(8,128)(2,1)} %q_ref.3, s32[512,1]{1,0:T(8,128)} %copy.51.qseg_ref, s32[16,1,512]{2,1,0:T(1,128)} %bitcast.91, bf16[16,2,512,128]{3,2,1,0:T(8,128)(2,1)} %bitcast.81, bf16[16,2,512,128]{3,2,1,0:T(8,128)(2,1)} %bitcast.82), custom_call_target="tpu_custom_call" | custom-call | tf_op jit(solution)/shard_map/pallas_call | solution.py:96
  176.4 0.9 pad_maximum_fusion.3
  177.3 4.2 %convolution_convert_fusion = bf16[512,7168]{1,0:T(8,128)(2,1)S(1)} fusion(bf16[512,256]{1,0:T(8,128)(2,1)S(1)} %bitcast.86, bf16[256,7168]{1,0:T(8,128)(2,1)} %param.16), kind=kOutput, calls=%fused_computation.2 | convolution fusion | flops 1882718208 | bytes 11272192 | tf_op jit(solution)/shard_map/dot_general | solution.py:175
  181.6 2.4 dynamic-slice_bitcast_fusion
  184.0 1.6 copy-done
  185.6 1.5 copy.54
  187.1 23.3 %all-to-all-start = ((bf16[16,2,4,2,16,256]{5,4,3,2,1,0:T(8,128)(2,1)}), bf16[16,2,4,2,16,256]{5,4,3,2,1,0:T(8,128)(2,1)S(1)}, u32[]{:S(2)}, u32[]{:S(2)}) async-start(bf16[16,2,4,2,16,256]{5,4,3,2,1,0:T(8,128)(2,1)} %copy.54), calls=%async_computation | async-start | bytes 4194304 | tf_op jit(solution)/shard_map/all_to_all | solution.py:42
  210.4 4.4 %convert_add_fusion = f32[4,2,32,7168]{3,2,1,0:T(8,128)S(1)} fusion(bf16[4,2,32,7168]{3,2,1,0:T(8,128)(2,1)} %collective-permute-done, bf16[2,4,2,32,7168]{4,3,2,1,0:T(8,128)(2,1)} %bitcast.78, s32[]{:T(128)S(6)} %select_n.105), kind=kLoop, calls=%fused_computation.3 | loop fusion | flops 5505024 | bytes 14680068 | tf_op jit(solution)/shard_map/add | solution.py:166
  214.8 2.9 %copy-done.1 = f32[4,2,32,7168]{3,2,1,0:T(8,128)} copy-done((f32[4,2,32,7168]{3,2,1,0:T(8,128)}, f32[4,2,32,7168]{3,2,1,0:T(8,128)S(1)}, u32[]{:S(2)}) %copy-start.1) | copy-done | bytes 7340056
  217.8 1.6 fusion.2
  219.4 1.5 collective-permute-start.1
  220.8 2.7 collective-permute-start.2
  223.5 1.5 collective-permute-start.3
  225.0 0.1 select_reduce_fusion.1
  225.1 38.2 %all-to-all-done = bf16[16,2,4,2,16,256]{5,4,3,2,1,0:T(8,128)(2,1)S(1)} async-done(((bf16[16,2,4,2,16,256]{5,4,3,2,1,0:T(8,128)(2,1)}), bf16[16,2,4,2,16,256]{5,4,3,2,1,0:T(8,128)(2,1)S(1)}, u32[]{:S(2)}, u32[]{:S(2)}) %all-to-all-start) | async-done | bytes 2097184 | tf_op jit(solution)/shard_map/all_to_all | solution.py:42
  263.4 1.6 copy.55
  265.0 2.3 gather_fusion.1
  267.3 2.7 fusion.1
  270.1 0.1 collective-permute-start.4
  270.2 0.3 select_bitcast_fusion
  270.5 0.1 slice_bitcast_fusion
  270.6 1.1 copy.56
  271.7 1.1 copy.57
  272.7 9.0 %collective-permute-done.4 = bf16[32,7168]{1,0:T(8,128)(2,1)S(1)} collective-permute-done((bf16[32,7168]{1,0:T(8,128)(2,1)S(1)}, bf16[32,7168]{1,0:T(8,128)(2,1)S(1)}, u32[]{:S(2)}, u32[]{:S(2)}) %collective-permute-start.4) | collective-permute-done | bytes 458784 | tf_op jit(solution)/shard_map/ppermute | solution.py:166
  281.8 0.8 fusion.5
  (36 shorter events, 0.3 us)
Async XLA Ops:
  7.2 2.9 %copy-start.6 = (s32[8192]{0:T(1024)S(1)}, s32[8192]{0:T(1024)}, u32[]{:S(2)}) copy-start(s32[8192]{0:T(1024)} %param.14) | copy-start | bytes 98308
  7.2 4.4 %copy-start.7 = (s32[512]{0:T(512)S(1)}, s32[512]{0:T(512)}, u32[]{:S(2)}) copy-start(s32[512]{0:T(512)} %param.19) | copy-start | bytes 6148
  7.2 5.5 %copy-start.4 = (bf16[4,512,256]{2,1,0:T(8,128)(2,1)S(1)}, bf16[4,512,256]{2,1,0:T(8,128)(2,1)}, u32[]{:S(2)}) copy-start(bf16[4,512,256]{2,1,0:T(8,128)(2,1)} %param.17) | copy-start | bytes 3145732
  7.2 5.5 %copy-start.3 = (bf16[4,512,256]{2,1,0:T(8,128)(2,1)S(1)}, bf16[4,512,256]{2,1,0:T(8,128)(2,1)}, u32[]{:S(2)}) copy-start(bf16[4,512,256]{2,1,0:T(8,128)(2,1)} %param.18) | copy-start | bytes 3145732
  7.2 82.7 %all-gather.7.cloned.1.call-start = ((), (), s32[]{:S(2)}) async-start(), calls=%async_computation.2 | async-start | bytes 4456448 | tf_op jit(solution)/shard_map/all_gather | solution.py:133
  9.3 159.2 %all-gather.5.cloned.1.call-start = ((), (), s32[]{:S(2)}) async-start(), calls=%async_computation.1 | async-start | bytes 4456448 | tf_op jit(solution)/shard_map/all_gather | solution.py:133
  168.5 7.9 %copy-start.5 = (bf16[512,128]{1,0:T(8,128)(2,1)S(1)}, bf16[512,128]{1,0:T(8,128)(2,1)}, u32[]{:S(2)}) copy-start(bf16[512,128]{1,0:T(8,128)(2,1)} %shard_map.120) | copy-start | bytes 393220
  177.3 4.2 %copy-start.2 = (bf16[512,256]{1,0:T(8,128)(2,1)}, bf16[512,256]{1,0:T(8,128)(2,1)S(1)}, u32[]{:S(2)}) copy-start(bf16[512,256]{1,0:T(8,128)(2,1)S(1)} %pad_maximum_fusion.3) | copy-start | bytes 786436
  181.6 4.0 %copy-start = (bf16[512,7168]{1,0:T(8,128)(2,1)}, bf16[512,7168]{1,0:T(8,128)(2,1)S(1)}, u32[]{:S(2)}) copy-start(bf16[512,7168]{1,0:T(8,128)(2,1)S(1)} %convolution_convert_fusion) | copy-start | bytes 22020100
  185.6 24.8 %collective-permute-start = (bf16[4,2,32,7168]{3,2,1,0:T(8,128)(2,1)}, bf16[4,2,32,7168]{3,2,1,0:T(8,128)(2,1)}, u32[]{:S(2)}, u32[]{:S(2)}) collective-permute-start(bf16[4,2,32,7168]{3,2,1,0:T(8,128)(2,1)} %dynamic-slice_bitcast_fusion), channel_id=1, source_target_pairs={{0,1},{1,0},{2,3},{3,2},{4,5},{5,4},{6,7},{7,6},{8,9},{9,8},{10,11... | collective-permute-start | bytes 11010056 | tf_op jit(solution)/shard_map/ppermute | solution.py:166
  187.1 76.2 %all-to-all-start = ((bf16[16,2,4,2,16,256]{5,4,3,2,1,0:T(8,128)(2,1)}), bf16[16,2,4,2,16,256]{5,4,3,2,1,0:T(8,128)(2,1)S(1)}, u32[]{:S(2)}, u32[]{:S(2)}) async-start(bf16[16,2,4,2,16,256]{5,4,3,2,1,0:T(8,128)(2,1)} %copy.54), calls=%async_computation | async-start | bytes 4194304 | tf_op jit(solution)/shard_map/all_to_all | solution.py:42
  214.8 2.9 %copy-start.1 = (f32[4,2,32,7168]{3,2,1,0:T(8,128)}, f32[4,2,32,7168]{3,2,1,0:T(8,128)S(1)}, u32[]{:S(2)}) copy-start(f32[4,2,32,7168]{3,2,1,0:T(8,128)S(1)} %convert_add_fusion) | copy-start | bytes 22020100
  219.4 47.9 %collective-permute-start.1 = (bf16[2,32,7168]{2,1,0:T(8,128)(2,1)}, bf16[2,32,7168]{2,1,0:T(8,128)(2,1)}, u32[]{:S(2)}, u32[]{:S(2)}) collective-permute-start(bf16[2,32,7168]{2,1,0:T(8,128)(2,1)} %get-tuple-element.35), channel_id=1, source_target_pairs={{0,4},{4,8},{8,12},{12,0},{1,5},{5,9},{9,13},{13,1},{2,6},{6,10},{... | collective-permute-start | bytes 2752520 | tf_op jit(solution)/shard_map/ppermute | solution.py:166
  220.8 46.5 %collective-permute-start.2 = (bf16[2,32,7168]{2,1,0:T(8,128)(2,1)}, bf16[2,32,7168]{2,1,0:T(8,128)(2,1)}, u32[]{:S(2)}, u32[]{:S(2)}) collective-permute-start(bf16[2,32,7168]{2,1,0:T(8,128)(2,1)} %get-tuple-element.37), channel_id=1, source_target_pairs={{0,8},{4,12},{8,0},{12,4},{1,9},{5,13},{9,1},{13,5},{2,10},{6,14},... | collective-permute-start | bytes 2752520 | tf_op jit(solution)/shard_map/ppermute | solution.py:166
  223.5 43.8 %collective-permute-start.3 = (bf16[2,32,7168]{2,1,0:T(8,128)(2,1)S(1)}, bf16[2,32,7168]{2,1,0:T(8,128)(2,1)}, u32[]{:S(2)}, u32[]{:S(2)}) collective-permute-start(bf16[2,32,7168]{2,1,0:T(8,128)(2,1)S(1)} %get-tuple-element.36), channel_id=1, source_target_pairs={{0,12},{4,0},{8,4},{12,8},{1,13},{5,1},{9,5},{13,9},{2,14},{6,2},{... | collective-permute-start | bytes 2752520 | tf_op jit(solution)/shard_map/ppermute | solution.py:166
  270.1 11.7 %collective-permute-start.4 = (bf16[32,7168]{1,0:T(8,128)(2,1)S(1)}, bf16[32,7168]{1,0:T(8,128)(2,1)S(1)}, u32[]{:S(2)}, u32[]{:S(2)}) collective-permute-start(bf16[32,7168]{1,0:T(8,128)(2,1)S(1)} %fusion.6), channel_id=1, source_target_pairs={{0,2},{2,0},{1,3},{3,1},{4,6},{6,4},{5,7},{7,5},{8,10},{10,8},{9,1... | collective-permute-start | bytes 1376264 | tf_op jit(solution)/shard_map/ppermute | solution.py:166
Sparse Core Ops, SparseCore 0:
  11.0 78.7 all-gather.6
  92.9 75.5 all-gather.4

commit v5 on v4

--- a/solution.py
+++ b/solution.py
@@ -88,7 +88,8 @@
 
 
 def attend_head(meta, queries, qseg, kseg, kv, head):
-    block_count, _, block_rows, width = kv.shape
+    block_count, _, block_rows, _ = kv.shape
+    width = HD
     rows = queries.shape[0]
     kernel = functools.partial(
         attention_kernel, block_count=block_count, block_rows=block_rows, scale=1.0 / math.sqrt(HD)
@@ -102,8 +103,8 @@
                 pl.BlockSpec((Q_ROWS, width), lambda i, meta: (i, head)),
                 pl.BlockSpec((Q_ROWS, 1), lambda i, meta: (i, 0)),
                 pl.BlockSpec((block_count, 1, block_rows), lambda i, meta: (0, 0, 0)),
-                pl.BlockSpec((block_count, None, block_rows, width), lambda i, meta: (0, 0, 0, 0)),
-                pl.BlockSpec((block_count, None, block_rows, width), lambda i, meta: (0, 1, 0, 0)),
+                pl.BlockSpec((block_count, None, block_rows, width), lambda i, meta: (0, 0, 0, head)),
+                pl.BlockSpec((block_count, None, block_rows, width), lambda i, meta: (0, 1, 0, head)),
             ],
             out_specs=pl.BlockSpec((Q_ROWS, width), lambda i, meta: (i, 0)),
         ),
@@ -126,14 +127,10 @@
     meta = jnp.concatenate([live.astype(jnp.int32), position.astype(jnp.int32)[None]])
     qseg = query_seg[:, None]
     kseg = seg_blocks[:, None, :]
-    outs = []
-    for head in range(head_count):
-        columns = slice(head * HD, (head + 1) * HD)
-        kv = jnp.stack([stretch_keys[:, columns], stretch_values[:, columns]])
-        kv_all = lax.all_gather(kv, SEQ, axis=0, tiled=False)
-        if outs:
-            moved, kv_all, outs = lax.optimization_barrier((moved, kv_all, outs))
-        outs.append(attend_head(meta, queries, qseg, kseg, kv_all, head))
+    kv = jnp.stack([stretch_keys, stretch_values])
+    kv_all = lax.all_gather(kv, SEQ, axis=0, tiled=False)
+    moved, kv_all = lax.optimization_barrier((moved, kv_all))
+    outs = [attend_head(meta, queries, qseg, kseg, kv_all, head) for head in range(head_count)]
     return (jnp.concatenate(outs, axis=1), moved)
 
 

time: 290 us -> 270 us (0.931); the launches traced: 289 us -> 266 us
  waiting for transfers between devices: 189 us -> 139 us
  starting transfers between devices: 29.1 us -> 51.5 us
  Pallas kernels: 15.6 us -> 18.6 us
    all_gather x2 -> x1, waiting for transfers between devices: 142 us -> 97.3 us  [attention(): kv_all = lax.all_gather(kv, SEQ, axis=0, tiled=False)]
    all_to_all x1, starting transfers between devices: 23.3 us -> 41.6 us  [place_pages(): lax.all_to_all(outgoing, SEQ, split_axis=0, concat_axis=0, tiled=True)]
    all_to_all x1, waiting for transfers between devices: 38.2 us -> 33.7 us  [place_pages(): lax.all_to_all(outgoing, SEQ, split_axis=0, concat_axis=0, tiled=True)]
    ppermute x5, starting transfers between devices: 5.7 us -> 9.87 us  [exchange(): total = total + lax.ppermute(sent, name, pairs).astype(jnp.float32)]
    pallas_call x2, Pallas kernels: 15.6 us -> 18.6 us  [attend_head(): pl.pallas_call(kernel, grid_spec=pltpu.PrefetchScalarGridSpec(num_scalar_...]
    unnamed x18 -> x14, local copies, waits for them, and re-layouts: 6.74 us -> 6.71 us
  transfers between devices with their start and end apart: 8 -> 7, of which waited for: 4 -> 4; matrix products, arithmetic and copies ran while one was open for 8% -> 9% of each run, Pallas kernels for 3% -> 0%
where the time goes in v5:
time: 270 us; the launch traced here: 266 us
  waiting for transfers between devices  139 us (51%)
  starting transfers between devices  51.5 us (19%)
  local copies, waits for them, and re-layouts  22 us (8%)
  Pallas kernels  18.6 us (7%)
  other arithmetic  15.9 us (6%)
  between operations  14.3 us (5%)
  matrix products  4.2 us (2%)
    all_gather x1, waiting for transfers between devices, attention(): kv_all = lax.all_gather(kv, SEQ, axis=0, tiled=False)  97.3 us
    all_to_all x1, starting transfers between devices, place_pages(): lax.all_to_all(outgoing, SEQ, split_axis=0, concat_axis=0, tiled=True)  41.6 us
    all_to_all x1, waiting for transfers between devices, place_pages(): lax.all_to_all(outgoing, SEQ, split_axis=0, concat_axis=0, tiled=True)  33.7 us
    pallas_call x2, Pallas kernels, attend_head(): pl.pallas_call(kernel, grid_spec=pltpu.PrefetchScalarGridSpec(num_scalar_...  18.6 us
    ppermute x5, starting transfers between devices, exchange(): total = total + lax.ppermute(sent, name, pairs).astype(jnp.float32)  9.87 us
    ppermute x5, waiting for transfers between devices, exchange(): total = total + lax.ppermute(sent, name, pairs).astype(jnp.float32)  8.45 us
    add x2, other arithmetic, exchange(): total = total + lax.ppermute(sent, name, pairs).astype(jnp.float32)  7.09 us
    unnamed x14, local copies, waits for them, and re-layouts  6.71 us
  transfers between devices with their start and end apart: 7, of which 4 were waited for; matrix products, arithmetic and copies ran while one was open for 9% of the time, Pallas kernels for 0%

profile of v5, /device:TPU:8, one launch (start us, length us, event | category | flops | bytes accessed | tf_op | source)
XLA Modules:
  0.0 266.0 jit_solution(6406605541405007213)
XLA Ops:
  7.2 2.0 pad_maximum_fusion.1
  9.3 0.8 reshape.109
  10.1 0.8 reshape.110
  10.9 0.5 constant_dynamic-slice_fusion
  11.4 0.1 copy.49
  11.5 0.1 select_reduce_fusion.2
  11.6 0.1 iota_add_fusion
  11.7 0.1 add.130
  11.8 0.4 fusion.10
  12.2 0.1 select_reduce_fusion
  12.3 0.1 reduce_sum.31
  12.4 1.5 pad_maximum_fusion
  14.0 2.3 gather_fusion
  16.2 0.3 select_bitcast_fusion.1
  16.5 0.2 copy.50
  16.7 0.9 copy.51.qseg_ref
  17.6 0.8 fusion.11
  18.4 0.7 fusion.15
  19.1 0.6 pad_add_fusion.meta_ref
  19.7 97.3 %all-gather.3.cloned.1.call-done = bf16[32,512,256]{2,1,0:T(8,128)(2,1)} async-done(((bf16[2,512,256]{2,1,0:T(8,128)(2,1)}), bf16[32,512,256]{2,1,0:T(8,128)(2,1)}) %all-gather.3.cloned.1.call-update) | async-done | bytes 8388624 | tf_op jit(solution)/shard_map/all_gather | solution.py:131
  117.0 9.2 %shard_map.120 = bf16[512,128]{1,0:T(8,128)(2,1)} custom-call(s32[17]{0:T(128)} %pad_add_fusion.meta_ref, bf16[512,256]{1,0:T(8,128)(2,1)} %q_ref.3, s32[512,1]{1,0:T(8,128)} %copy.51.qseg_ref, s32[16,1,512]{2,1,0:T(1,128)} %bitcast.83, bf16[16,2,512,256]{3,2,1,0:T(8,128)(2,1)} %bitcast.70, bf16[16,2,512,256]{3,2,1,0:T(8,128)(2,1)} %bitcast.71), custom_call_target="tpu_custom_call" | custom-call | tf_op jit(solution)/shard_map/pallas_call | solution.py:97
  126.3 9.4 %shard_map.121 = bf16[512,128]{1,0:T(8,128)(2,1)} custom-call(s32[17]{0:T(128)} %pad_add_fusion.meta_ref, bf16[512,256]{1,0:T(8,128)(2,1)} %q_ref.3, s32[512,1]{1,0:T(8,128)} %copy.51.qseg_ref, s32[16,1,512]{2,1,0:T(1,128)} %bitcast.84, bf16[16,2,512,256]{3,2,1,0:T(8,128)(2,1)} %bitcast.72, bf16[16,2,512,256]{3,2,1,0:T(8,128)(2,1)} %bitcast.73), custom_call_target="tpu_custom_call" | custom-call | tf_op jit(solution)/shard_map/pallas_call | solution.py:97
  135.6 0.9 pad_maximum_fusion.2
  136.6 4.2 %convolution_convert_fusion = bf16[512,7168]{1,0:T(8,128)(2,1)S(1)} fusion(bf16[512,256]{1,0:T(8,128)(2,1)S(1)} %bitcast.79, bf16[256,7168]{1,0:T(8,128)(2,1)} %param.16), kind=kOutput, calls=%fused_computation.2 | convolution fusion | flops 1882718208 | bytes 11272192 | tf_op jit(solution)/shard_map/dot_general | solution.py:172
  140.8 2.4 dynamic-slice_bitcast_fusion
  143.3 1.6 copy-done
  144.9 1.6 copy.54
  146.4 41.6 %all-to-all-start = ((bf16[16,2,4,2,16,256]{5,4,3,2,1,0:T(8,128)(2,1)}), bf16[16,2,4,2,16,256]{5,4,3,2,1,0:T(8,128)(2,1)S(1)}, u32[]{:S(2)}, u32[]{:S(2)}) async-start(bf16[16,2,4,2,16,256]{5,4,3,2,1,0:T(8,128)(2,1)} %copy.54), calls=%async_computation | async-start | bytes 4194304 | tf_op jit(solution)/shard_map/all_to_all | solution.py:42
  188.0 4.4 %convert_add_fusion = f32[4,2,32,7168]{3,2,1,0:T(8,128)S(1)} fusion(bf16[4,2,32,7168]{3,2,1,0:T(8,128)(2,1)} %collective-permute-done, bf16[2,4,2,32,7168]{4,3,2,1,0:T(8,128)(2,1)} %bitcast.75, s32[]{:T(128)S(6)} %select_n.105), kind=kLoop, calls=%fused_computation.3 | loop fusion | flops 5505024 | bytes 14680068 | tf_op jit(solution)/shard_map/add | solution.py:163
  192.4 2.9 %copy-done.1 = f32[4,2,32,7168]{3,2,1,0:T(8,128)} copy-done((f32[4,2,32,7168]{3,2,1,0:T(8,128)}, f32[4,2,32,7168]{3,2,1,0:T(8,128)S(1)}, u32[]{:S(2)}) %copy-start.1) | copy-done | bytes 7340056
  195.4 1.6 fusion.2
  196.9 1.5 collective-permute-start.1
  198.4 2.7 %collective-permute-start.2 = (bf16[2,32,7168]{2,1,0:T(8,128)(2,1)}, bf16[2,32,7168]{2,1,0:T(8,128)(2,1)}, u32[]{:S(2)}, u32[]{:S(2)}) collective-permute-start(bf16[2,32,7168]{2,1,0:T(8,128)(2,1)} %get-tuple-element.35), channel_id=1, source_target_pairs={{0,8},{4,12},{8,0},{12,4},{1,9},{5,13},{9,1},{13,5},{2,10},{6,14},... | collective-permute-start | bytes 2752520 | tf_op jit(solution)/shard_map/ppermute | solution.py:163
  201.1 1.5 collective-permute-start.3
  202.5 0.1 select_reduce_fusion.1
  202.7 33.7 %all-to-all-done = bf16[16,2,4,2,16,256]{5,4,3,2,1,0:T(8,128)(2,1)S(1)} async-done(((bf16[16,2,4,2,16,256]{5,4,3,2,1,0:T(8,128)(2,1)}), bf16[16,2,4,2,16,256]{5,4,3,2,1,0:T(8,128)(2,1)S(1)}, u32[]{:S(2)}, u32[]{:S(2)}) %all-to-all-start) | async-done | bytes 2097184 | tf_op jit(solution)/shard_map/all_to_all | solution.py:42
  236.4 1.6 copy.55
  238.0 2.3 gather_fusion.1
  240.3 1.0 collective-permute-done.2
  241.3 2.7 %fusion.1 = f32[2,32,7168]{2,1,0:T(8,128)S(1)} fusion(bf16[2,32,7168]{2,1,0:T(8,128)(2,1)} %collective-permute-done.3, bf16[2,32,7168]{2,1,0:T(8,128)(2,1)} %collective-permute-done.2, bf16[2,32,7168]{2,1,0:T(8,128)(2,1)} %collective-permute-done.1, f32[4,2,32,7168]{3,2,1,0:T(8,128)} %copy-done.1, s32[]{:T(128)S(6)} %select_n.108), kind=kLoop, calls=%fused_computation.10 | loop fusion | flops 2752512 | bytes 6422532 | tf_op jit(solution)/shard_map/add | solution.py:163
  244.0 0.1 fusion.6
  244.0 4.3 %collective-permute-start.4 = (bf16[32,7168]{1,0:T(8,128)(2,1)S(1)}, bf16[32,7168]{1,0:T(8,128)(2,1)S(1)}, u32[]{:S(2)}, u32[]{:S(2)}) collective-permute-start(bf16[32,7168]{1,0:T(8,128)(2,1)S(1)} %fusion.6), channel_id=1, source_target_pairs={{0,2},{2,0},{1,3},{3,1},{4,6},{6,4},{5,7},{7,5},{8,10},{10,8},{9,1... | collective-permute-start | bytes 1376264 | tf_op jit(solution)/shard_map/ppermute | solution.py:163
  248.3 0.3 select_bitcast_fusion
  248.5 0.1 slice_bitcast_fusion
  248.7 1.1 copy.56
  249.8 1.1 copy.57
  250.8 7.5 %collective-permute-done.4 = bf16[32,7168]{1,0:T(8,128)(2,1)S(1)} collective-permute-done((bf16[32,7168]{1,0:T(8,128)(2,1)S(1)}, bf16[32,7168]{1,0:T(8,128)(2,1)S(1)}, u32[]{:S(2)}, u32[]{:S(2)}) %collective-permute-start.4) | collective-permute-done | bytes 458784 | tf_op jit(solution)/shard_map/ppermute | solution.py:163
  258.3 0.8 fusion.5
  (27 shorter events, 0.2 us)
Async XLA Ops:
  7.2 5.2 %copy-start.4 = (bf16[4,512,256]{2,1,0:T(8,128)(2,1)S(1)}, bf16[4,512,256]{2,1,0:T(8,128)(2,1)}, u32[]{:S(2)}) copy-start(bf16[4,512,256]{2,1,0:T(8,128)(2,1)} %param.17) | copy-start | bytes 3145732
  7.2 5.2 %copy-start.3 = (bf16[4,512,256]{2,1,0:T(8,128)(2,1)S(1)}, bf16[4,512,256]{2,1,0:T(8,128)(2,1)}, u32[]{:S(2)}) copy-start(bf16[4,512,256]{2,1,0:T(8,128)(2,1)} %param.18) | copy-start | bytes 3145732
  7.2 109.9 %all-gather.3.cloned.1.call-start = ((), (), s32[]{:S(2)}) async-start(), calls=%async_computation.1 | async-start | bytes 8912896 | tf_op jit(solution)/shard_map/all_gather | solution.py:131
  126.3 9.4 %copy-start.5 = (bf16[512,128]{1,0:T(8,128)(2,1)S(1)}, bf16[512,128]{1,0:T(8,128)(2,1)}, u32[]{:S(2)}) copy-start(bf16[512,128]{1,0:T(8,128)(2,1)} %shard_map.120) | copy-start | bytes 393220
  136.6 4.2 %copy-start.2 = (bf16[512,256]{1,0:T(8,128)(2,1)}, bf16[512,256]{1,0:T(8,128)(2,1)S(1)}, u32[]{:S(2)}) copy-start(bf16[512,256]{1,0:T(8,128)(2,1)S(1)} %pad_maximum_fusion.2) | copy-start | bytes 786436
  140.8 4.0 %copy-start = (bf16[512,7168]{1,0:T(8,128)(2,1)}, bf16[512,7168]{1,0:T(8,128)(2,1)S(1)}, u32[]{:S(2)}) copy-start(bf16[512,7168]{1,0:T(8,128)(2,1)S(1)} %convolution_convert_fusion) | copy-start | bytes 22020100
  144.9 43.1 %collective-permute-start = (bf16[4,2,32,7168]{3,2,1,0:T(8,128)(2,1)}, bf16[4,2,32,7168]{3,2,1,0:T(8,128)(2,1)}, u32[]{:S(2)}, u32[]{:S(2)}) collective-permute-start(bf16[4,2,32,7168]{3,2,1,0:T(8,128)(2,1)} %dynamic-slice_bitcast_fusion), channel_id=1, source_target_pairs={{0,1},{1,0},{2,3},{3,2},{4,5},{5,4},{6,7},{7,6},{8,9},{9,8},{10,11... | collective-permute-start | bytes 11010056 | tf_op jit(solution)/shard_map/ppermute | solution.py:163
  146.4 89.9 %all-to-all-start = ((bf16[16,2,4,2,16,256]{5,4,3,2,1,0:T(8,128)(2,1)}), bf16[16,2,4,2,16,256]{5,4,3,2,1,0:T(8,128)(2,1)S(1)}, u32[]{:S(2)}, u32[]{:S(2)}) async-start(bf16[16,2,4,2,16,256]{5,4,3,2,1,0:T(8,128)(2,1)} %copy.54), calls=%async_computation | async-start | bytes 4194304 | tf_op jit(solution)/shard_map/all_to_all | solution.py:42
  192.4 2.9 %copy-start.1 = (f32[4,2,32,7168]{3,2,1,0:T(8,128)}, f32[4,2,32,7168]{3,2,1,0:T(8,128)S(1)}, u32[]{:S(2)}) copy-start(f32[4,2,32,7168]{3,2,1,0:T(8,128)S(1)} %convert_add_fusion) | copy-start | bytes 22020100
  196.9 43.3 %collective-permute-start.1 = (bf16[2,32,7168]{2,1,0:T(8,128)(2,1)}, bf16[2,32,7168]{2,1,0:T(8,128)(2,1)}, u32[]{:S(2)}, u32[]{:S(2)}) collective-permute-start(bf16[2,32,7168]{2,1,0:T(8,128)(2,1)} %get-tuple-element.33), channel_id=1, source_target_pairs={{0,4},{4,8},{8,12},{12,0},{1,5},{5,9},{9,13},{13,1},{2,6},{6,10},{... | collective-permute-start | bytes 2752520 | tf_op jit(solution)/shard_map/ppermute | solution.py:163
  198.4 42.8 %collective-permute-start.2 = (bf16[2,32,7168]{2,1,0:T(8,128)(2,1)}, bf16[2,32,7168]{2,1,0:T(8,128)(2,1)}, u32[]{:S(2)}, u32[]{:S(2)}) collective-permute-start(bf16[2,32,7168]{2,1,0:T(8,128)(2,1)} %get-tuple-element.35), channel_id=1, source_target_pairs={{0,8},{4,12},{8,0},{12,4},{1,9},{5,13},{9,1},{13,5},{2,10},{6,14},... | collective-permute-start | bytes 2752520 | tf_op jit(solution)/shard_map/ppermute | solution.py:163
  201.1 40.2 %collective-permute-start.3 = (bf16[2,32,7168]{2,1,0:T(8,128)(2,1)S(1)}, bf16[2,32,7168]{2,1,0:T(8,128)(2,1)}, u32[]{:S(2)}, u32[]{:S(2)}) collective-permute-start(bf16[2,32,7168]{2,1,0:T(8,128)(2,1)S(1)} %get-tuple-element.34), channel_id=1, source_target_pairs={{0,12},{4,0},{8,4},{12,8},{1,13},{5,1},{9,5},{13,9},{2,14},{6,2},{... | collective-permute-start | bytes 2752520 | tf_op jit(solution)/shard_map/ppermute | solution.py:163
  244.0 14.3 %collective-permute-start.4 = (bf16[32,7168]{1,0:T(8,128)(2,1)S(1)}, bf16[32,7168]{1,0:T(8,128)(2,1)S(1)}, u32[]{:S(2)}, u32[]{:S(2)}) collective-permute-start(bf16[32,7168]{1,0:T(8,128)(2,1)S(1)} %fusion.6), channel_id=1, source_target_pairs={{0,2},{2,0},{1,3},{3,1},{4,6},{6,4},{5,7},{7,5},{8,10},{10,8},{9,1... | collective-permute-start | bytes 1376264 | tf_op jit(solution)/shard_map/ppermute | solution.py:163
Sparse Core Ops, SparseCore 0:
  11.0 105.9 all-gather.2

commit v6 on v5

--- a/solution.py
+++ b/solution.py
@@ -46,69 +46,72 @@
     return (placed[0], placed[1])
 
 
-def attention_kernel(meta_ref, q_ref, qseg_ref, kseg_ref, k_ref, v_ref, o_ref, *, block_count, block_rows, scale):
-    chunk = pl.program_id(0)
+def attention_kernel(meta_ref, q_ref, qseg_ref, kseg_ref, k_ref, v_ref, o_ref, *, block_count, scale):
+    chunk = pl.program_id(1)
     query_block = meta_ref[block_count]
     q = q_ref[...]
     qseg = qseg_ref[...]
     rows = q.shape[0]
-    qpos = query_block * block_rows + chunk * rows + lax.broadcasted_iota(jnp.int32, (rows, 1), 0)
-    kiota = lax.broadcasted_iota(jnp.int32, (1, block_rows), 1)
-
-    def scores(c):
-        s = lax.dot_general(
-            q, k_ref[c], (((1,), (1,)), ((), ())), preferred_element_type=jnp.float32
-        ) * scale
-        allowed = (qseg == kseg_ref[c]) & (c * block_rows + kiota <= qpos)
-        return s, allowed
-
-    def max_body(c, m):
-        def live(m):
-            s, allowed = scores(c)
-            return jnp.maximum(m, jnp.max(jnp.where(allowed, s, -jnp.inf), axis=1, keepdims=True))
-
-        return lax.cond(meta_ref[c] != 0, live, lambda m: m, m)
-
-    m = lax.fori_loop(0, block_count, max_body, jnp.full((rows, 1), -jnp.inf, jnp.float32))
-
-    def sum_body(c, carry):
-        def live(carry):
-            l, acc = carry
-            s, allowed = scores(c)
-            w = jnp.where(allowed, jnp.exp(s - m), 0.0)
-            l = l + jnp.sum(w, axis=1, keepdims=True)
-            acc = acc + jnp.dot(w.astype(jnp.bfloat16), v_ref[c], preferred_element_type=jnp.float32)
-            return (l, acc)
-
-        return lax.cond(meta_ref[c] != 0, live, lambda x: x, carry)
-
-    initial = (jnp.zeros((rows, 1), jnp.float32), jnp.zeros((rows, q.shape[1]), jnp.float32))
-    l, acc = lax.fori_loop(0, block_count, sum_body, initial)
-    o_ref[...] = (acc / l).astype(o_ref.dtype)
-
-
-def attend_head(meta, queries, qseg, kseg, kv, head):
+    block_rows = k_ref.shape[1]
+    local_pos = chunk * rows + lax.broadcasted_iota(jnp.int32, (rows, 1), 0)
+    key_pos = lax.broadcasted_iota(jnp.int32, (1, block_rows), 1)
+
+    def step(c, carry, allowed):
+        row_best, weight_sum, numerator = carry
+        s = lax.dot_general(q, k_ref[c], (((1,), (1,)), ((), ())), preferred_element_type=jnp.float32) * scale
+        if allowed is not None:
+            s = jnp.where(allowed, s, -jnp.inf)
+        new_best = jnp.maximum(row_best, jnp.max(s, axis=1, keepdims=True))
+        rescale = jnp.exp(row_best - new_best)
+        w = jnp.exp(s - new_best)
+        weight_sum = rescale * weight_sum + jnp.sum(w, axis=1, keepdims=True)
+        added = jnp.dot(w.astype(jnp.bfloat16), v_ref[c], preferred_element_type=jnp.float32)
+        return (new_best, weight_sum, rescale * numerator + added)
+
+    initial = (
+        jnp.full((rows, 1), -jnp.inf, jnp.float32),
+        jnp.zeros((rows, 1), jnp.float32),
+        jnp.zeros((rows, q.shape[1]), jnp.float32),
+    )
+    carry = step(query_block, initial, (qseg == kseg_ref[query_block]) & (key_pos <= local_pos))
+
+    def body(c, carry):
+        flag = meta_ref[c]
+        return lax.cond(
+            flag == 0,
+            lambda x: x,
+            lambda x: lax.cond(
+                flag == 1,
+                lambda y: step(c, y, qseg == kseg_ref[c]),
+                lambda y: step(c, y, None),
+                x,
+            ),
+            carry,
+        )
+
+    _, weight_sum, numerator = lax.fori_loop(0, query_block, body, carry)
+    o_ref[...] = (numerator / weight_sum).astype(o_ref.dtype)
+
+
+def attend(meta, queries, qseg, kseg, kv):
     block_count, _, block_rows, _ = kv.shape
-    width = HD
-    rows = queries.shape[0]
-    kernel = functools.partial(
-        attention_kernel, block_count=block_count, block_rows=block_rows, scale=1.0 / math.sqrt(HD)
-    )
+    rows, feat_width = queries.shape
+    kernel = functools.partial(attention_kernel, block_count=block_count, scale=1.0 / math.sqrt(HD))
     return pl.pallas_call(
         kernel,
         grid_spec=pltpu.PrefetchScalarGridSpec(
             num_scalar_prefetch=1,
-            grid=(rows // Q_ROWS,),
+            grid=(feat_width // HD, rows // Q_ROWS),
             in_specs=[
-                pl.BlockSpec((Q_ROWS, width), lambda i, meta: (i, head)),
-                pl.BlockSpec((Q_ROWS, 1), lambda i, meta: (i, 0)),
-                pl.BlockSpec((block_count, 1, block_rows), lambda i, meta: (0, 0, 0)),
-                pl.BlockSpec((block_count, None, block_rows, width), lambda i, meta: (0, 0, 0, head)),
-                pl.BlockSpec((block_count, None, block_rows, width), lambda i, meta: (0, 1, 0, head)),
+                pl.BlockSpec((Q_ROWS, HD), lambda h, i, meta: (i, h)),
+                pl.BlockSpec((Q_ROWS, 1), lambda h, i, meta: (i, 0)),
+                pl.BlockSpec((block_count, 1, block_rows), lambda h, i, meta: (0, 0, 0)),
+                pl.BlockSpec((block_count, None, block_rows, HD), lambda h, i, meta: (0, 0, 0, h)),
+                pl.BlockSpec((block_count, None, block_rows, HD), lambda h, i, meta: (0, 1, 0, h)),
             ],
-            out_specs=pl.BlockSpec((Q_ROWS, width), lambda i, meta: (i, 0)),
+            out_specs=pl.BlockSpec((Q_ROWS, HD), lambda h, i, meta: (i, h)),
         ),
-        out_shape=jax.ShapeDtypeStruct((rows, width), queries.dtype),
+        out_shape=jax.ShapeDtypeStruct((rows, feat_width), queries.dtype),
     )(meta, queries, qseg, kseg, kv, kv)
 
 
@@ -121,17 +124,16 @@
     query_seg = lax.dynamic_index_in_dim(seg_blocks, position, 0, keepdims=False)
     live_row = lax.dynamic_index_in_dim(block_live, position, 0, keepdims=False)
     block_ids = jnp.arange(block_count, dtype=jnp.int32)
-    live = (block_ids == position) | (
-        (block_ids < position) & (live_row == 1) & (seg_blocks[:, -1] >= query_seg[0])
-    )
-    meta = jnp.concatenate([live.astype(jnp.int32), position.astype(jnp.int32)[None]])
+    earlier = (block_ids < position) & (live_row == 1) & (seg_blocks[:, -1] >= query_seg[0])
+    whole = earlier & (seg_blocks[:, 0] == query_seg[-1])
+    flags = jnp.where(whole, 2, jnp.where(earlier, 1, 0)).astype(jnp.int32)
+    meta = jnp.concatenate([flags, position.astype(jnp.int32)[None]])
     qseg = query_seg[:, None]
     kseg = seg_blocks[:, None, :]
     kv = jnp.stack([stretch_keys, stretch_values])
     kv_all = lax.all_gather(kv, SEQ, axis=0, tiled=False)
     moved, kv_all = lax.optimization_barrier((moved, kv_all))
-    outs = [attend_head(meta, queries, qseg, kseg, kv_all, head) for head in range(head_count)]
-    return (jnp.concatenate(outs, axis=1), moved)
+    return (attend(meta, queries, qseg, kseg, kv_all), moved)
 
 
 def local(

time: 270 us -> 258 us (0.956); the launches traced: 266 us -> 258 us
  Pallas kernels: 18.6 us -> 8.13 us
  waiting for transfers between devices: 139 us -> 144 us
  starting transfers between devices: 51.5 us -> 48.2 us
    pallas_call x2 -> x1, Pallas kernels: 18.6 us -> 8.13 us  [attend(): pl.pallas_call(kernel, grid_spec=pltpu.PrefetchScalarGridSpec(num_scalar_...]
    all_to_all x1, waiting for transfers between devices: 33.7 us -> 38.2 us  [place_pages(): lax.all_to_all(outgoing, SEQ, split_axis=0, concat_axis=0, tiled=True)]
    ppermute x5, starting transfers between devices: 9.87 us -> 5.8 us  [exchange(): total = total + lax.ppermute(sent, name, pairs).astype(jnp.float32)]
    unnamed x14 -> x10, local copies, waits for them, and re-layouts: 6.71 us -> 6.78 us
  transfers between devices with their start and end apart: 7 -> 7, of which waited for: 4 -> 3; matrix products, arithmetic and copies ran while one was open for 9% -> 10% of each run, Pallas kernels for 0% -> 0%
where the time goes in v6:
time: 258 us
  waiting for transfers between devices  144 us (56%)
  starting transfers between devices  48.2 us (19%)
  local copies, waits for them, and re-layouts  23.1 us (9%)
  other arithmetic  15.6 us (6%)
  between operations  14.3 us (6%)
  Pallas kernels  8.13 us (3%)
  matrix products  4.13 us (2%)
    all_gather x1, waiting for transfers between devices, attention(): kv_all = lax.all_gather(kv, SEQ, axis=0, tiled=False)  96.6 us
    all_to_all x1, starting transfers between devices, place_pages(): lax.all_to_all(outgoing, SEQ, split_axis=0, concat_axis=0, tiled=True)  42.3 us
    all_to_all x1, waiting for transfers between devices, place_pages(): lax.all_to_all(outgoing, SEQ, split_axis=0, concat_axis=0, tiled=True)  38.2 us
    ppermute x5, waiting for transfers between devices, exchange(): total = total + lax.ppermute(sent, name, pairs).astype(jnp.float32)  9.39 us
    pallas_call x1, Pallas kernels, attend(): pl.pallas_call(kernel, grid_spec=pltpu.PrefetchScalarGridSpec(num_scalar_...  8.13 us
    add x2, other arithmetic, exchange(): total = total + lax.ppermute(sent, name, pairs).astype(jnp.float32)  7.09 us
    unnamed x10, local copies, waits for them, and re-layouts  6.78 us
    ppermute x5, starting transfers between devices, exchange(): total = total + lax.ppermute(sent, name, pairs).astype(jnp.float32)  5.8 us
  transfers between devices with their start and end apart: 7, of which 3 were waited for; matrix products, arithmetic and copies ran while one was open for 10% of the time, Pallas kernels for 0%

profile of v6, /device:TPU:8, one launch (start us, length us, event | category | flops | bytes accessed | tf_op | source)
XLA Modules:
  0.0 257.6 jit_solution(16172907732298125876)
XLA Ops:
  7.2 0.0 all-gather.3.cloned.1.call-start
  7.2 2.0 pad_maximum_fusion.1
  9.2 0.0 all-gather.3.cloned.1.call-update
  9.3 0.8 reshape.113
  10.1 0.8 reshape.114
  10.9 0.1 copy.45
  11.0 0.1 select_reduce_fusion.2
  11.1 0.1 iota_add_fusion
  11.2 0.1 add.130
  11.3 0.4 fusion.10
  11.7 0.1 select_reduce_fusion
  11.8 0.1 reduce_sum.31
  11.9 1.6 pad_maximum_fusion
  13.5 2.3 gather_fusion
  15.8 0.3 select_bitcast_fusion.1
  16.0 0.2 copy.46
  16.2 0.9 copy.47.qseg_ref
  17.1 0.6 fusion.16
  17.7 1.4 fusion.11
  19.1 0.7 and_select_fusion.2
  19.8 0.6 pad_add_fusion.meta_ref
  20.4 96.6 %all-gather.3.cloned.1.call-done = bf16[32,512,256]{2,1,0:T(8,128)(2,1)} async-done(((bf16[2,512,256]{2,1,0:T(8,128)(2,1)}), bf16[32,512,256]{2,1,0:T(8,128)(2,1)}) %all-gather.3.cloned.1.call-update) | async-done | bytes 8388624 | tf_op jit(solution)/shard_map/all_gather | solution.py:134
  117.0 8.1 %shard_map.120 = bf16[512,256]{1,0:T(8,128)(2,1)} custom-call(s32[17]{0:T(128)} %pad_add_fusion.meta_ref, bf16[512,256]{1,0:T(8,128)(2,1)} %q_ref.1, s32[512,1]{1,0:T(8,128)} %copy.47.qseg_ref, s32[16,1,512]{2,1,0:T(1,128)} %bitcast.82, bf16[16,2,512,256]{3,2,1,0:T(8,128)(2,1)} %bitcast.69, bf16[16,2,512,256]{3,2,1,0:T(8,128)(2,1)} %bitcast.70), custom_call_target="tpu_custom_call" | custom-call | tf_op jit(solution)/shard_map/pallas_call | solution.py:100
  125.1 1.0 copy.48
  126.1 4.1 %convolution_convert_fusion = bf16[512,7168]{1,0:T(8,128)(2,1)S(1)} fusion(bf16[512,256]{1,0:T(8,128)(2,1)S(1)} %bitcast.77, bf16[256,7168]{1,0:T(8,128)(2,1)} %param.16), kind=kOutput, calls=%fused_computation.2 | convolution fusion | flops 1882718208 | bytes 11272192 | tf_op jit(solution)/shard_map/dot_general | solution.py:174
  130.3 2.4 dynamic-slice_bitcast_fusion
  132.6 1.7 copy-done
  134.3 1.6 copy.49
  135.9 42.3 %all-to-all-start = ((bf16[16,2,4,2,16,256]{5,4,3,2,1,0:T(8,128)(2,1)}), bf16[16,2,4,2,16,256]{5,4,3,2,1,0:T(8,128)(2,1)S(1)}, u32[]{:S(2)}, u32[]{:S(2)}) async-start(bf16[16,2,4,2,16,256]{5,4,3,2,1,0:T(8,128)(2,1)} %copy.49), calls=%async_computation | async-start | bytes 4194304 | tf_op jit(solution)/shard_map/all_to_all | solution.py:42
  178.2 4.4 %convert_add_fusion = f32[4,2,32,7168]{3,2,1,0:T(8,128)S(1)} fusion(bf16[4,2,32,7168]{3,2,1,0:T(8,128)(2,1)} %collective-permute-done, bf16[2,4,2,32,7168]{4,3,2,1,0:T(8,128)(2,1)} %bitcast.72, s32[]{:T(128)S(6)} %select_n.115), kind=kLoop, calls=%fused_computation.3 | loop fusion | flops 5505024 | bytes 14680068 | tf_op jit(solution)/shard_map/add | solution.py:165
  182.6 3.0 %copy-done.1 = f32[4,2,32,7168]{3,2,1,0:T(8,128)} copy-done((f32[4,2,32,7168]{3,2,1,0:T(8,128)}, f32[4,2,32,7168]{3,2,1,0:T(8,128)S(1)}, u32[]{:S(2)}) %copy-start.1) | copy-done | bytes 7340056
  185.5 1.6 fusion.2
  187.1 1.5 collective-permute-start.1
  188.6 2.7 %collective-permute-start.2 = (bf16[2,32,7168]{2,1,0:T(8,128)(2,1)}, bf16[2,32,7168]{2,1,0:T(8,128)(2,1)}, u32[]{:S(2)}, u32[]{:S(2)}) collective-permute-start(bf16[2,32,7168]{2,1,0:T(8,128)(2,1)} %get-tuple-element.37), channel_id=1, source_target_pairs={{0,8},{4,12},{8,0},{12,4},{1,9},{5,13},{9,1},{13,5},{2,10},{6,14},... | collective-permute-start | bytes 2752520 | tf_op jit(solution)/shard_map/ppermute | solution.py:165
  191.3 1.5 collective-permute-start.3
  192.8 0.1 select_reduce_fusion.1
  193.0 38.2 %all-to-all-done = bf16[16,2,4,2,16,256]{5,4,3,2,1,0:T(8,128)(2,1)S(1)} async-done(((bf16[16,2,4,2,16,256]{5,4,3,2,1,0:T(8,128)(2,1)}), bf16[16,2,4,2,16,256]{5,4,3,2,1,0:T(8,128)(2,1)S(1)}, u32[]{:S(2)}, u32[]{:S(2)}) %all-to-all-start) | async-done | bytes 2097184 | tf_op jit(solution)/shard_map/all_to_all | solution.py:42
  231.2 1.6 copy.50
  232.8 2.3 gather_fusion.1
  235.1 2.7 %fusion.1 = f32[2,32,7168]{2,1,0:T(8,128)S(1)} fusion(bf16[2,32,7168]{2,1,0:T(8,128)(2,1)} %collective-permute-done.3, bf16[2,32,7168]{2,1,0:T(8,128)(2,1)} %collective-permute-done.2, bf16[2,32,7168]{2,1,0:T(8,128)(2,1)} %collective-permute-done.1, f32[4,2,32,7168]{3,2,1,0:T(8,128)} %copy-done.1, s32[]{:T(128)S(6)} %select_n.118), kind=kLoop, calls=%fused_computation.10 | loop fusion | flops 2752512 | bytes 6422532 | tf_op jit(solution)/shard_map/add | solution.py:165
  237.8 0.1 fusion.6
  237.9 0.1 collective-permute-start.4
  238.0 0.3 select_bitcast_fusion
  238.2 0.1 slice_bitcast_fusion
  238.4 1.1 copy.51
  239.5 1.1 copy.52
  240.5 9.4 %collective-permute-done.4 = bf16[32,7168]{1,0:T(8,128)(2,1)S(1)} collective-permute-done((bf16[32,7168]{1,0:T(8,128)(2,1)S(1)}, bf16[32,7168]{1,0:T(8,128)(2,1)S(1)}, u32[]{:S(2)}, u32[]{:S(2)}) %collective-permute-start.4) | collective-permute-done | bytes 458784 | tf_op jit(solution)/shard_map/ppermute | solution.py:165
  249.9 0.8 fusion.5
  (21 shorter events, 0.1 us)
Async XLA Ops:
  7.2 4.7 %copy-start.3 = (bf16[4,512,256]{2,1,0:T(8,128)(2,1)S(1)}, bf16[4,512,256]{2,1,0:T(8,128)(2,1)}, u32[]{:S(2)}) copy-start(bf16[4,512,256]{2,1,0:T(8,128)(2,1)} %param.17) | copy-start | bytes 3145732
  7.2 4.7 %copy-start.2 = (bf16[4,512,256]{2,1,0:T(8,128)(2,1)S(1)}, bf16[4,512,256]{2,1,0:T(8,128)(2,1)}, u32[]{:S(2)}) copy-start(bf16[4,512,256]{2,1,0:T(8,128)(2,1)} %param.18) | copy-start | bytes 3145732
  7.2 109.8 %all-gather.3.cloned.1.call-start = ((), (), s32[]{:S(2)}) async-start(), calls=%async_computation.1 | async-start | bytes 8912896 | tf_op jit(solution)/shard_map/all_gather | solution.py:134
  130.2 4.1 %copy-start = (bf16[512,7168]{1,0:T(8,128)(2,1)}, bf16[512,7168]{1,0:T(8,128)(2,1)S(1)}, u32[]{:S(2)}) copy-start(bf16[512,7168]{1,0:T(8,128)(2,1)S(1)} %convolution_convert_fusion) | copy-start | bytes 22020100
  134.3 43.9 %collective-permute-start = (bf16[4,2,32,7168]{3,2,1,0:T(8,128)(2,1)}, bf16[4,2,32,7168]{3,2,1,0:T(8,128)(2,1)}, u32[]{:S(2)}, u32[]{:S(2)}) collective-permute-start(bf16[4,2,32,7168]{3,2,1,0:T(8,128)(2,1)} %dynamic-slice_bitcast_fusion), channel_id=1, source_target_pairs={{0,1},{1,0},{2,3},{3,2},{4,5},{5,4},{6,7},{7,6},{8,9},{9,8},{10,11... | collective-permute-start | bytes 11010056 | tf_op jit(solution)/shard_map/ppermute | solution.py:165
  135.9 95.3 %all-to-all-start = ((bf16[16,2,4,2,16,256]{5,4,3,2,1,0:T(8,128)(2,1)}), bf16[16,2,4,2,16,256]{5,4,3,2,1,0:T(8,128)(2,1)S(1)}, u32[]{:S(2)}, u32[]{:S(2)}) async-start(bf16[16,2,4,2,16,256]{5,4,3,2,1,0:T(8,128)(2,1)} %copy.49), calls=%async_computation | async-start | bytes 4194304 | tf_op jit(solution)/shard_map/all_to_all | solution.py:42
  182.6 3.0 %copy-start.1 = (f32[4,2,32,7168]{3,2,1,0:T(8,128)}, f32[4,2,32,7168]{3,2,1,0:T(8,128)S(1)}, u32[]{:S(2)}) copy-start(f32[4,2,32,7168]{3,2,1,0:T(8,128)S(1)} %convert_add_fusion) | copy-start | bytes 22020100
  187.1 47.9 %collective-permute-start.1 = (bf16[2,32,7168]{2,1,0:T(8,128)(2,1)}, bf16[2,32,7168]{2,1,0:T(8,128)(2,1)}, u32[]{:S(2)}, u32[]{:S(2)}) collective-permute-start(bf16[2,32,7168]{2,1,0:T(8,128)(2,1)} %get-tuple-element.35), channel_id=1, source_target_pairs={{0,4},{4,8},{8,12},{12,0},{1,5},{5,9},{9,13},{13,1},{2,6},{6,10},{... | collective-permute-start | bytes 2752520 | tf_op jit(solution)/shard_map/ppermute | solution.py:165
  188.6 46.4 %collective-permute-start.2 = (bf16[2,32,7168]{2,1,0:T(8,128)(2,1)}, bf16[2,32,7168]{2,1,0:T(8,128)(2,1)}, u32[]{:S(2)}, u32[]{:S(2)}) collective-permute-start(bf16[2,32,7168]{2,1,0:T(8,128)(2,1)} %get-tuple-element.37), channel_id=1, source_target_pairs={{0,8},{4,12},{8,0},{12,4},{1,9},{5,13},{9,1},{13,5},{2,10},{6,14},... | collective-permute-start | bytes 2752520 | tf_op jit(solution)/shard_map/ppermute | solution.py:165
  191.3 43.8 %collective-permute-start.3 = (bf16[2,32,7168]{2,1,0:T(8,128)(2,1)S(1)}, bf16[2,32,7168]{2,1,0:T(8,128)(2,1)}, u32[]{:S(2)}, u32[]{:S(2)}) collective-permute-start(bf16[2,32,7168]{2,1,0:T(8,128)(2,1)S(1)} %get-tuple-element.36), channel_id=1, source_target_pairs={{0,12},{4,0},{8,4},{12,8},{1,13},{5,1},{9,5},{13,9},{2,14},{6,2},{... | collective-permute-start | bytes 2752520 | tf_op jit(solution)/shard_map/ppermute | solution.py:165
  237.9 12.0 %collective-permute-start.4 = (bf16[32,7168]{1,0:T(8,128)(2,1)S(1)}, bf16[32,7168]{1,0:T(8,128)(2,1)S(1)}, u32[]{:S(2)}, u32[]{:S(2)}) collective-permute-start(bf16[32,7168]{1,0:T(8,128)(2,1)S(1)} %fusion.6), channel_id=1, source_target_pairs={{0,2},{2,0},{1,3},{3,1},{4,6},{6,4},{5,7},{7,5},{8,10},{10,8},{9,1... | collective-permute-start | bytes 1376264 | tf_op jit(solution)/shard_map/ppermute | solution.py:165
Sparse Core Ops, SparseCore 0:
  11.0 105.9 all-gather.2

commit v7 on v6

--- a/solution.py
+++ b/solution.py
@@ -35,11 +35,10 @@
     slot_of = (jnp.sum(jnp.where(hit[:, :, None], table, 0), axis=1) % page_count).reshape(-1)
     arrivals = jnp.arange(page_count, dtype=jnp.int32)
     inverse = jnp.sum(jnp.where(slot_of[None, :] == arrivals[:, None], arrivals[None, :], 0), axis=1)
-    return (outgoing, inverse)
-
-
-def place_pages(outgoing, inverse):
-    moved = lax.all_to_all(outgoing, SEQ, split_axis=0, concat_axis=0, tiled=True)
+    return (lax.all_to_all(outgoing, SEQ, split_axis=0, concat_axis=0, tiled=True), inverse)
+
+
+def place_pages(moved, inverse):
     _, kinds, layers, per_group, page_len, feat_width = moved.shape
     moved = moved.transpose(1, 2, 0, 3, 4, 5).reshape(kinds, layers, -1, page_len, feat_width)
     placed = jnp.take(moved, inverse, axis=2)

time: 258 us -> 282 us (1.093)
  the two profiles are of different devices: /device:TPU:8 before, /device:TPU:214 now
where the time goes in v7:
time: 282 us; the launch traced here: 278 us
  waiting for transfers between devices  180 us (64%)
  Pallas kernels  28.1 us (10%)
  local copies, waits for them, and re-layouts  22.2 us (8%)
  other arithmetic  16.8 us (6%)
  between operations  14.2 us (5%)
  starting transfers between devices  12.8 us (5%)
  matrix products  4.13 us (1%)
    all_gather x1, waiting for transfers between devices, attention(): kv_all = lax.all_gather(kv, SEQ, axis=0, tiled=False)  68.1 us
    all_to_all x1, waiting for transfers between devices, relayout(): lax.all_to_all(outgoing, SEQ, split_axis=0, concat_axis=0, tiled=True)  59 us
    ppermute x5, waiting for transfers between devices, exchange(): total = total + lax.ppermute(sent, name, pairs).astype(jnp.float32)  53.1 us
    pallas_call x1, Pallas kernels, attend(): pl.pallas_call(kernel, grid_spec=pltpu.PrefetchScalarGridSpec(num_scalar_...  28.1 us
    all_to_all x1, starting transfers between devices, relayout(): lax.all_to_all(outgoing, SEQ, split_axis=0, concat_axis=0, tiled=True)  8.85 us
    add x2, other arithmetic, exchange(): total = total + lax.ppermute(sent, name, pairs).astype(jnp.float32)  7.08 us
    unnamed x10, local copies, waits for them, and re-layouts  6.77 us
  transfers between devices with their start and end apart: 7, of which 7 were waited for; matrix products, arithmetic and copies ran while one was open for 7% of the time, Pallas kernels for 0%

profile of v7, /device:TPU:214, one launch (start us, length us, event | category | flops | bytes accessed | tf_op | source)
XLA Modules:
  0.0 278.4 jit_solution(9163834692001582403)
XLA Ops:
  7.2 2.0 pad_maximum_fusion.1
  9.2 0.8 reshape.114
  10.0 0.1 copy.45
  10.1 0.1 select_reduce_fusion.2
  10.3 0.1 iota_add_fusion
  10.3 0.1 add.130
  10.4 0.4 fusion.10
  10.8 0.1 select_reduce_fusion
  10.9 0.1 reduce_sum.31
  11.0 0.1 select_reduce_fusion.1
  11.2 2.8 %pad_maximum_fusion = bf16[2,4,32,16,256]{4,3,2,1,0:T(8,128)(2,1)} fusion(bf16[1,4,32,16,256]{4,3,2,1,0:T(8,128)(2,1)S(1)} %bitcast.78, bf16[1,4,32,16,256]{4,3,2,1,0:T(8,128)(2,1)} %bitcast.79), kind=kLoop, calls=%fused_computation.5 | loop fusion | flops 1048576 | bytes 4194304 | tf_op jit(solution)/shard_map/stack | solution.py:31
  14.0 2.3 gather_fusion
  16.3 0.3 broadcast_select_fusion
  16.5 1.6 copy.47
  18.2 8.9 %all-to-all-start = ((bf16[16,2,4,2,16,256]{5,4,3,2,1,0:T(8,128)(2,1)}), bf16[16,2,4,2,16,256]{5,4,3,2,1,0:T(8,128)(2,1)S(1)}, u32[]{:S(2)}, u32[]{:S(2)}) async-start(bf16[16,2,4,2,16,256]{5,4,3,2,1,0:T(8,128)(2,1)} %copy.47), calls=%async_computation | async-start | bytes 4194304 | tf_op jit(solution)/shard_map/all_to_all | solution.py:38
  27.1 0.9 copy.48.qseg_ref
  27.9 0.6 fusion.16
  28.5 1.4 fusion.11
  30.0 0.7 and_select_fusion.2
  30.7 0.6 pad_add_fusion.meta_ref
  31.2 59.0 %all-to-all-done = bf16[16,2,4,2,16,256]{5,4,3,2,1,0:T(8,128)(2,1)S(1)} async-done(((bf16[16,2,4,2,16,256]{5,4,3,2,1,0:T(8,128)(2,1)}), bf16[16,2,4,2,16,256]{5,4,3,2,1,0:T(8,128)(2,1)S(1)}, u32[]{:S(2)}, u32[]{:S(2)}) %all-to-all-start) | async-done | bytes 2097184 | tf_op jit(solution)/shard_map/all_to_all | solution.py:38
  90.3 68.1 %all-gather.3.cloned.1.call-done = bf16[32,512,256]{2,1,0:T(8,128)(2,1)} async-done(((bf16[2,512,256]{2,1,0:T(8,128)(2,1)}), bf16[32,512,256]{2,1,0:T(8,128)(2,1)}) %all-gather.3.cloned.1.call-update) | async-done | bytes 8388624 | tf_op jit(solution)/shard_map/all_gather | solution.py:133
  158.4 28.1 %shard_map.120 = bf16[512,256]{1,0:T(8,128)(2,1)} custom-call(s32[17]{0:T(128)} %pad_add_fusion.meta_ref, bf16[512,256]{1,0:T(8,128)(2,1)} %q_ref.1, s32[512,1]{1,0:T(8,128)} %copy.48.qseg_ref, s32[16,1,512]{2,1,0:T(1,128)} %bitcast.82, bf16[16,2,512,256]{3,2,1,0:T(8,128)(2,1)} %bitcast.69, bf16[16,2,512,256]{3,2,1,0:T(8,128)(2,1)} %bitcast.70), custom_call_target="tpu_custom_call" | custom-call | tf_op jit(solution)/shard_map/pallas_call | solution.py:99
  186.5 1.0 copy.49
  187.5 4.1 %convolution_convert_fusion = bf16[512,7168]{1,0:T(8,128)(2,1)S(1)} fusion(bf16[512,256]{1,0:T(8,128)(2,1)S(1)} %bitcast.77, bf16[256,7168]{1,0:T(8,128)(2,1)} %param.16), kind=kOutput, calls=%fused_computation.2 | convolution fusion | flops 1882718208 | bytes 11272192 | tf_op jit(solution)/shard_map/dot_general | solution.py:173
  191.6 2.4 dynamic-slice_bitcast_fusion
  194.0 1.7 copy-done
  195.6 0.1 collective-permute-start
  195.7 6.7 %collective-permute-done = bf16[4,2,32,7168]{3,2,1,0:T(8,128)(2,1)} collective-permute-done((bf16[4,2,32,7168]{3,2,1,0:T(8,128)(2,1)}, bf16[4,2,32,7168]{3,2,1,0:T(8,128)(2,1)}, u32[]{:S(2)}, u32[]{:S(2)}) %collective-permute-start) | collective-permute-done | bytes 3670048 | tf_op jit(solution)/shard_map/ppermute | solution.py:164
  202.4 4.4 %convert_add_fusion = f32[4,2,32,7168]{3,2,1,0:T(8,128)S(1)} fusion(bf16[4,2,32,7168]{3,2,1,0:T(8,128)(2,1)} %collective-permute-done, bf16[2,4,2,32,7168]{4,3,2,1,0:T(8,128)(2,1)} %bitcast.72, s32[]{:T(128)S(6)} %select_n.115), kind=kLoop, calls=%fused_computation.3 | loop fusion | flops 5505024 | bytes 14680068 | tf_op jit(solution)/shard_map/add | solution.py:164
  206.8 2.9 %copy-done.1 = f32[4,2,32,7168]{3,2,1,0:T(8,128)} copy-done((f32[4,2,32,7168]{3,2,1,0:T(8,128)}, f32[4,2,32,7168]{3,2,1,0:T(8,128)S(1)}, u32[]{:S(2)}) %copy-start.1) | copy-done | bytes 7340056
  209.7 1.6 fusion.2
  211.3 0.5 collective-permute-start.1
  211.9 2.4 collective-permute-start.2
  214.3 1.6 copy.50
  215.9 2.3 gather_fusion.1
  218.2 16.6 %collective-permute-done.1 = bf16[2,32,7168]{2,1,0:T(8,128)(2,1)} collective-permute-done((bf16[2,32,7168]{2,1,0:T(8,128)(2,1)}, bf16[2,32,7168]{2,1,0:T(8,128)(2,1)}, u32[]{:S(2)}, u32[]{:S(2)}) %collective-permute-start.1) | collective-permute-done | bytes 917536 | tf_op jit(solution)/shard_map/ppermute | solution.py:164
  234.8 2.1 collective-permute-done.2
  237.0 18.5 %collective-permute-done.3 = bf16[2,32,7168]{2,1,0:T(8,128)(2,1)} collective-permute-done((bf16[2,32,7168]{2,1,0:T(8,128)(2,1)S(1)}, bf16[2,32,7168]{2,1,0:T(8,128)(2,1)}, u32[]{:S(2)}, u32[]{:S(2)}) %collective-permute-start.3) | collective-permute-done | bytes 917536 | tf_op jit(solution)/shard_map/ppermute | solution.py:164
  255.5 2.7 fusion.1
  258.2 0.1 fusion.6
  258.2 0.9 collective-permute-start.4
  259.1 0.3 select_bitcast_fusion
  259.4 0.1 slice_bitcast_fusion
  259.5 1.1 copy.51
  260.6 1.1 copy.52
  261.7 9.1 %collective-permute-done.4 = bf16[32,7168]{1,0:T(8,128)(2,1)S(1)} collective-permute-done((bf16[32,7168]{1,0:T(8,128)(2,1)S(1)}, bf16[32,7168]{1,0:T(8,128)(2,1)S(1)}, u32[]{:S(2)}, u32[]{:S(2)}) %collective-permute-start.4) | collective-permute-done | bytes 458784 | tf_op jit(solution)/shard_map/ppermute | solution.py:164
  270.8 0.8 fusion.5
  (19 shorter events, 0.2 us)
Async XLA Ops:
  7.2 4.0 %copy-start.2 = (bf16[4,512,256]{2,1,0:T(8,128)(2,1)S(1)}, bf16[4,512,256]{2,1,0:T(8,128)(2,1)}, u32[]{:S(2)}) copy-start(bf16[4,512,256]{2,1,0:T(8,128)(2,1)} %param.18) | copy-start | bytes 3145732
  7.2 151.2 %all-gather.3.cloned.1.call-start = ((), (), s32[]{:S(2)}) async-start(), calls=%async_computation.1 | async-start | bytes 8912896 | tf_op jit(solution)/shard_map/all_gather | solution.py:133
  18.2 8.9 %copy-start.3 = (s32[8192]{0:T(1024)S(1)}, s32[8192]{0:T(1024)}, u32[]{:S(2)}) copy-start(s32[8192]{0:T(1024)} %param.14) | copy-start | bytes 98308
  18.2 72.1 %all-to-all-start = ((bf16[16,2,4,2,16,256]{5,4,3,2,1,0:T(8,128)(2,1)}), bf16[16,2,4,2,16,256]{5,4,3,2,1,0:T(8,128)(2,1)S(1)}, u32[]{:S(2)}, u32[]{:S(2)}) async-start(bf16[16,2,4,2,16,256]{5,4,3,2,1,0:T(8,128)(2,1)} %copy.47), calls=%async_computation | async-start | bytes 4194304 | tf_op jit(solution)/shard_map/all_to_all | solution.py:38
  191.6 4.1 %copy-start = (bf16[512,7168]{1,0:T(8,128)(2,1)}, bf16[512,7168]{1,0:T(8,128)(2,1)S(1)}, u32[]{:S(2)}) copy-start(bf16[512,7168]{1,0:T(8,128)(2,1)S(1)} %convolution_convert_fusion) | copy-start | bytes 22020100
  195.6 6.8 %collective-permute-start = (bf16[4,2,32,7168]{3,2,1,0:T(8,128)(2,1)}, bf16[4,2,32,7168]{3,2,1,0:T(8,128)(2,1)}, u32[]{:S(2)}, u32[]{:S(2)}) collective-permute-start(bf16[4,2,32,7168]{3,2,1,0:T(8,128)(2,1)} %dynamic-slice_bitcast_fusion), channel_id=1, source_target_pairs={{0,1},{1,0},{2,3},{3,2},{4,5},{5,4},{6,7},{7,6},{8,9},{9,8},{10,11... | collective-permute-start | bytes 11010056 | tf_op jit(solution)/shard_map/ppermute | solution.py:164
  206.8 3.0 %copy-start.1 = (f32[4,2,32,7168]{3,2,1,0:T(8,128)}, f32[4,2,32,7168]{3,2,1,0:T(8,128)S(1)}, u32[]{:S(2)}) copy-start(f32[4,2,32,7168]{3,2,1,0:T(8,128)S(1)} %convert_add_fusion) | copy-start | bytes 22020100
  211.3 23.5 %collective-permute-start.1 = (bf16[2,32,7168]{2,1,0:T(8,128)(2,1)}, bf16[2,32,7168]{2,1,0:T(8,128)(2,1)}, u32[]{:S(2)}, u32[]{:S(2)}) collective-permute-start(bf16[2,32,7168]{2,1,0:T(8,128)(2,1)} %get-tuple-element.35), channel_id=1, source_target_pairs={{0,4},{4,8},{8,12},{12,0},{1,5},{5,9},{9,13},{13,1},{2,6},{6,10},{... | collective-permute-start | bytes 2752520 | tf_op jit(solution)/shard_map/ppermute | solution.py:164
  211.9 25.1 %collective-permute-start.2 = (bf16[2,32,7168]{2,1,0:T(8,128)(2,1)}, bf16[2,32,7168]{2,1,0:T(8,128)(2,1)}, u32[]{:S(2)}, u32[]{:S(2)}) collective-permute-start(bf16[2,32,7168]{2,1,0:T(8,128)(2,1)} %get-tuple-element.37), channel_id=1, source_target_pairs={{0,8},{4,12},{8,0},{12,4},{1,9},{5,13},{9,1},{13,5},{2,10},{6,14},... | collective-permute-start | bytes 2752520 | tf_op jit(solution)/shard_map/ppermute | solution.py:164
  214.3 41.2 %collective-permute-start.3 = (bf16[2,32,7168]{2,1,0:T(8,128)(2,1)S(1)}, bf16[2,32,7168]{2,1,0:T(8,128)(2,1)}, u32[]{:S(2)}, u32[]{:S(2)}) collective-permute-start(bf16[2,32,7168]{2,1,0:T(8,128)(2,1)S(1)} %get-tuple-element.36), channel_id=1, source_target_pairs={{0,12},{4,0},{8,4},{12,8},{1,13},{5,1},{9,5},{13,9},{2,14},{6,2},{... | collective-permute-start | bytes 2752520 | tf_op jit(solution)/shard_map/ppermute | solution.py:164
  258.2 12.5 %collective-permute-start.4 = (bf16[32,7168]{1,0:T(8,128)(2,1)S(1)}, bf16[32,7168]{1,0:T(8,128)(2,1)S(1)}, u32[]{:S(2)}, u32[]{:S(2)}) collective-permute-start(bf16[32,7168]{1,0:T(8,128)(2,1)S(1)} %fusion.6), channel_id=1, source_target_pairs={{0,2},{2,0},{1,3},{3,1},{4,6},{6,4},{5,7},{7,5},{8,10},{10,8},{9,1... | collective-permute-start | bytes 1376264 | tf_op jit(solution)/shard_map/ppermute | solution.py:164
Sparse Core Ops, SparseCore 0:
  11.0 147.3 all-gather.2

commit v8 on v6

--- a/solution.py
+++ b/solution.py
@@ -32,16 +32,25 @@
     outgoing = jnp.take(both, send_pages, axis=2).reshape(2, layers, groups, per_group, page_len, feat_width)
     outgoing = outgoing.transpose(2, 0, 1, 3, 4, 5)
     hit = (table[:, :, 0] // page_count) == position
-    slot_of = (jnp.sum(jnp.where(hit[:, :, None], table, 0), axis=1) % page_count).reshape(-1)
+    slot_by_source = jnp.sum(jnp.where(hit[:, :, None], table, 0), axis=1) % page_count
+    sources = (position - run_ids) % groups
+    slot_of = jnp.take(slot_by_source, sources, axis=0).reshape(-1)
     arrivals = jnp.arange(page_count, dtype=jnp.int32)
     inverse = jnp.sum(jnp.where(slot_of[None, :] == arrivals[:, None], arrivals[None, :], 0), axis=1)
     return (outgoing, inverse)
 
 
 def place_pages(outgoing, inverse):
-    moved = lax.all_to_all(outgoing, SEQ, split_axis=0, concat_axis=0, tiled=True)
-    _, kinds, layers, per_group, page_len, feat_width = moved.shape
-    moved = moved.transpose(1, 2, 0, 3, 4, 5).reshape(kinds, layers, -1, page_len, feat_width)
+    groups = outgoing.shape[0]
+    position = lax.axis_index(SEQ)
+    arrived = [lax.dynamic_index_in_dim(outgoing, position, 0, keepdims=False)]
+    for shift in range(1, groups):
+        sent = lax.dynamic_index_in_dim(outgoing, (position + shift) % groups, 0, keepdims=False)
+        pairs = [(i, (i + shift) % groups) for i in range(groups)]
+        arrived.append(lax.ppermute(sent, SEQ, pairs))
+    moved = jnp.stack(arrived, axis=2)
+    kinds, layers, _, per_group, page_len, feat_width = moved.shape
+    moved = moved.reshape(kinds, layers, -1, page_len, feat_width)
     placed = jnp.take(moved, inverse, axis=2)
     return (placed[0], placed[1])
 

time: 258 us -> 324 us (1.26); the launches traced: 258 us -> 320 us
  starting transfers between devices: 48.2 us -> 108 us
  local copies, waits for them, and re-layouts: 23.1 us -> 32.9 us
  waiting for transfers between devices: 144 us -> 135 us
    ppermute x0 -> x15, starting transfers between devices: none -> 75.6 us  [place_pages(): arrived.append(lax.ppermute(sent, SEQ, pairs))]
    all_to_all x1 -> x0, starting transfers between devices: 42.3 us -> none  [place_pages(): lax.all_to_all(outgoing, SEQ, split_axis=0, concat_axis=0, tiled=True)]
    all_to_all x1 -> x0, waiting for transfers between devices: 38.2 us -> none  [place_pages(): lax.all_to_all(outgoing, SEQ, split_axis=0, concat_axis=0, tiled=True)]
    ppermute x5, starting transfers between devices: 5.8 us -> 32.6 us  [exchange(): total = total + lax.ppermute(sent, name, pairs).astype(jnp.float32)]
    ppermute x5, waiting for transfers between devices: 9.39 us -> 32.9 us  [exchange(): total = total + lax.ppermute(sent, name, pairs).astype(jnp.float32)]
    unnamed x10 -> x27, local copies, waits for them, and re-layouts: 6.78 us -> 18.2 us
    ppermute x0 -> x15, waiting for transfers between devices: none -> 6.05 us  [place_pages(): arrived.append(lax.ppermute(sent, SEQ, pairs))]
  transfers between devices with their start and end apart: 7 -> 21, of which waited for: 3 -> 7; matrix products, arithmetic and copies ran while one was open for 10% -> 11% of each run, Pallas kernels for 0% -> 0%
where the time goes in v8:
time: 324 us; the launch traced here: 320 us
  waiting for transfers between devices  135 us (42%)
  starting transfers between devices  108 us (33%)
  local copies, waits for them, and re-layouts  32.9 us (10%)
  other arithmetic  15.6 us (5%)
  between operations  14.3 us (4%)
  Pallas kernels  9.76 us (3%)
  matrix products  4.13 us (1%)
    all_gather x1, waiting for transfers between devices, attention(): kv_all = lax.all_gather(kv, SEQ, axis=0, tiled=False)  96 us
    ppermute x15, starting transfers between devices, place_pages(): arrived.append(lax.ppermute(sent, SEQ, pairs))  75.6 us
    ppermute x5, waiting for transfers between devices, exchange(): total = total + lax.ppermute(sent, name, pairs).astype(jnp.float32)  32.9 us
    ppermute x5, starting transfers between devices, exchange(): total = total + lax.ppermute(sent, name, pairs).astype(jnp.float32)  32.6 us
    unnamed x27, local copies, waits for them, and re-layouts  18.2 us
    pallas_call x1, Pallas kernels, attend(): pl.pallas_call(kernel, grid_spec=pltpu.PrefetchScalarGridSpec(num_scalar_...  9.76 us
    add x2, other arithmetic, exchange(): total = total + lax.ppermute(sent, name, pairs).astype(jnp.float32)  7.08 us
  transfers between devices with their start and end apart: 21, of which 7 were waited for; matrix products, arithmetic and copies ran while one was open for 11% of the time, Pallas kernels for 0%

profile of v8, /device:TPU:8, one launch (start us, length us, event | category | flops | bytes accessed | tf_op | source)
XLA Modules:
  0.0 320.0 jit_solution(14709566002232071881)
XLA Ops:
  7.2 2.0 pad_maximum_fusion.1
  9.3 0.8 reshape.161
  11.9 1.6 pad_maximum_fusion
  13.4 2.3 gather_fusion.1
  16.9 0.9 copy.32.qseg_ref
  18.3 1.4 fusion.12
  19.7 0.7 and_select_fusion.3
  21.0 96.0 %all-gather.3.cloned.1.call-done = bf16[32,512,256]{2,1,0:T(8,128)(2,1)} async-done(((bf16[2,512,256]{2,1,0:T(8,128)(2,1)}), bf16[32,512,256]{2,1,0:T(8,128)(2,1)}) %all-gather.3.cloned.1.call-update) | async-done | bytes 8388624 | tf_op jit(solution)/shard_map/all_gather | solution.py:143
  117.0 9.8 %shard_map.120 = bf16[512,256]{1,0:T(8,128)(2,1)} custom-call(s32[17]{0:T(128)} %pad_add_fusion.meta_ref, bf16[512,256]{1,0:T(8,128)(2,1)} %q_ref.1, s32[512,1]{1,0:T(8,128)} %copy.32.qseg_ref, s32[16,1,512]{2,1,0:T(1,128)} %bitcast.146, bf16[16,2,512,256]{3,2,1,0:T(8,128)(2,1)} %bitcast.133, bf16[16,2,512,256]{3,2,1,0:T(8,128)(2,1)} %bitcast.134), custom_call_target="tpu_custom_call" | custom-call | tf_op jit(solution)/shard_map/pallas_call | solution.py:109
  126.8 1.0 copy.33
  127.7 4.1 %convolution_convert_fusion = bf16[512,7168]{1,0:T(8,128)(2,1)S(1)} fusion(bf16[512,256]{1,0:T(8,128)(2,1)S(1)} %bitcast.141, bf16[256,7168]{1,0:T(8,128)(2,1)} %param.16), kind=kOutput, calls=%fused_computation.3 | convolution fusion | flops 1882718208 | bytes 11272192 | tf_op jit(solution)/shard_map/dot_general | solution.py:183
  131.9 2.4 dynamic-slice_bitcast_fusion
  134.3 1.6 copy-done
  135.9 0.9 dynamic-slice_bitcast_fusion.1
  136.9 5.7 %collective-permute-start.5 = (bf16[2,4,2,16,256]{4,3,2,1,0:T(8,128)(2,1)}, bf16[2,4,2,16,256]{4,3,2,1,0:T(8,128)(2,1)}, u32[]{:S(2)}, u32[]{:S(2)}) collective-permute-start(bf16[2,4,2,16,256]{4,3,2,1,0:T(8,128)(2,1)} %get-tuple-element.46), channel_id=1, source_target_pairs={{0,16},{16,32},{32,48},{48,64},{64,80},{80,96},{96,112},{112,128},... | collective-permute-start | bytes 393224 | tf_op jit(solution)/shard_map/ppermute | solution.py:50
  142.6 11.2 %collective-permute-start.6 = (bf16[2,4,2,16,256]{4,3,2,1,0:T(8,128)(2,1)}, bf16[2,4,2,16,256]{4,3,2,1,0:T(8,128)(2,1)S(1)}, u32[]{:S(2)}, u32[]{:S(2)}) collective-permute-start(bf16[2,4,2,16,256]{4,3,2,1,0:T(8,128)(2,1)} %get-tuple-element.45), channel_id=1, source_target_pairs={{0,32},{16,48},{32,64},{48,80},{64,96},{80,112},{96,128},{112,144}... | collective-permute-start | bytes 393224 | tf_op jit(solution)/shard_map/ppermute | solution.py:50
  153.8 8.5 %collective-permute-start.7 = (bf16[2,4,2,16,256]{4,3,2,1,0:T(8,128)(2,1)}, bf16[2,4,2,16,256]{4,3,2,1,0:T(8,128)(2,1)S(1)}, u32[]{:S(2)}, u32[]{:S(2)}) collective-permute-start(bf16[2,4,2,16,256]{4,3,2,1,0:T(8,128)(2,1)} %get-tuple-element.44), channel_id=1, source_target_pairs={{0,48},{16,64},{32,80},{48,96},{64,112},{80,128},{96,144},{112,160... | collective-permute-start | bytes 393224 | tf_op jit(solution)/shard_map/ppermute | solution.py:50
  162.3 6.7 %collective-permute-start.8 = (bf16[2,4,2,16,256]{4,3,2,1,0:T(8,128)(2,1)}, bf16[2,4,2,16,256]{4,3,2,1,0:T(8,128)(2,1)S(1)}, u32[]{:S(2)}, u32[]{:S(2)}) collective-permute-start(bf16[2,4,2,16,256]{4,3,2,1,0:T(8,128)(2,1)} %get-tuple-element.43), channel_id=1, source_target_pairs={{0,64},{16,80},{32,96},{48,112},{64,128},{80,144},{96,160},{112,17... | collective-permute-start | bytes 393224 | tf_op jit(solution)/shard_map/ppermute | solution.py:50
  169.0 0.7 bitcast_dynamic-update-slice_fusion.15
  169.7 9.3 %collective-permute-start.9 = (bf16[2,4,2,16,256]{4,3,2,1,0:T(8,128)(2,1)S(1)}, bf16[2,4,2,16,256]{4,3,2,1,0:T(8,128)(2,1)S(1)}, u32[]{:S(2)}, u32[]{:S(2)}) collective-permute-start(bf16[2,4,2,16,256]{4,3,2,1,0:T(8,128)(2,1)S(1)} %get-tuple-element.42), channel_id=1, source_target_pairs={{0,80},{16,96},{32,112},{48,128},{64,144},{80,160},{96,176},{112,1... | collective-permute-start | bytes 393224 | tf_op jit(solution)/shard_map/ppermute | solution.py:50
  179.0 1.6 bitcast_dynamic-update-slice_fusion.14
  180.6 4.6 %collective-permute-done.6 = bf16[2,4,2,16,256]{4,3,2,1,0:T(8,128)(2,1)S(1)} collective-permute-done((bf16[2,4,2,16,256]{4,3,2,1,0:T(8,128)(2,1)}, bf16[2,4,2,16,256]{4,3,2,1,0:T(8,128)(2,1)S(1)}, u32[]{:S(2)}, u32[]{:S(2)}) %collective-permute-start.6) | collective-permute-done | bytes 131104 | tf_op jit(solution)/shard_map/ppermute | solution.py:50
  185.1 0.7 bitcast_dynamic-update-slice_fusion.13
  185.8 3.0 collective-permute-start.11
  190.8 6.1 %collective-permute-start.13 = (bf16[2,4,2,16,256]{4,3,2,1,0:T(8,128)(2,1)S(1)}, bf16[2,4,2,16,256]{4,3,2,1,0:T(8,128)(2,1)S(1)}, u32[]{:S(2)}, u32[]{:S(2)}) collective-permute-start(bf16[2,4,2,16,256]{4,3,2,1,0:T(8,128)(2,1)S(1)} %get-tuple-element.38), channel_id=1, source_target_pairs={{0,144},{16,160},{32,176},{48,192},{64,208},{80,224},{96,240},{112... | collective-permute-start | bytes 393224 | tf_op jit(solution)/shard_map/ppermute | solution.py:50
  197.8 14.0 %collective-permute-start.14 = (bf16[2,4,2,16,256]{4,3,2,1,0:T(8,128)(2,1)S(1)}, bf16[2,4,2,16,256]{4,3,2,1,0:T(8,128)(2,1)S(1)}, u32[]{:S(2)}, u32[]{:S(2)}) collective-permute-start(bf16[2,4,2,16,256]{4,3,2,1,0:T(8,128)(2,1)S(1)} %get-tuple-element.37), channel_id=1, source_target_pairs={{0,160},{16,176},{32,192},{48,208},{64,224},{80,240},{96,0},{112,1... | collective-permute-start | bytes 393224 | tf_op jit(solution)/shard_map/ppermute | solution.py:50
  213.2 3.7 %collective-permute-start.16 = (bf16[2,4,2,16,256]{4,3,2,1,0:T(8,128)(2,1)S(1)}, bf16[2,4,2,16,256]{4,3,2,1,0:T(8,128)(2,1)S(1)}, u32[]{:S(2)}, u32[]{:S(2)}) collective-permute-start(bf16[2,4,2,16,256]{4,3,2,1,0:T(8,128)(2,1)S(1)} %get-tuple-element.35), channel_id=1, source_target_pairs={{0,192},{16,208},{32,224},{48,240},{64,0},{80,16},{96,32},{112,48}... | collective-permute-start | bytes 393224 | tf_op jit(solution)/shard_map/ppermute | solution.py:50
  217.5 1.6 collective-permute-start.17
  219.7 2.3 collective-permute-start.18
  222.7 0.7 bitcast_dynamic-update-slice_fusion.4
  223.3 4.4 %convert_add_fusion = f32[4,2,32,7168]{3,2,1,0:T(8,128)S(1)} fusion(bf16[4,2,32,7168]{3,2,1,0:T(8,128)(2,1)} %collective-permute-done, bf16[2,4,2,32,7168]{4,3,2,1,0:T(8,128)(2,1)} %bitcast.136, s32[]{:T(128)S(6)} %select_n.261), kind=kLoop, calls=%fused_computation.4 | loop fusion | flops 5505024 | bytes 14680068 | tf_op jit(solution)/shard_map/add | solution.py:174
  227.7 2.9 copy-done.1
  230.7 1.6 fusion.2
  232.3 1.4 collective-permute-start.1
  233.7 6.4 %collective-permute-start.2 = (bf16[2,32,7168]{2,1,0:T(8,128)(2,1)}, bf16[2,32,7168]{2,1,0:T(8,128)(2,1)}, u32[]{:S(2)}, u32[]{:S(2)}) collective-permute-start(bf16[2,32,7168]{2,1,0:T(8,128)(2,1)} %get-tuple-element.29), channel_id=1, source_target_pairs={{0,8},{4,12},{8,0},{12,4},{1,9},{5,13},{9,1},{13,5},{2,10},{6,14},... | collective-permute-start | bytes 2752520 | tf_op jit(solution)/shard_map/ppermute | solution.py:174
  241.2 3.0 collective-permute-start.19
  244.9 0.7 bitcast_dynamic-update-slice_fusion.1
  245.6 1.2 collective-permute-done.19
  246.7 0.7 bitcast_dynamic-update-slice_fusion
  247.5 2.3 gather_fusion.2
  249.7 9.6 %collective-permute-done.1 = bf16[2,32,7168]{2,1,0:T(8,128)(2,1)} collective-permute-done((bf16[2,32,7168]{2,1,0:T(8,128)(2,1)}, bf16[2,32,7168]{2,1,0:T(8,128)(2,1)}, u32[]{:S(2)}, u32[]{:S(2)}) %collective-permute-start.1) | collective-permute-done | bytes 917536 | tf_op jit(solution)/shard_map/ppermute | solution.py:174
  259.3 17.4 %collective-permute-done.2 = bf16[2,32,7168]{2,1,0:T(8,128)(2,1)} collective-permute-done((bf16[2,32,7168]{2,1,0:T(8,128)(2,1)}, bf16[2,32,7168]{2,1,0:T(8,128)(2,1)}, u32[]{:S(2)}, u32[]{:S(2)}) %collective-permute-start.2) | collective-permute-done | bytes 917536 | tf_op jit(solution)/shard_map/ppermute | solution.py:174
  276.7 2.7 fusion.1
  279.5 24.3 %collective-permute-start.4 = (bf16[32,7168]{1,0:T(8,128)(2,1)S(1)}, bf16[32,7168]{1,0:T(8,128)(2,1)S(1)}, u32[]{:S(2)}, u32[]{:S(2)}) collective-permute-start(bf16[32,7168]{1,0:T(8,128)(2,1)S(1)} %fusion.6), channel_id=1, source_target_pairs={{0,2},{2,0},{1,3},{3,1},{4,6},{6,4},{5,7},{7,5},{8,10},{10,8},{9,1... | collective-permute-start | bytes 1376264 | tf_op jit(solution)/shard_map/ppermute | solution.py:174
  304.3 1.1 copy.34
  305.3 1.1 copy.35
  306.4 5.9 %collective-permute-done.4 = bf16[32,7168]{1,0:T(8,128)(2,1)S(1)} collective-permute-done((bf16[32,7168]{1,0:T(8,128)(2,1)S(1)}, bf16[32,7168]{1,0:T(8,128)(2,1)S(1)}, u32[]{:S(2)}, u32[]{:S(2)}) %collective-permute-start.4) | collective-permute-done | bytes 458784 | tf_op jit(solution)/shard_map/ppermute | solution.py:174
  312.3 0.8 fusion.5
  (71 shorter events, 12.5 us)
Async XLA Ops:
  7.2 4.7 %copy-start.3 = (bf16[4,512,256]{2,1,0:T(8,128)(2,1)S(1)}, bf16[4,512,256]{2,1,0:T(8,128)(2,1)}, u32[]{:S(2)}) copy-start(bf16[4,512,256]{2,1,0:T(8,128)(2,1)} %param.17) | copy-start | bytes 3145732
  7.2 4.7 %copy-start.2 = (bf16[4,512,256]{2,1,0:T(8,128)(2,1)S(1)}, bf16[4,512,256]{2,1,0:T(8,128)(2,1)}, u32[]{:S(2)}) copy-start(bf16[4,512,256]{2,1,0:T(8,128)(2,1)} %param.18) | copy-start | bytes 3145732
  7.2 109.8 %all-gather.3.cloned.1.call-start = ((), (), s32[]{:S(2)}) async-start(), calls=%async_computation | async-start | bytes 8912896 | tf_op jit(solution)/shard_map/all_gather | solution.py:143
  16.1 0.8 copy-start.4
  131.9 4.0 %copy-start = (bf16[512,7168]{1,0:T(8,128)(2,1)}, bf16[512,7168]{1,0:T(8,128)(2,1)S(1)}, u32[]{:S(2)}) copy-start(bf16[512,7168]{1,0:T(8,128)(2,1)S(1)} %convolution_convert_fusion) | copy-start | bytes 22020100
  135.9 87.4 %collective-permute-start = (bf16[4,2,32,7168]{3,2,1,0:T(8,128)(2,1)}, bf16[4,2,32,7168]{3,2,1,0:T(8,128)(2,1)}, u32[]{:S(2)}, u32[]{:S(2)}) collective-permute-start(bf16[4,2,32,7168]{3,2,1,0:T(8,128)(2,1)} %dynamic-slice_bitcast_fusion), channel_id=1, source_target_pairs={{0,1},{1,0},{2,3},{3,2},{4,5},{5,4},{6,7},{7,6},{8,9},{9,8},{10,11... | collective-permute-start | bytes 11010056 | tf_op jit(solution)/shard_map/ppermute | solution.py:174
  136.9 32.8 %collective-permute-start.5 = (bf16[2,4,2,16,256]{4,3,2,1,0:T(8,128)(2,1)}, bf16[2,4,2,16,256]{4,3,2,1,0:T(8,128)(2,1)}, u32[]{:S(2)}, u32[]{:S(2)}) collective-permute-start(bf16[2,4,2,16,256]{4,3,2,1,0:T(8,128)(2,1)} %get-tuple-element.46), channel_id=1, source_target_pairs={{0,16},{16,32},{32,48},{48,64},{64,80},{80,96},{96,112},{112,128},... | collective-permute-start | bytes 393224 | tf_op jit(solution)/shard_map/ppermute | solution.py:50
  142.6 42.5 %collective-permute-start.6 = (bf16[2,4,2,16,256]{4,3,2,1,0:T(8,128)(2,1)}, bf16[2,4,2,16,256]{4,3,2,1,0:T(8,128)(2,1)S(1)}, u32[]{:S(2)}, u32[]{:S(2)}) collective-permute-start(bf16[2,4,2,16,256]{4,3,2,1,0:T(8,128)(2,1)} %get-tuple-element.45), channel_id=1, source_target_pairs={{0,32},{16,48},{32,64},{48,80},{64,96},{80,112},{96,128},{112,144}... | collective-permute-start | bytes 393224 | tf_op jit(solution)/shard_map/ppermute | solution.py:50
  153.8 32.0 %collective-permute-start.7 = (bf16[2,4,2,16,256]{4,3,2,1,0:T(8,128)(2,1)}, bf16[2,4,2,16,256]{4,3,2,1,0:T(8,128)(2,1)S(1)}, u32[]{:S(2)}, u32[]{:S(2)}) collective-permute-start(bf16[2,4,2,16,256]{4,3,2,1,0:T(8,128)(2,1)} %get-tuple-element.44), channel_id=1, source_target_pairs={{0,48},{16,64},{32,80},{48,96},{64,112},{80,128},{96,144},{112,160... | collective-permute-start | bytes 393224 | tf_op jit(solution)/shard_map/ppermute | solution.py:50
  162.3 27.2 %collective-permute-start.8 = (bf16[2,4,2,16,256]{4,3,2,1,0:T(8,128)(2,1)}, bf16[2,4,2,16,256]{4,3,2,1,0:T(8,128)(2,1)S(1)}, u32[]{:S(2)}, u32[]{:S(2)}) collective-permute-start(bf16[2,4,2,16,256]{4,3,2,1,0:T(8,128)(2,1)} %get-tuple-element.43), channel_id=1, source_target_pairs={{0,64},{16,80},{32,96},{48,112},{64,128},{80,144},{96,160},{112,17... | collective-permute-start | bytes 393224 | tf_op jit(solution)/shard_map/ppermute | solution.py:50
  169.7 21.1 %collective-permute-start.9 = (bf16[2,4,2,16,256]{4,3,2,1,0:T(8,128)(2,1)S(1)}, bf16[2,4,2,16,256]{4,3,2,1,0:T(8,128)(2,1)S(1)}, u32[]{:S(2)}, u32[]{:S(2)}) collective-permute-start(bf16[2,4,2,16,256]{4,3,2,1,0:T(8,128)(2,1)S(1)} %get-tuple-element.42), channel_id=1, source_target_pairs={{0,80},{16,96},{32,112},{48,128},{64,144},{80,160},{96,176},{112,1... | collective-permute-start | bytes 393224 | tf_op jit(solution)/shard_map/ppermute | solution.py:50
  185.1 12.7 %collective-permute-start.10 = (bf16[2,4,2,16,256]{4,3,2,1,0:T(8,128)(2,1)S(1)}, bf16[2,4,2,16,256]{4,3,2,1,0:T(8,128)(2,1)S(1)}, u32[]{:S(2)}, u32[]{:S(2)}) collective-permute-start(bf16[2,4,2,16,256]{4,3,2,1,0:T(8,128)(2,1)S(1)} %get-tuple-element.41), channel_id=1, source_target_pairs={{0,96},{16,112},{32,128},{48,144},{64,160},{80,176},{96,192},{112,... | collective-permute-start | bytes 393224 | tf_op jit(solution)/shard_map/ppermute | solution.py:50
  185.8 26.7 %collective-permute-start.11 = (bf16[2,4,2,16,256]{4,3,2,1,0:T(8,128)(2,1)S(1)}, bf16[2,4,2,16,256]{4,3,2,1,0:T(8,128)(2,1)S(1)}, u32[]{:S(2)}, u32[]{:S(2)}) collective-permute-start(bf16[2,4,2,16,256]{4,3,2,1,0:T(8,128)(2,1)S(1)} %get-tuple-element.40), channel_id=1, source_target_pairs={{0,112},{16,128},{32,144},{48,160},{64,176},{80,192},{96,208},{112... | collective-permute-start | bytes 393224 | tf_op jit(solution)/shard_map/ppermute | solution.py:50
  189.5 23.7 %collective-permute-start.12 = (bf16[2,4,2,16,256]{4,3,2,1,0:T(8,128)(2,1)S(1)}, bf16[2,4,2,16,256]{4,3,2,1,0:T(8,128)(2,1)S(1)}, u32[]{:S(2)}, u32[]{:S(2)}) collective-permute-start(bf16[2,4,2,16,256]{4,3,2,1,0:T(8,128)(2,1)S(1)} %get-tuple-element.39), channel_id=1, source_target_pairs={{0,128},{16,144},{32,160},{48,176},{64,192},{80,208},{96,224},{112... | collective-permute-start | bytes 393224 | tf_op jit(solution)/shard_map/ppermute | solution.py:50
  190.8 26.7 %collective-permute-start.13 = (bf16[2,4,2,16,256]{4,3,2,1,0:T(8,128)(2,1)S(1)}, bf16[2,4,2,16,256]{4,3,2,1,0:T(8,128)(2,1)S(1)}, u32[]{:S(2)}, u32[]{:S(2)}) collective-permute-start(bf16[2,4,2,16,256]{4,3,2,1,0:T(8,128)(2,1)S(1)} %get-tuple-element.38), channel_id=1, source_target_pairs={{0,144},{16,160},{32,176},{48,192},{64,208},{80,224},{96,240},{112... | collective-permute-start | bytes 393224 | tf_op jit(solution)/shard_map/ppermute | solution.py:50
  197.8 21.9 %collective-permute-start.14 = (bf16[2,4,2,16,256]{4,3,2,1,0:T(8,128)(2,1)S(1)}, bf16[2,4,2,16,256]{4,3,2,1,0:T(8,128)(2,1)S(1)}, u32[]{:S(2)}, u32[]{:S(2)}) collective-permute-start(bf16[2,4,2,16,256]{4,3,2,1,0:T(8,128)(2,1)S(1)} %get-tuple-element.37), channel_id=1, source_target_pairs={{0,160},{16,176},{32,192},{48,208},{64,224},{80,240},{96,0},{112,1... | collective-permute-start | bytes 393224 | tf_op jit(solution)/shard_map/ppermute | solution.py:50
  212.5 10.2 %collective-permute-start.15 = (bf16[2,4,2,16,256]{4,3,2,1,0:T(8,128)(2,1)S(1)}, bf16[2,4,2,16,256]{4,3,2,1,0:T(8,128)(2,1)S(1)}, u32[]{:S(2)}, u32[]{:S(2)}) collective-permute-start(bf16[2,4,2,16,256]{4,3,2,1,0:T(8,128)(2,1)S(1)} %get-tuple-element.36), channel_id=1, source_target_pairs={{0,176},{16,192},{32,208},{48,224},{64,240},{80,0},{96,16},{112,32... | collective-permute-start | bytes 393224 | tf_op jit(solution)/shard_map/ppermute | solution.py:50
  213.2 26.9 %collective-permute-start.16 = (bf16[2,4,2,16,256]{4,3,2,1,0:T(8,128)(2,1)S(1)}, bf16[2,4,2,16,256]{4,3,2,1,0:T(8,128)(2,1)S(1)}, u32[]{:S(2)}, u32[]{:S(2)}) collective-permute-start(bf16[2,4,2,16,256]{4,3,2,1,0:T(8,128)(2,1)S(1)} %get-tuple-element.35), channel_id=1, source_target_pairs={{0,192},{16,208},{32,224},{48,240},{64,0},{80,16},{96,32},{112,48}... | collective-permute-start | bytes 393224 | tf_op jit(solution)/shard_map/ppermute | solution.py:50
  217.5 23.7 %collective-permute-start.17 = (bf16[2,4,2,16,256]{4,3,2,1,0:T(8,128)(2,1)S(1)}, bf16[2,4,2,16,256]{4,3,2,1,0:T(8,128)(2,1)S(1)}, u32[]{:S(2)}, u32[]{:S(2)}) collective-permute-start(bf16[2,4,2,16,256]{4,3,2,1,0:T(8,128)(2,1)S(1)} %get-tuple-element.34), channel_id=1, source_target_pairs={{0,208},{16,224},{32,240},{48,0},{64,16},{80,32},{96,48},{112,64},... | collective-permute-start | bytes 393224 | tf_op jit(solution)/shard_map/ppermute | solution.py:50
  219.7 25.1 %collective-permute-start.18 = (bf16[2,4,2,16,256]{4,3,2,1,0:T(8,128)(2,1)S(1)}, bf16[2,4,2,16,256]{4,3,2,1,0:T(8,128)(2,1)S(1)}, u32[]{:S(2)}, u32[]{:S(2)}) collective-permute-start(bf16[2,4,2,16,256]{4,3,2,1,0:T(8,128)(2,1)S(1)} %get-tuple-element.33), channel_id=1, source_target_pairs={{0,224},{16,240},{32,0},{48,16},{64,32},{80,48},{96,64},{112,80},{... | collective-permute-start | bytes 393224 | tf_op jit(solution)/shard_map/ppermute | solution.py:50
  227.7 2.9 copy-start.1
  232.3 27.1 %collective-permute-start.1 = (bf16[2,32,7168]{2,1,0:T(8,128)(2,1)}, bf16[2,32,7168]{2,1,0:T(8,128)(2,1)}, u32[]{:S(2)}, u32[]{:S(2)}) collective-permute-start(bf16[2,32,7168]{2,1,0:T(8,128)(2,1)} %get-tuple-element.27), channel_id=1, source_target_pairs={{0,4},{4,8},{8,12},{12,0},{1,5},{5,9},{9,13},{13,1},{2,6},{6,10},{... | collective-permute-start | bytes 2752520 | tf_op jit(solution)/shard_map/ppermute | solution.py:174
  233.7 43.0 %collective-permute-start.2 = (bf16[2,32,7168]{2,1,0:T(8,128)(2,1)}, bf16[2,32,7168]{2,1,0:T(8,128)(2,1)}, u32[]{:S(2)}, u32[]{:S(2)}) collective-permute-start(bf16[2,32,7168]{2,1,0:T(8,128)(2,1)} %get-tuple-element.29), channel_id=1, source_target_pairs={{0,8},{4,12},{8,0},{12,4},{1,9},{5,13},{9,1},{13,5},{2,10},{6,14},... | collective-permute-start | bytes 2752520 | tf_op jit(solution)/shard_map/ppermute | solution.py:174
  240.1 36.6 %collective-permute-start.3 = (bf16[2,32,7168]{2,1,0:T(8,128)(2,1)S(1)}, bf16[2,32,7168]{2,1,0:T(8,128)(2,1)}, u32[]{:S(2)}, u32[]{:S(2)}) collective-permute-start(bf16[2,32,7168]{2,1,0:T(8,128)(2,1)S(1)} %get-tuple-element.28), channel_id=1, source_target_pairs={{0,12},{4,0},{8,4},{12,8},{1,13},{5,1},{9,5},{13,9},{2,14},{6,2},{... | collective-permute-start | bytes 2752520 | tf_op jit(solution)/shard_map/ppermute | solution.py:174
  241.2 5.5 %collective-permute-start.19 = (bf16[2,4,2,16,256]{4,3,2,1,0:T(8,128)(2,1)S(1)}, bf16[2,4,2,16,256]{4,3,2,1,0:T(8,128)(2,1)S(1)}, u32[]{:S(2)}, u32[]{:S(2)}) collective-permute-start(bf16[2,4,2,16,256]{4,3,2,1,0:T(8,128)(2,1)S(1)} %get-tuple-element.32), channel_id=1, source_target_pairs={{0,240},{16,0},{32,16},{48,32},{64,48},{80,64},{96,80},{112,96},{1... | collective-permute-start | bytes 393224 | tf_op jit(solution)/shard_map/ppermute | solution.py:50
  279.5 32.8 %collective-permute-start.4 = (bf16[32,7168]{1,0:T(8,128)(2,1)S(1)}, bf16[32,7168]{1,0:T(8,128)(2,1)S(1)}, u32[]{:S(2)}, u32[]{:S(2)}) collective-permute-start(bf16[32,7168]{1,0:T(8,128)(2,1)S(1)} %fusion.6), channel_id=1, source_target_pairs={{0,2},{2,0},{1,3},{3,1},{4,6},{6,4},{5,7},{7,5},{8,10},{10,8},{9,1... | collective-permute-start | bytes 1376264 | tf_op jit(solution)/shard_map/ppermute | solution.py:174
Sparse Core Ops, SparseCore 0:
  11.0 105.9 all-gather.2

commit v9 on v6

--- a/solution.py
+++ b/solution.py
@@ -149,8 +149,8 @@
 ):
     moved, inverse = relayout(cache_keys, cache_values, page_table)
     attended, moved = attention(queries, stretch_keys, stretch_values, segment_ids, block_live, moved)
+    projected, moved = reduce_rows(attended, out_weight, moved)
     decode_keys, decode_values = place_pages(moved, inverse)
-    projected = reduce_rows(attended, out_weight)
     return (attended, projected, decode_keys, decode_values)
 
 
@@ -166,7 +166,7 @@
     return total
 
 
-def reduce_rows(attended, out_weight):
+def reduce_rows(attended, out_weight, moved):
     x_size, zl_size, c_size = [lax.axis_size(name) for name in HEAD]
     rows, width = attended.shape
     share = rows // (x_size * zl_size * c_size)
@@ -174,9 +174,10 @@
     partial = jnp.dot(order, out_weight, preferred_element_type=jnp.float32).astype(jnp.bfloat16)
     columns = partial.shape[1]
     total = exchange(partial.reshape(c_size, x_size, zl_size, share, columns), "c")
+    total, moved = lax.optimization_barrier((total, moved))
     total = exchange(total.reshape(x_size, zl_size, share, columns), "x")
     total = exchange(total.reshape(zl_size, share, columns), "zl")
-    return total.astype(jnp.bfloat16)
+    return (total.astype(jnp.bfloat16), moved)
 
 
 def solution(mesh):

time: 258 us -> 273 us (1.058)
  starting transfers between devices: 48.2 us -> 58 us
  waiting for transfers between devices: 144 us -> 147 us
    ppermute x5, waiting for transfers between devices: 9.39 us -> 50.1 us  [exchange(): total = total + lax.ppermute(sent, name, pairs).astype(jnp.float32)]
    all_to_all x1, waiting for transfers between devices: 38.2 us -> 0.01 us  [place_pages(): lax.all_to_all(outgoing, SEQ, split_axis=0, concat_axis=0, tiled=True)]
    ppermute x5, starting transfers between devices: 5.8 us -> 16.8 us  [exchange(): total = total + lax.ppermute(sent, name, pairs).astype(jnp.float32)]
  transfers between devices with their start and end apart: 7 -> 7, of which waited for: 3 -> 3; matrix products, arithmetic and copies ran while one was open for 10% -> 6% of each run, Pallas kernels for 0% -> 0%
where the time goes in v9:
time: 273 us; the launch traced here: 275 us
  waiting for transfers between devices  147 us (54%)
  starting transfers between devices  58 us (21%)
  local copies, waits for them, and re-layouts  24.5 us (9%)
  other arithmetic  17.2 us (6%)
  between operations  14.3 us (5%)
  Pallas kernels  9.77 us (4%)
  matrix products  4.13 us (2%)
    all_gather x1, waiting for transfers between devices, attention(): kv_all = lax.all_gather(kv, SEQ, axis=0, tiled=False)  96.6 us
    ppermute x5, waiting for transfers between devices, exchange(): total = total + lax.ppermute(sent, name, pairs).astype(jnp.float32)  50.1 us
    all_to_all x1, starting transfers between devices, place_pages(): lax.all_to_all(outgoing, SEQ, split_axis=0, concat_axis=0, tiled=True)  41.2 us
    ppermute x5, starting transfers between devices, exchange(): total = total + lax.ppermute(sent, name, pairs).astype(jnp.float32)  16.8 us
    pallas_call x1, Pallas kernels, attend(): pl.pallas_call(kernel, grid_spec=pltpu.PrefetchScalarGridSpec(num_scalar_...  9.77 us
    add x2, other arithmetic, exchange(): total = total + lax.ppermute(sent, name, pairs).astype(jnp.float32)  7.09 us
    unnamed x10, local copies, waits for them, and re-layouts  6.78 us
  transfers between devices with their start and end apart: 7, of which 3 were waited for; matrix products, arithmetic and copies ran while one was open for 6% of the time, Pallas kernels for 0%

profile of v9, /device:TPU:8, one launch (start us, length us, event | category | flops | bytes accessed | tf_op | source)
XLA Modules:
  0.0 274.7 jit_solution(14428798785445458163)
XLA Ops:
  7.2 0.0 all-gather.3.cloned.1.call-start
  7.2 2.0 pad_maximum_fusion.1
  9.2 0.0 all-gather.3.cloned.1.call-update
  9.3 0.8 reshape.113
  10.1 0.8 reshape.114
  10.9 0.1 copy.45
  11.0 0.1 select_reduce_fusion.2
  11.1 0.1 iota_add_fusion
  11.2 0.1 add.130
  11.3 0.4 fusion.10
  11.7 0.1 select_reduce_fusion
  11.8 0.1 reduce_sum.31
  11.9 1.6 pad_maximum_fusion
  13.5 2.3 gather_fusion
  15.8 0.3 select_bitcast_fusion.1
  16.0 0.2 copy.46
  16.2 0.9 copy.47.qseg_ref
  17.1 0.6 fusion.16
  17.7 1.4 fusion.11
  19.1 0.7 and_select_fusion.2
  19.8 0.6 pad_add_fusion.meta_ref
  20.4 96.6 %all-gather.3.cloned.1.call-done = bf16[32,512,256]{2,1,0:T(8,128)(2,1)} async-done(((bf16[2,512,256]{2,1,0:T(8,128)(2,1)}), bf16[32,512,256]{2,1,0:T(8,128)(2,1)}) %all-gather.3.cloned.1.call-update) | async-done | bytes 8388624 | tf_op jit(solution)/shard_map/all_gather | solution.py:134
  117.0 9.8 %shard_map.120 = bf16[512,256]{1,0:T(8,128)(2,1)} custom-call(s32[17]{0:T(128)} %pad_add_fusion.meta_ref, bf16[512,256]{1,0:T(8,128)(2,1)} %q_ref.1, s32[512,1]{1,0:T(8,128)} %copy.47.qseg_ref, s32[16,1,512]{2,1,0:T(1,128)} %bitcast.82, bf16[16,2,512,256]{3,2,1,0:T(8,128)(2,1)} %bitcast.69, bf16[16,2,512,256]{3,2,1,0:T(8,128)(2,1)} %bitcast.70), custom_call_target="tpu_custom_call" | custom-call | tf_op jit(solution)/shard_map/pallas_call | solution.py:100
  126.8 1.0 copy.48
  127.7 4.1 %convolution_convert_fusion = bf16[512,7168]{1,0:T(8,128)(2,1)S(1)} fusion(bf16[512,256]{1,0:T(8,128)(2,1)S(1)} %bitcast.77, bf16[256,7168]{1,0:T(8,128)(2,1)} %param.16), kind=kOutput, calls=%fused_computation.2 | convolution fusion | flops 1882718208 | bytes 11272192 | tf_op jit(solution)/shard_map/dot_general | solution.py:174
  131.9 2.4 dynamic-slice_bitcast_fusion
  134.3 1.7 copy-done
  135.9 6.7 %collective-permute-done = bf16[4,2,32,7168]{3,2,1,0:T(8,128)(2,1)} collective-permute-done((bf16[4,2,32,7168]{3,2,1,0:T(8,128)(2,1)}, bf16[4,2,32,7168]{3,2,1,0:T(8,128)(2,1)}, u32[]{:S(2)}, u32[]{:S(2)}) %collective-permute-start) | collective-permute-done | bytes 3670048 | tf_op jit(solution)/shard_map/ppermute | solution.py:165
  142.7 4.4 %convert_add_fusion = f32[4,2,32,7168]{3,2,1,0:T(8,128)S(1)} fusion(bf16[4,2,32,7168]{3,2,1,0:T(8,128)(2,1)} %collective-permute-done, bf16[2,4,2,32,7168]{4,3,2,1,0:T(8,128)(2,1)} %bitcast.72, s32[]{:T(128)S(6)} %select_n.115), kind=kLoop, calls=%fused_computation.3 | loop fusion | flops 5505024 | bytes 14680068 | tf_op jit(solution)/shard_map/add | solution.py:165
  147.1 3.0 %copy-done.1 = f32[4,2,32,7168]{3,2,1,0:T(8,128)} copy-done((f32[4,2,32,7168]{3,2,1,0:T(8,128)}, f32[4,2,32,7168]{3,2,1,0:T(8,128)S(1)}, u32[]{:S(2)}) %copy-start.1) | copy-done | bytes 7340056
  150.0 1.6 fusion.2
  151.6 1.5 collective-permute-start.1
  153.1 6.8 %collective-permute-start.2 = (bf16[2,32,7168]{2,1,0:T(8,128)(2,1)}, bf16[2,32,7168]{2,1,0:T(8,128)(2,1)}, u32[]{:S(2)}, u32[]{:S(2)}) collective-permute-start(bf16[2,32,7168]{2,1,0:T(8,128)(2,1)} %get-tuple-element.41), channel_id=1, source_target_pairs={{0,8},{4,12},{8,0},{12,4},{1,9},{5,13},{9,1},{13,5},{2,10},{6,14},... | collective-permute-start | bytes 2752520 | tf_op jit(solution)/shard_map/ppermute | solution.py:165
  159.8 0.0 collective-permute-start.3
  159.8 0.1 select_reduce_fusion.1
  160.0 1.6 copy.49
  161.6 41.2 %all-to-all-start = ((bf16[16,2,4,2,16,256]{5,4,3,2,1,0:T(8,128)(2,1)}), bf16[16,2,4,2,16,256]{5,4,3,2,1,0:T(8,128)(2,1)S(1)}, u32[]{:S(2)}, u32[]{:S(2)}) async-start(bf16[16,2,4,2,16,256]{5,4,3,2,1,0:T(8,128)(2,1)} %copy.49), calls=%async_computation | async-start | bytes 4194304 | tf_op jit(solution)/shard_map/all_to_all | solution.py:42
  202.8 2.7 fusion.1
  205.5 0.1 fusion.6
  205.6 8.5 %collective-permute-start.4 = (bf16[32,7168]{1,0:T(8,128)(2,1)S(1)}, bf16[32,7168]{1,0:T(8,128)(2,1)S(1)}, u32[]{:S(2)}, u32[]{:S(2)}) collective-permute-start(bf16[32,7168]{1,0:T(8,128)(2,1)S(1)} %fusion.6), channel_id=1, source_target_pairs={{0,2},{2,0},{1,3},{3,1},{4,6},{6,4},{5,7},{7,5},{8,10},{10,8},{9,1... | collective-permute-start | bytes 1376264 | tf_op jit(solution)/shard_map/ppermute | solution.py:165
  214.2 43.4 %collective-permute-done.4 = bf16[32,7168]{1,0:T(8,128)(2,1)S(1)} collective-permute-done((bf16[32,7168]{1,0:T(8,128)(2,1)S(1)}, bf16[32,7168]{1,0:T(8,128)(2,1)S(1)}, u32[]{:S(2)}, u32[]{:S(2)}) %collective-permute-start.4) | collective-permute-done | bytes 458784 | tf_op jit(solution)/shard_map/ppermute | solution.py:165
  257.5 0.9 fusion.5
  258.4 1.6 copy.50
  260.0 3.6 %gather_fusion.1 = bf16[32,2,4,16,256]{4,3,2,1,0:T(8,128)(2,1)} fusion(bf16[2,4,32,16,256]{4,3,2,1,0:T(8,128)(2,1)} %bitcast.75, s32[1024]{0:T(1024)S(1)} %pad_clamp_fusion), kind=kCustom, calls=%fused_computation.1.clone | custom fusion | bytes 4194432 | tf_op jit(solution)/shard_map/jit(_take)/gather | solution.py:45
  263.6 1.8 select_bitcast_fusion
  265.4 0.2 slice_bitcast_fusion
  265.7 1.1 copy.51
  266.7 1.1 copy.52
  (21 shorter events, 0.1 us)
Async XLA Ops:
  7.2 4.7 %copy-start.3 = (bf16[4,512,256]{2,1,0:T(8,128)(2,1)S(1)}, bf16[4,512,256]{2,1,0:T(8,128)(2,1)}, u32[]{:S(2)}) copy-start(bf16[4,512,256]{2,1,0:T(8,128)(2,1)} %param.17) | copy-start | bytes 3145732
  7.2 4.7 %copy-start.2 = (bf16[4,512,256]{2,1,0:T(8,128)(2,1)S(1)}, bf16[4,512,256]{2,1,0:T(8,128)(2,1)}, u32[]{:S(2)}) copy-start(bf16[4,512,256]{2,1,0:T(8,128)(2,1)} %param.18) | copy-start | bytes 3145732
  7.2 109.8 %all-gather.3.cloned.1.call-start = ((), (), s32[]{:S(2)}) async-start(), calls=%async_computation.1 | async-start | bytes 8912896 | tf_op jit(solution)/shard_map/all_gather | solution.py:134
  131.9 4.1 %copy-start = (bf16[512,7168]{1,0:T(8,128)(2,1)}, bf16[512,7168]{1,0:T(8,128)(2,1)S(1)}, u32[]{:S(2)}) copy-start(bf16[512,7168]{1,0:T(8,128)(2,1)S(1)} %convolution_convert_fusion) | copy-start | bytes 22020100
  135.9 6.8 %collective-permute-start = (bf16[4,2,32,7168]{3,2,1,0:T(8,128)(2,1)}, bf16[4,2,32,7168]{3,2,1,0:T(8,128)(2,1)}, u32[]{:S(2)}, u32[]{:S(2)}) collective-permute-start(bf16[4,2,32,7168]{3,2,1,0:T(8,128)(2,1)} %dynamic-slice_bitcast_fusion), channel_id=1, source_target_pairs={{0,1},{1,0},{2,3},{3,2},{4,5},{5,4},{6,7},{7,6},{8,9},{9,8},{10,11... | collective-permute-start | bytes 11010056 | tf_op jit(solution)/shard_map/ppermute | solution.py:165
  147.1 3.0 %copy-start.1 = (f32[4,2,32,7168]{3,2,1,0:T(8,128)}, f32[4,2,32,7168]{3,2,1,0:T(8,128)S(1)}, u32[]{:S(2)}) copy-start(f32[4,2,32,7168]{3,2,1,0:T(8,128)S(1)} %convert_add_fusion) | copy-start | bytes 22020100
  151.6 51.2 %collective-permute-start.1 = (bf16[2,32,7168]{2,1,0:T(8,128)(2,1)}, bf16[2,32,7168]{2,1,0:T(8,128)(2,1)}, u32[]{:S(2)}, u32[]{:S(2)}) collective-permute-start(bf16[2,32,7168]{2,1,0:T(8,128)(2,1)} %get-tuple-element.39), channel_id=1, source_target_pairs={{0,4},{4,8},{8,12},{12,0},{1,5},{5,9},{9,13},{13,1},{2,6},{6,10},{... | collective-permute-start | bytes 2752520 | tf_op jit(solution)/shard_map/ppermute | solution.py:165
  153.1 49.7 %collective-permute-start.2 = (bf16[2,32,7168]{2,1,0:T(8,128)(2,1)}, bf16[2,32,7168]{2,1,0:T(8,128)(2,1)}, u32[]{:S(2)}, u32[]{:S(2)}) collective-permute-start(bf16[2,32,7168]{2,1,0:T(8,128)(2,1)} %get-tuple-element.41), channel_id=1, source_target_pairs={{0,8},{4,12},{8,0},{12,4},{1,9},{5,13},{9,1},{13,5},{2,10},{6,14},... | collective-permute-start | bytes 2752520 | tf_op jit(solution)/shard_map/ppermute | solution.py:165
  159.8 43.0 %collective-permute-start.3 = (bf16[2,32,7168]{2,1,0:T(8,128)(2,1)S(1)}, bf16[2,32,7168]{2,1,0:T(8,128)(2,1)}, u32[]{:S(2)}, u32[]{:S(2)}) collective-permute-start(bf16[2,32,7168]{2,1,0:T(8,128)(2,1)S(1)} %get-tuple-element.40), channel_id=1, source_target_pairs={{0,12},{4,0},{8,4},{12,8},{1,13},{5,1},{9,5},{13,9},{2,14},{6,2},{... | collective-permute-start | bytes 2752520 | tf_op jit(solution)/shard_map/ppermute | solution.py:165
  161.6 96.8 %all-to-all-start = ((bf16[16,2,4,2,16,256]{5,4,3,2,1,0:T(8,128)(2,1)}), bf16[16,2,4,2,16,256]{5,4,3,2,1,0:T(8,128)(2,1)S(1)}, u32[]{:S(2)}, u32[]{:S(2)}) async-start(bf16[16,2,4,2,16,256]{5,4,3,2,1,0:T(8,128)(2,1)} %copy.49), calls=%async_computation | async-start | bytes 4194304 | tf_op jit(solution)/shard_map/all_to_all | solution.py:42
  205.6 51.9 %collective-permute-start.4 = (bf16[32,7168]{1,0:T(8,128)(2,1)S(1)}, bf16[32,7168]{1,0:T(8,128)(2,1)S(1)}, u32[]{:S(2)}, u32[]{:S(2)}) collective-permute-start(bf16[32,7168]{1,0:T(8,128)(2,1)S(1)} %fusion.6), channel_id=1, source_target_pairs={{0,2},{2,0},{1,3},{3,1},{4,6},{6,4},{5,7},{7,5},{8,10},{10,8},{9,1... | collective-permute-start | bytes 1376264 | tf_op jit(solution)/shard_map/ppermute | solution.py:165
Sparse Core Ops, SparseCore 0:
  11.0 105.9 all-gather.2

commit v10 on v6

--- a/solution.py
+++ b/solution.py
@@ -12,7 +12,7 @@
 HD = 128
 SEQ = ("zh", "y")
 HEAD = ("x", "zl", "c")
-Q_ROWS = 256
+Q_ROWS = 512
 
 
 def relayout(cache_keys, cache_values, page_table):
@@ -170,10 +170,19 @@
     x_size, zl_size, c_size = [lax.axis_size(name) for name in HEAD]
     rows, width = attended.shape
     share = rows // (x_size * zl_size * c_size)
-    order = attended.reshape(x_size, zl_size, c_size, share, width).transpose(2, 0, 1, 3, 4).reshape(rows, width)
-    partial = jnp.dot(order, out_weight, preferred_element_type=jnp.float32).astype(jnp.bfloat16)
-    columns = partial.shape[1]
-    total = exchange(partial.reshape(c_size, x_size, zl_size, share, columns), "c")
+    order = attended.reshape(x_size, zl_size, c_size, share, width).transpose(2, 0, 1, 3, 4)
+    columns = out_weight.shape[1]
+    me = lax.axis_index("c")
+    total = None
+    for shift in range(c_size):
+        rows_for = lax.dynamic_index_in_dim(order, (me + shift) % c_size, 0, keepdims=False)
+        piece = jnp.dot(rows_for.reshape(-1, width), out_weight, preferred_element_type=jnp.float32)
+        piece = piece.astype(jnp.bfloat16).reshape(x_size, zl_size, share, columns)
+        if shift:
+            pairs = [(i, (i + shift) % c_size) for i in range(c_size)]
+            total = total + lax.ppermute(piece, "c", pairs).astype(jnp.float32)
+        else:
+            total = piece.astype(jnp.float32)
     total = exchange(total.reshape(x_size, zl_size, share, columns), "x")
     total = exchange(total.reshape(zl_size, share, columns), "zl")
     return total.astype(jnp.bfloat16)

time: 258 us -> 251 us (0.973)
  local copies, waits for them, and re-layouts: 23.1 us -> 19.1 us
  matrix products: 4.13 us -> 8.12 us
  starting transfers between devices: 48.2 us -> 44.4 us
    add x2 -> x1, other arithmetic: 7.09 us -> 2.71 us  [exchange(): total = total + lax.ppermute(sent, name, pairs).astype(jnp.float32)]
    dot_general x1 -> x2, matrix products: 4.13 us -> 8.12 us  [reduce_rows(): jnp.dot(rows_for.reshape(-1, width), out_weight, preferred_element_type=j...]
    all_to_all x1, starting transfers between devices: 42.3 us -> 38.8 us  [place_pages(): lax.all_to_all(outgoing, SEQ, split_axis=0, concat_axis=0, tiled=True)]
    add x0 -> x1, other arithmetic: none -> 3.26 us  [reduce_rows(): total = total + lax.ppermute(piece, 'c', pairs).astype(jnp.float32)]
    unnamed x10 -> x8, local copies, waits for them, and re-layouts: 6.78 us -> 5.1 us
    ppermute x5 -> x4, waiting for transfers between devices: 9.39 us -> 8.94 us  [exchange(): total = total + lax.ppermute(sent, name, pairs).astype(jnp.float32)]
    ppermute x5 -> x4, starting transfers between devices: 5.8 us -> 5.59 us  [exchange(): total = total + lax.ppermute(sent, name, pairs).astype(jnp.float32)]
  transfers between devices with their start and end apart: 7 -> 7, of which waited for: 3 -> 3; matrix products, arithmetic and copies ran while one was open for 10% -> 11% of each run, Pallas kernels for 0% -> 0%
where the time goes in v10:
time: 251 us; the launch traced here: 250 us
  waiting for transfers between devices  142 us (57%)
  starting transfers between devices  44.4 us (18%)
  local copies, waits for them, and re-layouts  19.1 us (8%)
  other arithmetic  14.4 us (6%)
  between operations  14.3 us (6%)
  matrix products  8.12 us (3%)
  Pallas kernels  7.49 us (3%)
    all_gather x1, waiting for transfers between devices, attention(): kv_all = lax.all_gather(kv, SEQ, axis=0, tiled=False)  96.6 us
    all_to_all x1, starting transfers between devices, place_pages(): lax.all_to_all(outgoing, SEQ, split_axis=0, concat_axis=0, tiled=True)  38.8 us
    all_to_all x1, waiting for transfers between devices, place_pages(): lax.all_to_all(outgoing, SEQ, split_axis=0, concat_axis=0, tiled=True)  36.3 us
    ppermute x4, waiting for transfers between devices, exchange(): total = total + lax.ppermute(sent, name, pairs).astype(jnp.float32)  8.94 us
    dot_general x2, matrix products, reduce_rows(): jnp.dot(rows_for.reshape(-1, width), out_weight, preferred_element_type=j...  8.12 us
    pallas_call x1, Pallas kernels, attend(): pl.pallas_call(kernel, grid_spec=pltpu.PrefetchScalarGridSpec(num_scalar_...  7.49 us
    ppermute x4, starting transfers between devices, exchange(): total = total + lax.ppermute(sent, name, pairs).astype(jnp.float32)  5.59 us
    unnamed x8, local copies, waits for them, and re-layouts  5.1 us
  transfers between devices with their start and end apart: 7, of which 3 were waited for; matrix products, arithmetic and copies ran while one was open for 11% of the time, Pallas kernels for 0%

profile of v10, /device:TPU:8, one launch (start us, length us, event | category | flops | bytes accessed | tf_op | source)
XLA Modules:
  0.0 249.7 jit_solution(10726671446235378715)
XLA Ops:
  7.2 0.0 all-gather.3.cloned.1.call-start
  7.2 2.0 pad_maximum_fusion.1
  9.2 0.0 all-gather.3.cloned.1.call-update
  9.3 0.8 reshape.123
  10.1 0.8 reshape.124
  10.9 0.1 copy.40
  11.0 0.1 select_reduce_fusion.2
  11.1 0.1 iota_add_fusion
  11.2 0.1 add.133
  11.3 0.4 fusion.10
  11.7 0.1 select_reduce_fusion
  11.8 0.1 reduce_sum.31
  11.9 1.6 pad_maximum_fusion
  13.5 2.3 gather_fusion
  15.8 0.3 select_bitcast_fusion.1
  16.0 0.2 copy.41
  16.2 0.9 copy.42.qseg_ref
  17.1 0.6 fusion.16
  17.7 1.4 fusion.11
  19.1 0.7 and_select_fusion.2
  19.8 0.6 pad_add_fusion.meta_ref
  20.4 96.6 %all-gather.3.cloned.1.call-done = bf16[32,512,256]{2,1,0:T(8,128)(2,1)} async-done(((bf16[2,512,256]{2,1,0:T(8,128)(2,1)}), bf16[32,512,256]{2,1,0:T(8,128)(2,1)}) %all-gather.3.cloned.1.call-update) | async-done | bytes 8388624 | tf_op jit(solution)/shard_map/all_gather | solution.py:134
  117.0 7.5 %shard_map.120 = bf16[512,256]{1,0:T(8,128)(2,1)} custom-call(s32[17]{0:T(128)} %pad_add_fusion.meta_ref, bf16[512,256]{1,0:T(8,128)(2,1)} %q_ref.1, s32[512,1]{1,0:T(8,128)} %copy.42.qseg_ref, s32[16,1,512]{2,1,0:T(1,128)} %bitcast.80, bf16[16,2,512,256]{3,2,1,0:T(8,128)(2,1)} %bitcast.67, bf16[16,2,512,256]{3,2,1,0:T(8,128)(2,1)} %bitcast.68), custom_call_target="tpu_custom_call" | custom-call | tf_op jit(solution)/shard_map/pallas_call | solution.py:100
  124.5 1.0 constant_dynamic-slice_fusion.1
  125.5 5.0 %convolution_convert_fusion = bf16[256,7168]{1,0:T(8,128)(2,1)} fusion(bf16[256,256]{1,0:T(8,128)(2,1)S(1)} %bitcast.77, bf16[256,7168]{1,0:T(8,128)(2,1)} %param.16), kind=kOutput, calls=%fused_computation.2 | convolution fusion | flops 941359104 | bytes 7471104 | tf_op jit(solution)/shard_map/dot_general | solution.py:179
  130.5 1.6 copy.43
  132.1 38.8 %all-to-all-start = ((bf16[16,2,4,2,16,256]{5,4,3,2,1,0:T(8,128)(2,1)}), bf16[16,2,4,2,16,256]{5,4,3,2,1,0:T(8,128)(2,1)S(1)}, u32[]{:S(2)}, u32[]{:S(2)}) async-start(bf16[16,2,4,2,16,256]{5,4,3,2,1,0:T(8,128)(2,1)} %copy.43), calls=%async_computation | async-start | bytes 4194304 | tf_op jit(solution)/shard_map/all_to_all | solution.py:42
  170.8 3.2 %convolution_convert_fusion.1 = bf16[256,7168]{1,0:T(8,128)(2,1)S(1)} fusion(bf16[256,256]{1,0:T(8,128)(2,1)S(1)} %bitcast.76, bf16[256,7168]{1,0:T(8,128)(2,1)} %param.16), kind=kOutput, calls=%fused_computation.3 | convolution fusion | flops 941359104 | bytes 7471104 | tf_op jit(solution)/shard_map/dot_general | solution.py:179
  174.0 0.0 collective-permute-done
  174.0 3.3 %convert_add_fusion = f32[4,2,32,7168]{3,2,1,0:T(8,128)S(1)} fusion(bf16[4,2,32,7168]{3,2,1,0:T(8,128)(2,1)S(1)} %bitcast.69, bf16[4,2,32,7168]{3,2,1,0:T(8,128)(2,1)} %collective-permute-done), kind=kLoop, calls=%fused_computation.4 | loop fusion | flops 5505024 | bytes 14680064 | tf_op jit(solution)/shard_map/add | solution.py:183
  177.3 3.0 %copy-done = f32[4,2,32,7168]{3,2,1,0:T(8,128)} copy-done((f32[4,2,32,7168]{3,2,1,0:T(8,128)}, f32[4,2,32,7168]{3,2,1,0:T(8,128)S(1)}, u32[]{:S(2)}) %copy-start) | copy-done | bytes 7340056
  180.2 1.6 fusion.2
  181.8 1.4 collective-permute-start.1
  183.2 2.7 %collective-permute-start.2 = (bf16[2,32,7168]{2,1,0:T(8,128)(2,1)}, bf16[2,32,7168]{2,1,0:T(8,128)(2,1)}, u32[]{:S(2)}, u32[]{:S(2)}) collective-permute-start(bf16[2,32,7168]{2,1,0:T(8,128)(2,1)} %get-tuple-element.37), channel_id=1, source_target_pairs={{0,8},{4,12},{8,0},{12,4},{1,9},{5,13},{9,1},{13,5},{2,10},{6,14},... | collective-permute-start | bytes 2752520 | tf_op jit(solution)/shard_map/ppermute | solution.py:165
  185.9 1.5 collective-permute-start.3
  187.3 0.1 select_reduce_fusion.1
  187.5 36.3 %all-to-all-done = bf16[16,2,4,2,16,256]{5,4,3,2,1,0:T(8,128)(2,1)S(1)} async-done(((bf16[16,2,4,2,16,256]{5,4,3,2,1,0:T(8,128)(2,1)}), bf16[16,2,4,2,16,256]{5,4,3,2,1,0:T(8,128)(2,1)S(1)}, u32[]{:S(2)}, u32[]{:S(2)}) %all-to-all-start) | async-done | bytes 2097184 | tf_op jit(solution)/shard_map/all_to_all | solution.py:42
  223.8 1.6 copy.44
  225.4 2.3 gather_fusion.1
  227.7 2.7 %fusion.1 = f32[2,32,7168]{2,1,0:T(8,128)S(1)} fusion(bf16[2,32,7168]{2,1,0:T(8,128)(2,1)} %collective-permute-done.3, bf16[2,32,7168]{2,1,0:T(8,128)(2,1)} %collective-permute-done.2, bf16[2,32,7168]{2,1,0:T(8,128)(2,1)} %collective-permute-done.1, f32[4,2,32,7168]{3,2,1,0:T(8,128)} %copy-done, s32[]{:T(128)S(6)} %select_n.123), kind=kLoop, calls=%fused_computation.10 | loop fusion | flops 2752512 | bytes 6422532 | tf_op jit(solution)/shard_map/add | solution.py:165
  230.4 0.1 fusion.6
  230.5 0.1 collective-permute-start.4
  230.6 0.3 select_bitcast_fusion
  230.8 0.1 slice_bitcast_fusion
  231.0 1.1 copy.45
  232.1 1.1 copy.46
  233.1 8.9 %collective-permute-done.4 = bf16[32,7168]{1,0:T(8,128)(2,1)S(1)} collective-permute-done((bf16[32,7168]{1,0:T(8,128)(2,1)S(1)}, bf16[32,7168]{1,0:T(8,128)(2,1)S(1)}, u32[]{:S(2)}, u32[]{:S(2)}) %collective-permute-start.4) | collective-permute-done | bytes 458784 | tf_op jit(solution)/shard_map/ppermute | solution.py:165
  242.1 0.8 fusion.5
  (19 shorter events, 0.1 us)
Async XLA Ops:
  7.2 4.7 %copy-start.2 = (bf16[4,512,256]{2,1,0:T(8,128)(2,1)S(1)}, bf16[4,512,256]{2,1,0:T(8,128)(2,1)}, u32[]{:S(2)}) copy-start(bf16[4,512,256]{2,1,0:T(8,128)(2,1)} %param.17) | copy-start | bytes 3145732
  7.2 4.7 %copy-start.1 = (bf16[4,512,256]{2,1,0:T(8,128)(2,1)S(1)}, bf16[4,512,256]{2,1,0:T(8,128)(2,1)}, u32[]{:S(2)}) copy-start(bf16[4,512,256]{2,1,0:T(8,128)(2,1)} %param.18) | copy-start | bytes 3145732
  7.2 109.8 %all-gather.3.cloned.1.call-start = ((), (), s32[]{:S(2)}) async-start(), calls=%async_computation.1 | async-start | bytes 8912896 | tf_op jit(solution)/shard_map/all_gather | solution.py:134
  130.4 43.6 %collective-permute-start = (bf16[4,2,32,7168]{3,2,1,0:T(8,128)(2,1)}, bf16[4,2,32,7168]{3,2,1,0:T(8,128)(2,1)}, u32[]{:S(2)}, u32[]{:S(2)}) collective-permute-start(bf16[4,2,32,7168]{3,2,1,0:T(8,128)(2,1)} %bitcast.20), channel_id=1, source_target_pairs={{0,1},{1,0},{2,3},{3,2},{4,5},{5,4},{6,7},{7,6},{8,9},{9,8},{10,11... | collective-permute-start | bytes 11010056 | tf_op jit(solution)/shard_map/ppermute | solution.py:183
  132.1 91.7 %all-to-all-start = ((bf16[16,2,4,2,16,256]{5,4,3,2,1,0:T(8,128)(2,1)}), bf16[16,2,4,2,16,256]{5,4,3,2,1,0:T(8,128)(2,1)S(1)}, u32[]{:S(2)}, u32[]{:S(2)}) async-start(bf16[16,2,4,2,16,256]{5,4,3,2,1,0:T(8,128)(2,1)} %copy.43), calls=%async_computation | async-start | bytes 4194304 | tf_op jit(solution)/shard_map/all_to_all | solution.py:42
  177.3 3.0 %copy-start = (f32[4,2,32,7168]{3,2,1,0:T(8,128)}, f32[4,2,32,7168]{3,2,1,0:T(8,128)S(1)}, u32[]{:S(2)}) copy-start(f32[4,2,32,7168]{3,2,1,0:T(8,128)S(1)} %convert_add_fusion) | copy-start | bytes 22020100
  181.8 45.8 %collective-permute-start.1 = (bf16[2,32,7168]{2,1,0:T(8,128)(2,1)}, bf16[2,32,7168]{2,1,0:T(8,128)(2,1)}, u32[]{:S(2)}, u32[]{:S(2)}) collective-permute-start(bf16[2,32,7168]{2,1,0:T(8,128)(2,1)} %get-tuple-element.35), channel_id=1, source_target_pairs={{0,4},{4,8},{8,12},{12,0},{1,5},{5,9},{9,13},{13,1},{2,6},{6,10},{... | collective-permute-start | bytes 2752520 | tf_op jit(solution)/shard_map/ppermute | solution.py:165
  183.2 44.5 %collective-permute-start.2 = (bf16[2,32,7168]{2,1,0:T(8,128)(2,1)}, bf16[2,32,7168]{2,1,0:T(8,128)(2,1)}, u32[]{:S(2)}, u32[]{:S(2)}) collective-permute-start(bf16[2,32,7168]{2,1,0:T(8,128)(2,1)} %get-tuple-element.37), channel_id=1, source_target_pairs={{0,8},{4,12},{8,0},{12,4},{1,9},{5,13},{9,1},{13,5},{2,10},{6,14},... | collective-permute-start | bytes 2752520 | tf_op jit(solution)/shard_map/ppermute | solution.py:165
  185.9 41.8 %collective-permute-start.3 = (bf16[2,32,7168]{2,1,0:T(8,128)(2,1)S(1)}, bf16[2,32,7168]{2,1,0:T(8,128)(2,1)}, u32[]{:S(2)}, u32[]{:S(2)}) collective-permute-start(bf16[2,32,7168]{2,1,0:T(8,128)(2,1)S(1)} %get-tuple-element.36), channel_id=1, source_target_pairs={{0,12},{4,0},{8,4},{12,8},{1,13},{5,1},{9,5},{13,9},{2,14},{6,2},{... | collective-permute-start | bytes 2752520 | tf_op jit(solution)/shard_map/ppermute | solution.py:165
  230.5 11.6 %collective-permute-start.4 = (bf16[32,7168]{1,0:T(8,128)(2,1)S(1)}, bf16[32,7168]{1,0:T(8,128)(2,1)S(1)}, u32[]{:S(2)}, u32[]{:S(2)}) collective-permute-start(bf16[32,7168]{1,0:T(8,128)(2,1)S(1)} %fusion.6), channel_id=1, source_target_pairs={{0,2},{2,0},{1,3},{3,1},{4,6},{6,4},{5,7},{7,5},{8,10},{10,8},{9,1... | collective-permute-start | bytes 1376264 | tf_op jit(solution)/shard_map/ppermute | solution.py:165
Sparse Core Ops, SparseCore 0:
  11.0 105.9 all-gather.2

commit v11 on v10

--- a/solution.py
+++ b/solution.py
@@ -40,10 +40,9 @@
 
 def place_pages(outgoing, inverse):
     moved = lax.all_to_all(outgoing, SEQ, split_axis=0, concat_axis=0, tiled=True)
-    _, kinds, layers, per_group, page_len, feat_width = moved.shape
-    moved = moved.transpose(1, 2, 0, 3, 4, 5).reshape(kinds, layers, -1, page_len, feat_width)
-    placed = jnp.take(moved, inverse, axis=2)
-    return (placed[0], placed[1])
+    per_group = moved.shape[3]
+    source, page = inverse // per_group, inverse % per_group
+    return tuple(moved[source, kind, :, page].transpose(1, 0, 2, 3) for kind in range(moved.shape[1]))
 
 
 def attention_kernel(meta_ref, q_ref, qseg_ref, kseg_ref, k_ref, v_ref, o_ref, *, block_count, scale):

time: 251 us -> 253 us (level)
  starting transfers between devices: 44.4 us -> 53 us
  waiting for transfers between devices: 142 us -> 136 us
  local copies, waits for them, and re-layouts: 19.1 us -> 16.5 us
    ppermute x4, starting transfers between devices: 5.59 us -> 19.3 us  [exchange(): total = total + lax.ppermute(sent, name, pairs).astype(jnp.float32)]
    all_to_all x1, waiting for transfers between devices: 36.3 us -> 30.5 us  [place_pages(): lax.all_to_all(outgoing, SEQ, split_axis=0, concat_axis=0, tiled=True)]
    all_to_all x1, starting transfers between devices: 38.8 us -> 33.7 us  [place_pages(): lax.all_to_all(outgoing, SEQ, split_axis=0, concat_axis=0, tiled=True)]
    ppermute x1, waiting for transfers between devices: 0.01 us -> 3.58 us  [reduce_rows(): total = total + lax.ppermute(piece, 'c', pairs).astype(jnp.float32)]
    ppermute x4, waiting for transfers between devices: 8.94 us -> 6.07 us  [exchange(): total = total + lax.ppermute(sent, name, pairs).astype(jnp.float32)]
    unnamed x8 -> x12, local copies, waits for them, and re-layouts: 5.1 us -> 5.94 us
  transfers between devices with their start and end apart: 7 -> 7, of which waited for: 3 -> 5; matrix products, arithmetic and copies ran while one was open for 11% -> 9% of each run, Pallas kernels for 0% -> 0%
where the time goes in v11:
time: 253 us; the launch traced here: 252 us
  waiting for transfers between devices  136 us (54%)
  starting transfers between devices  53 us (21%)
  local copies, waits for them, and re-layouts  16.5 us (7%)
  other arithmetic  16.5 us (7%)
  between operations  14.2 us (6%)
  matrix products  8.19 us (3%)
  Pallas kernels  7.49 us (3%)
    all_gather x1, waiting for transfers between devices, attention(): kv_all = lax.all_gather(kv, SEQ, axis=0, tiled=False)  96 us
    all_to_all x1, starting transfers between devices, place_pages(): lax.all_to_all(outgoing, SEQ, split_axis=0, concat_axis=0, tiled=True)  33.7 us
    all_to_all x1, waiting for transfers between devices, place_pages(): lax.all_to_all(outgoing, SEQ, split_axis=0, concat_axis=0, tiled=True)  30.5 us
    ppermute x4, starting transfers between devices, exchange(): total = total + lax.ppermute(sent, name, pairs).astype(jnp.float32)  19.3 us
    dot_general x2, matrix products, reduce_rows(): jnp.dot(rows_for.reshape(-1, width), out_weight, preferred_element_type=j...  8.19 us
    pallas_call x1, Pallas kernels, attend(): pl.pallas_call(kernel, grid_spec=pltpu.PrefetchScalarGridSpec(num_scalar_...  7.49 us
    ppermute x4, waiting for transfers between devices, exchange(): total = total + lax.ppermute(sent, name, pairs).astype(jnp.float32)  6.07 us
    unnamed x12, local copies, waits for them, and re-layouts  5.94 us
  transfers between devices with their start and end apart: 7, of which 5 were waited for; matrix products, arithmetic and copies ran while one was open for 9% of the time, Pallas kernels for 0%

profile of v11, /device:TPU:8, one launch (start us, length us, event | category | flops | bytes accessed | tf_op | source)
XLA Modules:
  0.0 251.9 jit_solution(14356601496522188294)
XLA Ops:
  7.2 0.0 all-gather.3.cloned.1.call-start
  7.2 2.0 pad_maximum_fusion.1
  9.2 0.0 all-gather.3.cloned.1.call-update
  9.3 0.8 reshape.239
  10.1 0.8 reshape.240
  10.9 0.1 copy.39
  11.0 0.6 fusion.22
  11.6 1.5 fusion.12
  13.0 0.7 and_select_fusion.3
  13.7 0.1 select_reduce_fusion.2
  13.9 0.1 copy.40
  14.0 0.1 copy.41
  14.1 0.1 add.204
  14.2 0.9 copy.44.qseg_ref
  15.1 1.5 pad_maximum_fusion
  16.6 2.3 gather_fusion
  18.9 0.6 pad_add_fusion.meta_ref
  19.5 1.6 fusion
  21.0 96.0 %all-gather.3.cloned.1.call-done = bf16[32,512,256]{2,1,0:T(8,128)(2,1)} async-done(((bf16[2,512,256]{2,1,0:T(8,128)(2,1)}), bf16[32,512,256]{2,1,0:T(8,128)(2,1)}) %all-gather.3.cloned.1.call-update) | async-done | bytes 8388624 | tf_op jit(solution)/shard_map/all_gather | solution.py:133
  117.0 7.5 %shard_map.120 = bf16[512,256]{1,0:T(8,128)(2,1)} custom-call(s32[17]{0:T(128)} %pad_add_fusion.meta_ref, bf16[512,256]{1,0:T(8,128)(2,1)} %q_ref.1, s32[512,1]{1,0:T(8,128)} %copy.44.qseg_ref, s32[16,1,512]{2,1,0:T(1,128)} %bitcast.105, bf16[16,2,512,256]{3,2,1,0:T(8,128)(2,1)} %bitcast.92, bf16[16,2,512,256]{3,2,1,0:T(8,128)(2,1)} %bitcast.93), custom_call_target="tpu_custom_call" | custom-call | tf_op jit(solution)/shard_map/pallas_call | solution.py:99
  124.5 1.0 constant_dynamic-slice_fusion.1
  125.5 5.0 %convolution_convert_fusion = bf16[256,7168]{1,0:T(8,128)(2,1)} fusion(bf16[256,256]{1,0:T(8,128)(2,1)S(1)} %bitcast.102, bf16[256,7168]{1,0:T(8,128)(2,1)} %param.14), kind=kOutput, calls=%fused_computation.3 | convolution fusion | flops 941359104 | bytes 7471104 | tf_op jit(solution)/shard_map/dot_general | solution.py:178
  130.5 0.0 collective-permute-start
  130.5 3.2 %convolution_convert_fusion.1 = bf16[256,7168]{1,0:T(8,128)(2,1)S(1)} fusion(bf16[256,256]{1,0:T(8,128)(2,1)S(1)} %bitcast.101, bf16[256,7168]{1,0:T(8,128)(2,1)} %param.14), kind=kOutput, calls=%fused_computation.4 | convolution fusion | flops 941359104 | bytes 7471104 | tf_op jit(solution)/shard_map/dot_general | solution.py:178
  133.7 3.6 %collective-permute-done = bf16[4,2,32,7168]{3,2,1,0:T(8,128)(2,1)} collective-permute-done((bf16[4,2,32,7168]{3,2,1,0:T(8,128)(2,1)}, bf16[4,2,32,7168]{3,2,1,0:T(8,128)(2,1)}, u32[]{:S(2)}, u32[]{:S(2)}) %collective-permute-start) | collective-permute-done | bytes 3670048 | tf_op jit(solution)/shard_map/ppermute | solution.py:182
  137.3 3.3 %convert_add_fusion = f32[4,2,32,7168]{3,2,1,0:T(8,128)S(1)} fusion(bf16[4,2,32,7168]{3,2,1,0:T(8,128)(2,1)S(1)} %bitcast.94, bf16[4,2,32,7168]{3,2,1,0:T(8,128)(2,1)} %collective-permute-done), kind=kLoop, calls=%fused_computation.5 | loop fusion | flops 5505024 | bytes 14680064 | tf_op jit(solution)/shard_map/add | solution.py:182
  140.6 3.0 %copy-done = f32[4,2,32,7168]{3,2,1,0:T(8,128)} copy-done((f32[4,2,32,7168]{3,2,1,0:T(8,128)}, f32[4,2,32,7168]{3,2,1,0:T(8,128)S(1)}, u32[]{:S(2)}) %copy-start) | copy-done | bytes 7340056
  143.5 1.6 fusion.3
  145.1 1.5 collective-permute-start.1
  146.6 5.3 %collective-permute-start.3 = (bf16[2,32,7168]{2,1,0:T(8,128)(2,1)}, bf16[2,32,7168]{2,1,0:T(8,128)(2,1)}, u32[]{:S(2)}, u32[]{:S(2)}) collective-permute-start(bf16[2,32,7168]{2,1,0:T(8,128)(2,1)} %get-tuple-element.35), channel_id=1, source_target_pairs={{0,12},{4,0},{8,4},{12,8},{1,13},{5,1},{9,5},{13,9},{2,14},{6,2},{... | collective-permute-start | bytes 2752520 | tf_op jit(solution)/shard_map/ppermute | solution.py:164
  151.9 1.5 collective-permute-start.2
  153.3 33.7 %all-to-all-start = ((bf16[16,2,4,2,16,256]{5,4,3,2,1,0:T(8,128)(2,1)}), bf16[16,2,4,2,16,256]{5,4,3,2,1,0:T(8,128)(2,1)S(1)}, u32[]{:S(2)}, u32[]{:S(2)}) async-start(bf16[16,2,4,2,16,256]{5,4,3,2,1,0:T(8,128)(2,1)} %fusion), calls=%async_computation | async-start | bytes 4194304 | tf_op jit(solution)/shard_map/all_to_all | solution.py:42
  187.0 0.4 fusion.11
  187.4 0.1 select_reduce_fusion
  187.5 0.1 reduce_sum.33
  187.6 4.2 %collective-permute-done.3 = bf16[2,32,7168]{2,1,0:T(8,128)(2,1)} collective-permute-done((bf16[2,32,7168]{2,1,0:T(8,128)(2,1)}, bf16[2,32,7168]{2,1,0:T(8,128)(2,1)}, u32[]{:S(2)}, u32[]{:S(2)}) %collective-permute-start.3) | collective-permute-done | bytes 917536 | tf_op jit(solution)/shard_map/ppermute | solution.py:164
  191.8 1.9 collective-permute-done.2
  193.7 2.7 %fusion.2 = f32[2,32,7168]{2,1,0:T(8,128)S(1)} fusion(bf16[2,32,7168]{2,1,0:T(8,128)(2,1)} %collective-permute-done.3, bf16[2,32,7168]{2,1,0:T(8,128)(2,1)} %collective-permute-done.2, bf16[2,32,7168]{2,1,0:T(8,128)(2,1)} %collective-permute-done.1, f32[4,2,32,7168]{3,2,1,0:T(8,128)} %copy-done, s32[]{:T(128)S(6)} %select_n.187), kind=kLoop, calls=%fused_computation.11 | loop fusion | flops 2752512 | bytes 6422532 | tf_op jit(solution)/shard_map/add | solution.py:164
  196.4 0.9 fusion.7
  197.3 11.0 %collective-permute-start.4 = (bf16[32,7168]{1,0:T(8,128)(2,1)}, bf16[32,7168]{1,0:T(8,128)(2,1)}, u32[]{:S(2)}, u32[]{:S(2)}) collective-permute-start(bf16[32,7168]{1,0:T(8,128)(2,1)} %fusion.7), channel_id=1, source_target_pairs={{0,2},{2,0},{1,3},{3,1},{4,6},{6,4},{5,7},{7,5},{8,10},{10,8},{9,1... | collective-permute-start | bytes 1376264 | tf_op jit(solution)/shard_map/ppermute | solution.py:164
  208.4 0.1 select_reduce_fusion.1
  208.5 30.5 %all-to-all-done = bf16[16,2,4,2,16,256]{5,4,3,2,1,0:T(8,128)(2,1)S(1)} async-done(((bf16[16,2,4,2,16,256]{5,4,3,2,1,0:T(8,128)(2,1)}), bf16[16,2,4,2,16,256]{5,4,3,2,1,0:T(8,128)(2,1)S(1)}, u32[]{:S(2)}, u32[]{:S(2)}) %all-to-all-start) | async-done | bytes 2097184 | tf_op jit(solution)/shard_map/all_to_all | solution.py:42
  239.0 0.7 gather_fusion.1
  239.6 1.1 copy.45
  240.7 0.7 gather_fusion.2
  241.4 1.1 copy.46
  242.4 0.8 copy-done.2
  243.2 1.9 fusion.6
  (19 shorter events, 0.1 us)
Async XLA Ops:
  7.2 7.9 %copy-start.3 = (bf16[4,512,256]{2,1,0:T(8,128)(2,1)S(1)}, bf16[4,512,256]{2,1,0:T(8,128)(2,1)}, u32[]{:S(2)}) copy-start(bf16[4,512,256]{2,1,0:T(8,128)(2,1)} %param.16) | copy-start | bytes 3145732
  7.2 7.9 %copy-start.4 = (bf16[4,512,256]{2,1,0:T(8,128)(2,1)S(1)}, bf16[4,512,256]{2,1,0:T(8,128)(2,1)}, u32[]{:S(2)}) copy-start(bf16[4,512,256]{2,1,0:T(8,128)(2,1)} %param.15) | copy-start | bytes 3145732
  7.2 109.8 %all-gather.3.cloned.1.call-start = ((), (), s32[]{:S(2)}) async-start(), calls=%async_computation.1 | async-start | bytes 8912896 | tf_op jit(solution)/shard_map/all_gather | solution.py:133
  130.5 6.8 %collective-permute-start = (bf16[4,2,32,7168]{3,2,1,0:T(8,128)(2,1)}, bf16[4,2,32,7168]{3,2,1,0:T(8,128)(2,1)}, u32[]{:S(2)}, u32[]{:S(2)}) collective-permute-start(bf16[4,2,32,7168]{3,2,1,0:T(8,128)(2,1)} %bitcast.21), channel_id=1, source_target_pairs={{0,1},{1,0},{2,3},{3,2},{4,5},{5,4},{6,7},{7,6},{8,9},{9,8},{10,11... | collective-permute-start | bytes 11010056 | tf_op jit(solution)/shard_map/ppermute | solution.py:182
  140.5 3.0 %copy-start = (f32[4,2,32,7168]{3,2,1,0:T(8,128)}, f32[4,2,32,7168]{3,2,1,0:T(8,128)S(1)}, u32[]{:S(2)}) copy-start(f32[4,2,32,7168]{3,2,1,0:T(8,128)S(1)} %convert_add_fusion) | copy-start | bytes 22020100
  145.1 42.5 %collective-permute-start.1 = (bf16[2,32,7168]{2,1,0:T(8,128)(2,1)}, bf16[2,32,7168]{2,1,0:T(8,128)(2,1)}, u32[]{:S(2)}, u32[]{:S(2)}) collective-permute-start(bf16[2,32,7168]{2,1,0:T(8,128)(2,1)} %get-tuple-element.34), channel_id=1, source_target_pairs={{0,4},{4,8},{8,12},{12,0},{1,5},{5,9},{9,13},{13,1},{2,6},{6,10},{... | collective-permute-start | bytes 2752520 | tf_op jit(solution)/shard_map/ppermute | solution.py:164
  146.6 45.2 %collective-permute-start.3 = (bf16[2,32,7168]{2,1,0:T(8,128)(2,1)}, bf16[2,32,7168]{2,1,0:T(8,128)(2,1)}, u32[]{:S(2)}, u32[]{:S(2)}) collective-permute-start(bf16[2,32,7168]{2,1,0:T(8,128)(2,1)} %get-tuple-element.35), channel_id=1, source_target_pairs={{0,12},{4,0},{8,4},{12,8},{1,13},{5,1},{9,5},{13,9},{2,14},{6,2},{... | collective-permute-start | bytes 2752520 | tf_op jit(solution)/shard_map/ppermute | solution.py:164
  151.9 41.8 %collective-permute-start.2 = (bf16[2,32,7168]{2,1,0:T(8,128)(2,1)S(1)}, bf16[2,32,7168]{2,1,0:T(8,128)(2,1)}, u32[]{:S(2)}, u32[]{:S(2)}) collective-permute-start(bf16[2,32,7168]{2,1,0:T(8,128)(2,1)S(1)} %get-tuple-element.36), channel_id=1, source_target_pairs={{0,8},{4,12},{8,0},{12,4},{1,9},{5,13},{9,1},{13,5},{2,10},{6,14},... | collective-permute-start | bytes 2752520 | tf_op jit(solution)/shard_map/ppermute | solution.py:164
  153.3 85.6 %all-to-all-start = ((bf16[16,2,4,2,16,256]{5,4,3,2,1,0:T(8,128)(2,1)}), bf16[16,2,4,2,16,256]{5,4,3,2,1,0:T(8,128)(2,1)S(1)}, u32[]{:S(2)}, u32[]{:S(2)}) async-start(bf16[16,2,4,2,16,256]{5,4,3,2,1,0:T(8,128)(2,1)} %fusion), calls=%async_computation | async-start | bytes 4194304 | tf_op jit(solution)/shard_map/all_to_all | solution.py:42
  196.4 12.1 %copy-start.1 = (f32[2,32,7168]{2,1,0:T(8,128)}, f32[2,32,7168]{2,1,0:T(8,128)S(1)}, u32[]{:S(2)}) copy-start(f32[2,32,7168]{2,1,0:T(8,128)S(1)} %fusion.2) | copy-start | bytes 5505028
  197.3 45.1 %collective-permute-start.4 = (bf16[32,7168]{1,0:T(8,128)(2,1)}, bf16[32,7168]{1,0:T(8,128)(2,1)}, u32[]{:S(2)}, u32[]{:S(2)}) collective-permute-start(bf16[32,7168]{1,0:T(8,128)(2,1)} %fusion.7), channel_id=1, source_target_pairs={{0,2},{2,0},{1,3},{3,1},{4,6},{6,4},{5,7},{7,5},{8,10},{10,8},{9,1... | collective-permute-start | bytes 1376264 | tf_op jit(solution)/shard_map/ppermute | solution.py:164
  241.4 1.9 copy-start.2
Sparse Core Ops, SparseCore 0:
  11.0 105.9 all-gather.2

commit v12 on v10

--- a/solution.py
+++ b/solution.py
@@ -38,8 +38,7 @@
     return (outgoing, inverse)
 
 
-def place_pages(outgoing, inverse):
-    moved = lax.all_to_all(outgoing, SEQ, split_axis=0, concat_axis=0, tiled=True)
+def place_pages(moved, inverse):
     _, kinds, layers, per_group, page_len, feat_width = moved.shape
     moved = moved.transpose(1, 2, 0, 3, 4, 5).reshape(kinds, layers, -1, page_len, feat_width)
     placed = jnp.take(moved, inverse, axis=2)
@@ -149,8 +148,9 @@
 ):
     moved, inverse = relayout(cache_keys, cache_values, page_table)
     attended, moved = attention(queries, stretch_keys, stretch_values, segment_ids, block_live, moved)
+    moved = lax.all_to_all(moved, SEQ, split_axis=0, concat_axis=0, tiled=True)
+    projected, moved = reduce_rows(attended, out_weight, moved)
     decode_keys, decode_values = place_pages(moved, inverse)
-    projected = reduce_rows(attended, out_weight)
     return (attended, projected, decode_keys, decode_values)
 
 
@@ -166,7 +166,7 @@
     return total
 
 
-def reduce_rows(attended, out_weight):
+def reduce_rows(attended, out_weight, moved):
     x_size, zl_size, c_size = [lax.axis_size(name) for name in HEAD]
     rows, width = attended.shape
     share = rows // (x_size * zl_size * c_size)
@@ -184,8 +184,9 @@
         else:
             total = piece.astype(jnp.float32)
     total = exchange(total.reshape(x_size, zl_size, share, columns), "x")
+    total, moved = lax.optimization_barrier((total, moved))
     total = exchange(total.reshape(zl_size, share, columns), "zl")
-    return total.astype(jnp.bfloat16)
+    return (total.astype(jnp.bfloat16), moved)
 
 
 def solution(mesh):

time: 251 us -> 250 us (level)
    all_to_all x1, waiting for transfers between devices: 36.3 us -> 0.01 us  [local(): moved = lax.all_to_all(moved, SEQ, split_axis=0, concat_axis=0, tiled=True)]
    ppermute x4, waiting for transfers between devices: 8.94 us -> 45.1 us  [exchange(): total = total + lax.ppermute(sent, name, pairs).astype(jnp.float32)]
    unnamed x8 -> x10, local copies, waits for them, and re-layouts: 5.1 us -> 5.09 us
  transfers between devices with their start and end apart: 7 -> 7, of which waited for: 3 -> 4; matrix products, arithmetic and copies ran while one was open for 11% -> 12% of each run, Pallas kernels for 0% -> 0%
where the time goes in v12:
time: 250 us
  waiting for transfers between devices  142 us (57%)
  starting transfers between devices  42.9 us (17%)
  local copies, waits for them, and re-layouts  20.2 us (8%)
  other arithmetic  15.6 us (6%)
  between operations  14.3 us (6%)
  matrix products  8.12 us (3%)
  Pallas kernels  7.49 us (3%)
    all_gather x1, waiting for transfers between devices, attention(): kv_all = lax.all_gather(kv, SEQ, axis=0, tiled=False)  96.5 us
    ppermute x4, waiting for transfers between devices, exchange(): total = total + lax.ppermute(sent, name, pairs).astype(jnp.float32)  45.1 us
    all_to_all x1, starting transfers between devices, local(): moved = lax.all_to_all(moved, SEQ, split_axis=0, concat_axis=0, tiled=True)  37 us
    dot_general x2, matrix products, reduce_rows(): jnp.dot(rows_for.reshape(-1, width), out_weight, preferred_element_type=j...  8.12 us
    pallas_call x1, Pallas kernels, attend(): pl.pallas_call(kernel, grid_spec=pltpu.PrefetchScalarGridSpec(num_scalar_...  7.49 us
    ppermute x4, starting transfers between devices, exchange(): total = total + lax.ppermute(sent, name, pairs).astype(jnp.float32)  5.93 us
    unnamed x10, local copies, waits for them, and re-layouts  5.09 us
  transfers between devices with their start and end apart: 7, of which 4 were waited for; matrix products, arithmetic and copies ran while one was open for 12% of the time, Pallas kernels for 0%

profile of v12, /device:TPU:8, one launch (start us, length us, event | category | flops | bytes accessed | tf_op | source)
XLA Modules:
  0.0 250.4 jit_solution(11235054448573271068)
XLA Ops:
  7.2 0.0 all-gather.3.cloned.1.call-start
  7.2 2.0 pad_maximum_fusion.1
  9.2 0.0 all-gather.3.cloned.1.call-update
  9.3 0.8 reshape.123
  10.1 0.8 reshape.124
  10.9 0.1 copy.40
  11.0 0.1 select_reduce_fusion.2
  11.1 0.1 iota_add_fusion
  11.2 0.1 add.133
  11.3 0.4 fusion.10
  11.7 0.1 select_reduce_fusion
  11.8 0.1 reduce_sum.31
  11.9 0.1 select_reduce_fusion.1
  12.0 1.5 pad_maximum_fusion
  13.6 2.3 gather_fusion
  15.9 0.3 select_bitcast_fusion.1
  16.2 0.2 copy.41
  16.4 0.9 copy.42.qseg_ref
  17.2 0.6 fusion.16
  17.8 1.4 fusion.11
  19.2 0.7 and_select_fusion.2
  19.9 0.6 pad_add_fusion.meta_ref
  20.5 96.5 %all-gather.3.cloned.1.call-done = bf16[32,512,256]{2,1,0:T(8,128)(2,1)} async-done(((bf16[2,512,256]{2,1,0:T(8,128)(2,1)}), bf16[32,512,256]{2,1,0:T(8,128)(2,1)}) %all-gather.3.cloned.1.call-update) | async-done | bytes 8388624 | tf_op jit(solution)/shard_map/all_gather | solution.py:133
  117.0 7.5 %shard_map.120 = bf16[512,256]{1,0:T(8,128)(2,1)} custom-call(s32[17]{0:T(128)} %pad_add_fusion.meta_ref, bf16[512,256]{1,0:T(8,128)(2,1)} %q_ref.1, s32[512,1]{1,0:T(8,128)} %copy.42.qseg_ref, s32[16,1,512]{2,1,0:T(1,128)} %bitcast.80, bf16[16,2,512,256]{3,2,1,0:T(8,128)(2,1)} %bitcast.67, bf16[16,2,512,256]{3,2,1,0:T(8,128)(2,1)} %bitcast.68), custom_call_target="tpu_custom_call" | custom-call | tf_op jit(solution)/shard_map/pallas_call | solution.py:99
  124.5 1.0 constant_dynamic-slice_fusion.1
  125.5 5.0 %convolution_convert_fusion = bf16[256,7168]{1,0:T(8,128)(2,1)} fusion(bf16[256,256]{1,0:T(8,128)(2,1)S(1)} %bitcast.77, bf16[256,7168]{1,0:T(8,128)(2,1)} %param.16), kind=kOutput, calls=%fused_computation.2 | convolution fusion | flops 941359104 | bytes 7471104 | tf_op jit(solution)/shard_map/dot_general | solution.py:179
  130.5 1.6 copy.43
  132.1 37.0 %all-to-all-start = ((bf16[16,2,4,2,16,256]{5,4,3,2,1,0:T(8,128)(2,1)}), bf16[16,2,4,2,16,256]{5,4,3,2,1,0:T(8,128)(2,1)S(1)}, u32[]{:S(2)}, u32[]{:S(2)}) async-start(bf16[16,2,4,2,16,256]{5,4,3,2,1,0:T(8,128)(2,1)} %copy.43), calls=%async_computation | async-start | bytes 4194304 | tf_op jit(solution)/shard_map/all_to_all | solution.py:151
  169.0 3.2 %convolution_convert_fusion.1 = bf16[256,7168]{1,0:T(8,128)(2,1)S(1)} fusion(bf16[256,256]{1,0:T(8,128)(2,1)S(1)} %bitcast.76, bf16[256,7168]{1,0:T(8,128)(2,1)} %param.16), kind=kOutput, calls=%fused_computation.3 | convolution fusion | flops 941359104 | bytes 7471104 | tf_op jit(solution)/shard_map/dot_general | solution.py:179
  172.2 3.3 %convert_add_fusion = f32[4,2,32,7168]{3,2,1,0:T(8,128)S(1)} fusion(bf16[4,2,32,7168]{3,2,1,0:T(8,128)(2,1)S(1)} %bitcast.69, bf16[4,2,32,7168]{3,2,1,0:T(8,128)(2,1)} %collective-permute-done), kind=kLoop, calls=%fused_computation.4 | loop fusion | flops 5505024 | bytes 14680064 | tf_op jit(solution)/shard_map/add | solution.py:183
  175.5 2.9 %copy-done = f32[4,2,32,7168]{3,2,1,0:T(8,128)} copy-done((f32[4,2,32,7168]{3,2,1,0:T(8,128)}, f32[4,2,32,7168]{3,2,1,0:T(8,128)S(1)}, u32[]{:S(2)}) %copy-start) | copy-done | bytes 7340056
  178.4 1.6 fusion.2
  180.0 1.5 collective-permute-start.1
  181.5 2.6 %collective-permute-start.2 = (bf16[2,32,7168]{2,1,0:T(8,128)(2,1)}, bf16[2,32,7168]{2,1,0:T(8,128)(2,1)}, u32[]{:S(2)}, u32[]{:S(2)}) collective-permute-start(bf16[2,32,7168]{2,1,0:T(8,128)(2,1)} %get-tuple-element.41), channel_id=1, source_target_pairs={{0,8},{4,12},{8,0},{12,4},{1,9},{5,13},{9,1},{13,5},{2,10},{6,14},... | collective-permute-start | bytes 2752520 | tf_op jit(solution)/shard_map/ppermute | solution.py:165
  184.2 1.6 collective-permute-start.3
  185.7 18.1 %collective-permute-done.1 = bf16[2,32,7168]{2,1,0:T(8,128)(2,1)} collective-permute-done((bf16[2,32,7168]{2,1,0:T(8,128)(2,1)}, bf16[2,32,7168]{2,1,0:T(8,128)(2,1)}, u32[]{:S(2)}, u32[]{:S(2)}) %collective-permute-start.1) | collective-permute-done | bytes 917536 | tf_op jit(solution)/shard_map/ppermute | solution.py:165
  203.9 20.5 %collective-permute-done.2 = bf16[2,32,7168]{2,1,0:T(8,128)(2,1)} collective-permute-done((bf16[2,32,7168]{2,1,0:T(8,128)(2,1)}, bf16[2,32,7168]{2,1,0:T(8,128)(2,1)}, u32[]{:S(2)}, u32[]{:S(2)}) %collective-permute-start.2) | collective-permute-done | bytes 917536 | tf_op jit(solution)/shard_map/ppermute | solution.py:165
  224.3 3.9 %fusion.1 = f32[2,32,7168]{2,1,0:T(8,128)} fusion(bf16[2,32,7168]{2,1,0:T(8,128)(2,1)} %collective-permute-done.3, bf16[2,32,7168]{2,1,0:T(8,128)(2,1)} %collective-permute-done.2, bf16[2,32,7168]{2,1,0:T(8,128)(2,1)} %collective-permute-done.1, f32[4,2,32,7168]{3,2,1,0:T(8,128)} %copy-done, s32[]{:T(128)S(6)} %select_n.123), kind=kLoop, calls=%fused_computation.10 | loop fusion | flops 2752512 | bytes 6422532 | tf_op jit(solution)/shard_map/add | solution.py:165
  228.3 1.6 copy.44
  229.9 1.2 fusion.6
  231.1 0.2 collective-permute-start.4
  231.3 2.3 gather_fusion.1
  233.6 0.3 select_bitcast_fusion
  233.9 0.1 slice_bitcast_fusion
  234.0 1.1 copy.45
  235.1 1.1 copy.46
  236.2 6.5 %collective-permute-done.4 = bf16[32,7168]{1,0:T(8,128)(2,1)S(1)} collective-permute-done((bf16[32,7168]{1,0:T(8,128)(2,1)S(1)}, bf16[32,7168]{1,0:T(8,128)(2,1)S(1)}, u32[]{:S(2)}, u32[]{:S(2)}) %collective-permute-start.4) | collective-permute-done | bytes 458784 | tf_op jit(solution)/shard_map/ppermute | solution.py:165
  242.7 0.8 fusion.5
  (20 shorter events, 0.1 us)
Async XLA Ops:
  7.2 4.9 %copy-start.3 = (bf16[4,512,256]{2,1,0:T(8,128)(2,1)S(1)}, bf16[4,512,256]{2,1,0:T(8,128)(2,1)}, u32[]{:S(2)}) copy-start(bf16[4,512,256]{2,1,0:T(8,128)(2,1)} %param.17) | copy-start | bytes 3145732
  7.2 4.9 %copy-start.2 = (bf16[4,512,256]{2,1,0:T(8,128)(2,1)S(1)}, bf16[4,512,256]{2,1,0:T(8,128)(2,1)}, u32[]{:S(2)}) copy-start(bf16[4,512,256]{2,1,0:T(8,128)(2,1)} %param.18) | copy-start | bytes 3145732
  7.2 109.8 %all-gather.3.cloned.1.call-start = ((), (), s32[]{:S(2)}) async-start(), calls=%async_computation.1 | async-start | bytes 8912896 | tf_op jit(solution)/shard_map/all_gather | solution.py:133
  130.4 41.8 %collective-permute-start = (bf16[4,2,32,7168]{3,2,1,0:T(8,128)(2,1)}, bf16[4,2,32,7168]{3,2,1,0:T(8,128)(2,1)}, u32[]{:S(2)}, u32[]{:S(2)}) collective-permute-start(bf16[4,2,32,7168]{3,2,1,0:T(8,128)(2,1)} %bitcast.20), channel_id=1, source_target_pairs={{0,1},{1,0},{2,3},{3,2},{4,5},{5,4},{6,7},{7,6},{8,9},{9,8},{10,11... | collective-permute-start | bytes 11010056 | tf_op jit(solution)/shard_map/ppermute | solution.py:183
  132.1 96.2 %all-to-all-start = ((bf16[16,2,4,2,16,256]{5,4,3,2,1,0:T(8,128)(2,1)}), bf16[16,2,4,2,16,256]{5,4,3,2,1,0:T(8,128)(2,1)S(1)}, u32[]{:S(2)}, u32[]{:S(2)}) async-start(bf16[16,2,4,2,16,256]{5,4,3,2,1,0:T(8,128)(2,1)} %copy.43), calls=%async_computation | async-start | bytes 4194304 | tf_op jit(solution)/shard_map/all_to_all | solution.py:151
  175.5 3.0 %copy-start = (f32[4,2,32,7168]{3,2,1,0:T(8,128)}, f32[4,2,32,7168]{3,2,1,0:T(8,128)S(1)}, u32[]{:S(2)}) copy-start(f32[4,2,32,7168]{3,2,1,0:T(8,128)S(1)} %convert_add_fusion) | copy-start | bytes 22020100
  180.0 23.8 %collective-permute-start.1 = (bf16[2,32,7168]{2,1,0:T(8,128)(2,1)}, bf16[2,32,7168]{2,1,0:T(8,128)(2,1)}, u32[]{:S(2)}, u32[]{:S(2)}) collective-permute-start(bf16[2,32,7168]{2,1,0:T(8,128)(2,1)} %get-tuple-element.39), channel_id=1, source_target_pairs={{0,4},{4,8},{8,12},{12,0},{1,5},{5,9},{9,13},{13,1},{2,6},{6,10},{... | collective-permute-start | bytes 2752520 | tf_op jit(solution)/shard_map/ppermute | solution.py:165
  181.5 42.8 %collective-permute-start.2 = (bf16[2,32,7168]{2,1,0:T(8,128)(2,1)}, bf16[2,32,7168]{2,1,0:T(8,128)(2,1)}, u32[]{:S(2)}, u32[]{:S(2)}) collective-permute-start(bf16[2,32,7168]{2,1,0:T(8,128)(2,1)} %get-tuple-element.41), channel_id=1, source_target_pairs={{0,8},{4,12},{8,0},{12,4},{1,9},{5,13},{9,1},{13,5},{2,10},{6,14},... | collective-permute-start | bytes 2752520 | tf_op jit(solution)/shard_map/ppermute | solution.py:165
  184.2 40.2 %collective-permute-start.3 = (bf16[2,32,7168]{2,1,0:T(8,128)(2,1)S(1)}, bf16[2,32,7168]{2,1,0:T(8,128)(2,1)}, u32[]{:S(2)}, u32[]{:S(2)}) collective-permute-start(bf16[2,32,7168]{2,1,0:T(8,128)(2,1)S(1)} %get-tuple-element.40), channel_id=1, source_target_pairs={{0,12},{4,0},{8,4},{12,8},{1,13},{5,1},{9,5},{13,9},{2,14},{6,2},{... | collective-permute-start | bytes 2752520 | tf_op jit(solution)/shard_map/ppermute | solution.py:165
  231.1 11.6 %collective-permute-start.4 = (bf16[32,7168]{1,0:T(8,128)(2,1)S(1)}, bf16[32,7168]{1,0:T(8,128)(2,1)S(1)}, u32[]{:S(2)}, u32[]{:S(2)}) collective-permute-start(bf16[32,7168]{1,0:T(8,128)(2,1)S(1)} %fusion.6), channel_id=1, source_target_pairs={{0,2},{2,0},{1,3},{3,1},{4,6},{6,4},{5,7},{7,5},{8,10},{10,8},{9,1... | collective-permute-start | bytes 1376264 | tf_op jit(solution)/shard_map/ppermute | solution.py:165
  234.0 8.7 %copy-start.1 = (f32[2,32,7168]{2,1,0:T(8,128)S(1)}, f32[2,32,7168]{2,1,0:T(8,128)}, u32[]{:S(2)}) copy-start(f32[2,32,7168]{2,1,0:T(8,128)} %fusion.1) | copy-start | bytes 5505028
Sparse Core Ops, SparseCore 0:
  11.0 105.9 all-gather.2

commit v13 on v10

--- a/solution.py
+++ b/solution.py
@@ -39,7 +39,8 @@
 
 
 def place_pages(outgoing, inverse):
-    moved = lax.all_to_all(outgoing, SEQ, split_axis=0, concat_axis=0, tiled=True)
+    moved = lax.all_to_all(outgoing, SEQ[0], split_axis=0, concat_axis=0, tiled=True)
+    moved = moved.reshape(-1, *moved.shape[2:])
     _, kinds, layers, per_group, page_len, feat_width = moved.shape
     moved = moved.transpose(1, 2, 0, 3, 4, 5).reshape(kinds, layers, -1, page_len, feat_width)
     placed = jnp.take(moved, inverse, axis=2)
@@ -132,6 +133,9 @@
     kseg = seg_blocks[:, None, :]
     kv = jnp.stack([stretch_keys, stretch_values])
     kv_all = lax.all_gather(kv, SEQ, axis=0, tiled=False)
+    planes = lax.axis_size(SEQ[0])
+    moved = moved.reshape(planes, -1, *moved.shape[1:])
+    moved = lax.all_to_all(moved, SEQ[1], split_axis=1, concat_axis=1, tiled=True)
     moved, kv_all = lax.optimization_barrier((moved, kv_all))
     return (attend(meta, queries, qseg, kseg, kv_all), moved)
 

time: 251 us -> 255 us (1.016)
  starting transfers between devices: 44.4 us -> 48.1 us
    all_gather x1, waiting for transfers between devices: 96.6 us -> 68.5 us  [attention(): kv_all = lax.all_gather(kv, SEQ, axis=0, tiled=False)]
    all_to_all x1 -> x2, waiting for transfers between devices: 36.3 us -> 60.1 us  [the longest x1 31.9 us: place_pages(): lax.all_to_all(outgoing, SEQ[0], split_axis=0, concat_axis=0, tiled=True)]
    all_to_all x1 -> x2, starting transfers between devices: 38.8 us -> 42.4 us  [the longest x1 36.5 us: place_pages(): lax.all_to_all(outgoing, SEQ[0], split_axis=0, concat_axis=0, tiled=True)]
    ppermute x4, waiting for transfers between devices: 8.94 us -> 12.3 us  [exchange(): total = total + lax.ppermute(sent, name, pairs).astype(jnp.float32)]
  transfers between devices with their start and end apart: 7 -> 8, of which waited for: 3 -> 5; matrix products, arithmetic and copies ran while one was open for 11% -> 12% of each run, Pallas kernels for 0% -> 0%
where the time goes in v13:
time: 255 us; the launch traced here: 253 us
  waiting for transfers between devices  141 us (55%)
  starting transfers between devices  48.1 us (19%)
  local copies, waits for them, and re-layouts  20 us (8%)
  other arithmetic  15.6 us (6%)
  between operations  14.3 us (6%)
  matrix products  8.12 us (3%)
  Pallas kernels  6.08 us (2%)
    all_gather x1, waiting for transfers between devices, attention(): kv_all = lax.all_gather(kv, SEQ, axis=0, tiled=False)  68.5 us
    all_to_all x1, starting transfers between devices, place_pages(): lax.all_to_all(outgoing, SEQ[0], split_axis=0, concat_axis=0, tiled=True)  36.5 us
    all_to_all x1, waiting for transfers between devices, place_pages(): lax.all_to_all(outgoing, SEQ[0], split_axis=0, concat_axis=0, tiled=True)  31.9 us
    all_to_all x1, waiting for transfers between devices, attention(): lax.all_to_all(moved, SEQ[1], split_axis=1, concat_axis=1, tiled=True)  28.3 us
    ppermute x4, waiting for transfers between devices, exchange(): total = total + lax.ppermute(sent, name, pairs).astype(jnp.float32)  12.3 us
    dot_general x2, matrix products, reduce_rows(): jnp.dot(rows_for.reshape(-1, width), out_weight, preferred_element_type=j...  8.12 us
    pallas_call x1, Pallas kernels, attend(): pl.pallas_call(kernel, grid_spec=pltpu.PrefetchScalarGridSpec(num_scalar_...  6.08 us
    all_to_all x1, starting transfers between devices, attention(): lax.all_to_all(moved, SEQ[1], split_axis=1, concat_axis=1, tiled=True)  5.89 us
  transfers between devices with their start and end apart: 8, of which 5 were waited for; matrix products, arithmetic and copies ran while one was open for 12% of the time, Pallas kernels for 0%

profile of v13, /device:TPU:8, one launch (start us, length us, event | category | flops | bytes accessed | tf_op | source)
XLA Modules:
  0.0 253.1 jit_solution(8864022560575822095)
XLA Ops:
  7.2 2.0 pad_maximum_fusion.1
  9.2 0.8 reshape.130
  10.0 0.1 copy.54
  10.1 0.1 select_reduce_fusion.2
  10.3 0.1 iota_add_fusion
  10.3 0.1 add.133
  10.4 0.4 fusion.10
  10.8 0.1 select_reduce_fusion
  10.9 0.1 reduce_sum.31
  11.0 0.1 select_reduce_fusion.1
  11.2 2.8 %pad_maximum_fusion = bf16[2,4,32,16,256]{4,3,2,1,0:T(8,128)(2,1)} fusion(bf16[1,4,32,16,256]{4,3,2,1,0:T(8,128)(2,1)S(1)} %bitcast.78, bf16[1,4,32,16,256]{4,3,2,1,0:T(8,128)(2,1)} %bitcast.79), kind=kLoop, calls=%fused_computation.5 | loop fusion | flops 1048576 | bytes 4194304 | tf_op jit(solution)/shard_map/stack | solution.py:31
  14.0 2.3 gather_fusion
  16.3 0.3 broadcast_select_fusion
  16.5 1.6 copy.57
  18.1 5.9 %all-to-all-start = ((bf16[4,4,2,4,2,16,256]{6,5,4,0,3,2,1:T(8,128)(2,1)}), bf16[4,4,2,4,2,16,256]{6,5,4,0,3,2,1:T(8,128)(2,1)S(1)}, u32[]{:S(2)}, u32[]{:S(2)}) async-start(bf16[4,4,2,4,2,16,256]{6,5,4,0,3,2,1:T(8,128)(2,1)} %copy.57), calls=%async_computation | async-start | bytes 4194304 | tf_op jit(solution)/shard_map/all_to_all | solution.py:138
  24.1 0.9 copy.58.qseg_ref
  24.9 0.6 fusion.16
  25.5 1.4 fusion.11
  26.9 0.7 and_select_fusion.2
  27.6 0.6 pad_add_fusion.meta_ref
  28.2 28.3 %all-to-all-done = bf16[4,4,2,4,2,16,256]{6,5,4,0,3,2,1:T(8,128)(2,1)S(1)} async-done(((bf16[4,4,2,4,2,16,256]{6,5,4,0,3,2,1:T(8,128)(2,1)}), bf16[4,4,2,4,2,16,256]{6,5,4,0,3,2,1:T(8,128)(2,1)S(1)}, u32[]{:S(2)}, u32[]{:S(2)}) %all-to-all-start) | async-done | bytes 2097184 | tf_op jit(solution)/shard_map/all_to_all | solution.py:138
  56.5 68.5 %all-gather.3.cloned.1.call-done = bf16[32,512,256]{2,1,0:T(8,128)(2,1)} async-done(((bf16[2,512,256]{2,1,0:T(8,128)(2,1)}), bf16[32,512,256]{2,1,0:T(8,128)(2,1)}) %all-gather.3.cloned.1.call-update) | async-done | bytes 8388624 | tf_op jit(solution)/shard_map/all_gather | solution.py:135
  125.0 6.1 %shard_map.120 = bf16[512,256]{1,0:T(8,128)(2,1)} custom-call(s32[17]{0:T(128)} %pad_add_fusion.meta_ref, bf16[512,256]{1,0:T(8,128)(2,1)} %q_ref.1, s32[512,1]{1,0:T(8,128)} %copy.58.qseg_ref, s32[16,1,512]{2,1,0:T(1,128)} %bitcast.84, bf16[16,2,512,256]{3,2,1,0:T(8,128)(2,1)} %bitcast.71, bf16[16,2,512,256]{3,2,1,0:T(8,128)(2,1)} %bitcast.72), custom_call_target="tpu_custom_call" | custom-call | tf_op jit(solution)/shard_map/pallas_call | solution.py:101
  131.1 1.0 constant_dynamic-slice_fusion.1
  132.1 5.0 %convolution_convert_fusion = bf16[256,7168]{1,0:T(8,128)(2,1)} fusion(bf16[256,256]{1,0:T(8,128)(2,1)S(1)} %bitcast.81, bf16[256,7168]{1,0:T(8,128)(2,1)} %param.16), kind=kOutput, calls=%fused_computation.2 | convolution fusion | flops 941359104 | bytes 7471104 | tf_op jit(solution)/shard_map/dot_general | solution.py:183
  137.0 1.6 copy.59
  138.7 36.5 %all-to-all-start.1 = ((bf16[4,4,2,4,2,16,256]{6,5,4,1,3,2,0:T(8,128)(2,1)}), bf16[4,4,2,4,2,16,256]{6,5,4,1,3,2,0:T(8,128)(2,1)S(1)}, u32[]{:S(2)}, u32[]{:S(2)}) async-start(bf16[4,4,2,4,2,16,256]{6,5,4,1,3,2,0:T(8,128)(2,1)} %copy.59), calls=%async_computation.1 | async-start | bytes 4194304 | tf_op jit(solution)/shard_map/all_to_all | solution.py:42
  175.2 3.2 %convolution_convert_fusion.1 = bf16[256,7168]{1,0:T(8,128)(2,1)S(1)} fusion(bf16[256,256]{1,0:T(8,128)(2,1)S(1)} %bitcast.80, bf16[256,7168]{1,0:T(8,128)(2,1)} %param.16), kind=kOutput, calls=%fused_computation.3 | convolution fusion | flops 941359104 | bytes 7471104 | tf_op jit(solution)/shard_map/dot_general | solution.py:183
  178.3 3.3 %convert_add_fusion = f32[4,2,32,7168]{3,2,1,0:T(8,128)S(1)} fusion(bf16[4,2,32,7168]{3,2,1,0:T(8,128)(2,1)S(1)} %bitcast.73, bf16[4,2,32,7168]{3,2,1,0:T(8,128)(2,1)} %collective-permute-done), kind=kLoop, calls=%fused_computation.4 | loop fusion | flops 5505024 | bytes 14680064 | tf_op jit(solution)/shard_map/add | solution.py:187
  181.6 2.9 %copy-done = f32[4,2,32,7168]{3,2,1,0:T(8,128)} copy-done((f32[4,2,32,7168]{3,2,1,0:T(8,128)}, f32[4,2,32,7168]{3,2,1,0:T(8,128)S(1)}, u32[]{:S(2)}) %copy-start) | copy-done | bytes 7340056
  184.6 1.6 fusion.2
  186.1 1.5 collective-permute-start.1
  187.6 2.7 %collective-permute-start.2 = (bf16[2,32,7168]{2,1,0:T(8,128)(2,1)}, bf16[2,32,7168]{2,1,0:T(8,128)(2,1)}, u32[]{:S(2)}, u32[]{:S(2)}) collective-permute-start(bf16[2,32,7168]{2,1,0:T(8,128)(2,1)} %get-tuple-element.41), channel_id=1, source_target_pairs={{0,8},{4,12},{8,0},{12,4},{1,9},{5,13},{9,1},{13,5},{2,10},{6,14},... | collective-permute-start | bytes 2752520 | tf_op jit(solution)/shard_map/ppermute | solution.py:169
  190.3 1.4 collective-permute-start.3
  191.8 31.9 %all-to-all-done.1 = bf16[4,4,2,4,2,16,256]{6,5,4,1,3,2,0:T(8,128)(2,1)S(1)} async-done(((bf16[4,4,2,4,2,16,256]{6,5,4,1,3,2,0:T(8,128)(2,1)}), bf16[4,4,2,4,2,16,256]{6,5,4,1,3,2,0:T(8,128)(2,1)S(1)}, u32[]{:S(2)}, u32[]{:S(2)}) %all-to-all-start.1) | async-done | bytes 2097184 | tf_op jit(solution)/shard_map/all_to_all | solution.py:42
  223.6 0.2 copy.60
  223.8 1.6 copy.61
  225.4 2.3 gather_fusion.1
  227.7 3.1 %collective-permute-done.2 = bf16[2,32,7168]{2,1,0:T(8,128)(2,1)} collective-permute-done((bf16[2,32,7168]{2,1,0:T(8,128)(2,1)}, bf16[2,32,7168]{2,1,0:T(8,128)(2,1)}, u32[]{:S(2)}, u32[]{:S(2)}) %collective-permute-start.2) | collective-permute-done | bytes 917536 | tf_op jit(solution)/shard_map/ppermute | solution.py:169
  230.8 2.7 %fusion.1 = f32[2,32,7168]{2,1,0:T(8,128)S(1)} fusion(bf16[2,32,7168]{2,1,0:T(8,128)(2,1)} %collective-permute-done.3, bf16[2,32,7168]{2,1,0:T(8,128)(2,1)} %collective-permute-done.2, bf16[2,32,7168]{2,1,0:T(8,128)(2,1)} %collective-permute-done.1, f32[4,2,32,7168]{3,2,1,0:T(8,128)} %copy-done, s32[]{:T(128)S(6)} %select_n.123), kind=kLoop, calls=%fused_computation.10 | loop fusion | flops 2752512 | bytes 6422532 | tf_op jit(solution)/shard_map/add | solution.py:169
  233.5 0.1 fusion.6
  233.5 0.1 collective-permute-start.4
  233.6 0.3 select_bitcast_fusion
  233.9 0.1 slice_bitcast_fusion
  234.1 1.1 copy.62
  235.1 1.1 copy.63
  236.2 9.3 %collective-permute-done.4 = bf16[32,7168]{1,0:T(8,128)(2,1)S(1)} collective-permute-done((bf16[32,7168]{1,0:T(8,128)(2,1)S(1)}, bf16[32,7168]{1,0:T(8,128)(2,1)S(1)}, u32[]{:S(2)}, u32[]{:S(2)}) %collective-permute-start.4) | collective-permute-done | bytes 458784 | tf_op jit(solution)/shard_map/ppermute | solution.py:169
  245.5 0.8 fusion.5
  (21 shorter events, 0.2 us)
Async XLA Ops:
  7.2 4.0 %copy-start.1 = (bf16[4,512,256]{2,1,0:T(8,128)(2,1)S(1)}, bf16[4,512,256]{2,1,0:T(8,128)(2,1)}, u32[]{:S(2)}) copy-start(bf16[4,512,256]{2,1,0:T(8,128)(2,1)} %param.18) | copy-start | bytes 3145732
  7.2 117.8 %all-gather.3.cloned.1.call-start = ((), (), s32[]{:S(2)}) async-start(), calls=%async_computation.2 | async-start | bytes 8912896 | tf_op jit(solution)/shard_map/all_gather | solution.py:135
  18.1 5.9 %copy-start.2 = (s32[8192]{0:T(1024)S(1)}, s32[8192]{0:T(1024)}, u32[]{:S(2)}) copy-start(s32[8192]{0:T(1024)} %param.14) | copy-start | bytes 98308
  18.1 38.3 %all-to-all-start = ((bf16[4,4,2,4,2,16,256]{6,5,4,0,3,2,1:T(8,128)(2,1)}), bf16[4,4,2,4,2,16,256]{6,5,4,0,3,2,1:T(8,128)(2,1)S(1)}, u32[]{:S(2)}, u32[]{:S(2)}) async-start(bf16[4,4,2,4,2,16,256]{6,5,4,0,3,2,1:T(8,128)(2,1)} %copy.57), calls=%async_computation | async-start | bytes 4194304 | tf_op jit(solution)/shard_map/all_to_all | solution.py:138
  137.0 41.3 %collective-permute-start = (bf16[4,2,32,7168]{3,2,1,0:T(8,128)(2,1)}, bf16[4,2,32,7168]{3,2,1,0:T(8,128)(2,1)}, u32[]{:S(2)}, u32[]{:S(2)}) collective-permute-start(bf16[4,2,32,7168]{3,2,1,0:T(8,128)(2,1)} %bitcast.22), channel_id=1, source_target_pairs={{0,1},{1,0},{2,3},{3,2},{4,5},{5,4},{6,7},{7,6},{8,9},{9,8},{10,11... | collective-permute-start | bytes 11010056 | tf_op jit(solution)/shard_map/ppermute | solution.py:187
  138.7 85.0 %all-to-all-start.1 = ((bf16[4,4,2,4,2,16,256]{6,5,4,1,3,2,0:T(8,128)(2,1)}), bf16[4,4,2,4,2,16,256]{6,5,4,1,3,2,0:T(8,128)(2,1)S(1)}, u32[]{:S(2)}, u32[]{:S(2)}) async-start(bf16[4,4,2,4,2,16,256]{6,5,4,1,3,2,0:T(8,128)(2,1)} %copy.59), calls=%async_computation.1 | async-start | bytes 4194304 | tf_op jit(solution)/shard_map/all_to_all | solution.py:42
  181.6 2.9 %copy-start = (f32[4,2,32,7168]{3,2,1,0:T(8,128)}, f32[4,2,32,7168]{3,2,1,0:T(8,128)S(1)}, u32[]{:S(2)}) copy-start(f32[4,2,32,7168]{3,2,1,0:T(8,128)S(1)} %convert_add_fusion) | copy-start | bytes 22020100
  186.1 41.6 %collective-permute-start.1 = (bf16[2,32,7168]{2,1,0:T(8,128)(2,1)}, bf16[2,32,7168]{2,1,0:T(8,128)(2,1)}, u32[]{:S(2)}, u32[]{:S(2)}) collective-permute-start(bf16[2,32,7168]{2,1,0:T(8,128)(2,1)} %get-tuple-element.39), channel_id=1, source_target_pairs={{0,4},{4,8},{8,12},{12,0},{1,5},{5,9},{9,13},{13,1},{2,6},{6,10},{... | collective-permute-start | bytes 2752520 | tf_op jit(solution)/shard_map/ppermute | solution.py:169
  187.6 43.2 %collective-permute-start.2 = (bf16[2,32,7168]{2,1,0:T(8,128)(2,1)}, bf16[2,32,7168]{2,1,0:T(8,128)(2,1)}, u32[]{:S(2)}, u32[]{:S(2)}) collective-permute-start(bf16[2,32,7168]{2,1,0:T(8,128)(2,1)} %get-tuple-element.41), channel_id=1, source_target_pairs={{0,8},{4,12},{8,0},{12,4},{1,9},{5,13},{9,1},{13,5},{2,10},{6,14},... | collective-permute-start | bytes 2752520 | tf_op jit(solution)/shard_map/ppermute | solution.py:169
  190.3 40.4 %collective-permute-start.3 = (bf16[2,32,7168]{2,1,0:T(8,128)(2,1)S(1)}, bf16[2,32,7168]{2,1,0:T(8,128)(2,1)}, u32[]{:S(2)}, u32[]{:S(2)}) collective-permute-start(bf16[2,32,7168]{2,1,0:T(8,128)(2,1)S(1)} %get-tuple-element.40), channel_id=1, source_target_pairs={{0,12},{4,0},{8,4},{12,8},{1,13},{5,1},{9,5},{13,9},{2,14},{6,2},{... | collective-permute-start | bytes 2752520 | tf_op jit(solution)/shard_map/ppermute | solution.py:169
  233.5 11.9 %collective-permute-start.4 = (bf16[32,7168]{1,0:T(8,128)(2,1)S(1)}, bf16[32,7168]{1,0:T(8,128)(2,1)S(1)}, u32[]{:S(2)}, u32[]{:S(2)}) collective-permute-start(bf16[32,7168]{1,0:T(8,128)(2,1)S(1)} %fusion.6), channel_id=1, source_target_pairs={{0,2},{2,0},{1,3},{3,1},{4,6},{6,4},{5,7},{7,5},{8,10},{10,8},{9,1... | collective-permute-start | bytes 1376264 | tf_op jit(solution)/shard_map/ppermute | solution.py:169
Sparse Core Ops, SparseCore 0:
  11.0 113.9 all-gather.2

commit v14 on v10

--- a/solution.py
+++ b/solution.py
@@ -63,14 +63,14 @@
             s = jnp.where(allowed, s, -jnp.inf)
         new_best = jnp.maximum(row_best, jnp.max(s, axis=1, keepdims=True))
         rescale = jnp.exp(row_best - new_best)
-        w = jnp.exp(s - new_best)
-        weight_sum = rescale * weight_sum + jnp.sum(w, axis=1, keepdims=True)
-        added = jnp.dot(w.astype(jnp.bfloat16), v_ref[c], preferred_element_type=jnp.float32)
-        return (new_best, weight_sum, rescale * numerator + added)
+        w = jnp.exp(s - new_best).astype(jnp.bfloat16)
+        sums = jnp.dot(w, jnp.ones((block_rows, numerator.shape[1]), jnp.bfloat16), preferred_element_type=jnp.float32)
+        added = jnp.dot(w, v_ref[c], preferred_element_type=jnp.float32)
+        return (new_best, rescale * weight_sum + sums, rescale * numerator + added)
 
     initial = (
         jnp.full((rows, 1), -jnp.inf, jnp.float32),
-        jnp.zeros((rows, 1), jnp.float32),
+        jnp.zeros((rows, q.shape[1]), jnp.float32),
         jnp.zeros((rows, q.shape[1]), jnp.float32),
     )
     carry = step(query_block, initial, (qseg == kseg_ref[query_block]) & (key_pos <= local_pos))

time: 251 us -> 253 us (level)
  no operation moved by 1% of the time
where the time goes in v14:
time: 253 us; the launch traced here: 252 us
  waiting for transfers between devices  142 us (56%)
  starting transfers between devices  46.1 us (18%)
  local copies, waits for them, and re-layouts  19.1 us (8%)
  other arithmetic  14.4 us (6%)
  between operations  14.3 us (6%)
  matrix products  8.12 us (3%)
  Pallas kernels  7.98 us (3%)
    all_gather x1, waiting for transfers between devices, attention(): kv_all = lax.all_gather(kv, SEQ, axis=0, tiled=False)  96.6 us
    all_to_all x1, starting transfers between devices, place_pages(): lax.all_to_all(outgoing, SEQ, split_axis=0, concat_axis=0, tiled=True)  40.3 us
    all_to_all x1, waiting for transfers between devices, place_pages(): lax.all_to_all(outgoing, SEQ, split_axis=0, concat_axis=0, tiled=True)  36.1 us
    ppermute x4, waiting for transfers between devices, exchange(): total = total + lax.ppermute(sent, name, pairs).astype(jnp.float32)  9.15 us
    dot_general x2, matrix products, reduce_rows(): jnp.dot(rows_for.reshape(-1, width), out_weight, preferred_element_type=j...  8.12 us
    pallas_call x1, Pallas kernels, attend(): pl.pallas_call(kernel, grid_spec=pltpu.PrefetchScalarGridSpec(num_scalar_...  7.98 us
    ppermute x4, starting transfers between devices, exchange(): total = total + lax.ppermute(sent, name, pairs).astype(jnp.float32)  5.7 us
    unnamed x8, local copies, waits for them, and re-layouts  5.1 us
  transfers between devices with their start and end apart: 7, of which 3 were waited for; matrix products, arithmetic and copies ran while one was open for 11% of the time, Pallas kernels for 0%

profile of v14, /device:TPU:8, one launch (start us, length us, event | category | flops | bytes accessed | tf_op | source)
XLA Modules:
  0.0 251.9 jit_solution(2267538599783202035)
XLA Ops:
  7.2 0.0 all-gather.3.cloned.1.call-start
  7.2 2.0 pad_maximum_fusion.1
  9.2 0.0 all-gather.3.cloned.1.call-update
  9.3 0.8 reshape.123
  10.1 0.8 reshape.124
  10.9 0.1 copy.40
  11.0 0.1 select_reduce_fusion.2
  11.1 0.1 iota_add_fusion
  11.2 0.1 add.133
  11.3 0.4 fusion.10
  11.7 0.1 select_reduce_fusion
  11.8 0.1 reduce_sum.31
  11.9 1.6 pad_maximum_fusion
  13.5 2.3 gather_fusion
  15.8 0.3 select_bitcast_fusion.1
  16.0 0.2 copy.41
  16.2 0.9 copy.42.qseg_ref
  17.1 0.6 fusion.16
  17.7 1.4 fusion.11
  19.1 0.7 and_select_fusion.2
  19.8 0.6 pad_add_fusion.meta_ref
  20.4 96.6 %all-gather.3.cloned.1.call-done = bf16[32,512,256]{2,1,0:T(8,128)(2,1)} async-done(((bf16[2,512,256]{2,1,0:T(8,128)(2,1)}), bf16[32,512,256]{2,1,0:T(8,128)(2,1)}) %all-gather.3.cloned.1.call-update) | async-done | bytes 8388624 | tf_op jit(solution)/shard_map/all_gather | solution.py:134
  117.0 8.0 %shard_map.120 = bf16[512,256]{1,0:T(8,128)(2,1)} custom-call(s32[17]{0:T(128)} %pad_add_fusion.meta_ref, bf16[512,256]{1,0:T(8,128)(2,1)} %q_ref.1, s32[512,1]{1,0:T(8,128)} %copy.42.qseg_ref, s32[16,1,512]{2,1,0:T(1,128)} %bitcast.80, bf16[16,2,512,256]{3,2,1,0:T(8,128)(2,1)} %bitcast.67, bf16[16,2,512,256]{3,2,1,0:T(8,128)(2,1)} %bitcast.68), custom_call_target="tpu_custom_call" | custom-call | tf_op jit(solution)/shard_map/pallas_call | solution.py:100
  125.0 1.0 constant_dynamic-slice_fusion.1
  126.0 5.0 %convolution_convert_fusion = bf16[256,7168]{1,0:T(8,128)(2,1)} fusion(bf16[256,256]{1,0:T(8,128)(2,1)S(1)} %bitcast.77, bf16[256,7168]{1,0:T(8,128)(2,1)} %param.16), kind=kOutput, calls=%fused_computation.2 | convolution fusion | flops 941359104 | bytes 7471104 | tf_op jit(solution)/shard_map/dot_general | solution.py:179
  130.9 1.6 copy.43
  132.6 40.3 %all-to-all-start = ((bf16[16,2,4,2,16,256]{5,4,3,2,1,0:T(8,128)(2,1)}), bf16[16,2,4,2,16,256]{5,4,3,2,1,0:T(8,128)(2,1)S(1)}, u32[]{:S(2)}, u32[]{:S(2)}) async-start(bf16[16,2,4,2,16,256]{5,4,3,2,1,0:T(8,128)(2,1)} %copy.43), calls=%async_computation | async-start | bytes 4194304 | tf_op jit(solution)/shard_map/all_to_all | solution.py:42
  172.9 3.2 %convolution_convert_fusion.1 = bf16[256,7168]{1,0:T(8,128)(2,1)S(1)} fusion(bf16[256,256]{1,0:T(8,128)(2,1)S(1)} %bitcast.76, bf16[256,7168]{1,0:T(8,128)(2,1)} %param.16), kind=kOutput, calls=%fused_computation.3 | convolution fusion | flops 941359104 | bytes 7471104 | tf_op jit(solution)/shard_map/dot_general | solution.py:179
  176.1 0.0 collective-permute-done
  176.1 3.3 %convert_add_fusion = f32[4,2,32,7168]{3,2,1,0:T(8,128)S(1)} fusion(bf16[4,2,32,7168]{3,2,1,0:T(8,128)(2,1)S(1)} %bitcast.69, bf16[4,2,32,7168]{3,2,1,0:T(8,128)(2,1)} %collective-permute-done), kind=kLoop, calls=%fused_computation.4 | loop fusion | flops 5505024 | bytes 14680064 | tf_op jit(solution)/shard_map/add | solution.py:183
  179.4 3.0 %copy-done = f32[4,2,32,7168]{3,2,1,0:T(8,128)} copy-done((f32[4,2,32,7168]{3,2,1,0:T(8,128)}, f32[4,2,32,7168]{3,2,1,0:T(8,128)S(1)}, u32[]{:S(2)}) %copy-start) | copy-done | bytes 7340056
  182.3 1.6 fusion.2
  183.9 1.5 collective-permute-start.1
  185.4 2.7 %collective-permute-start.2 = (bf16[2,32,7168]{2,1,0:T(8,128)(2,1)}, bf16[2,32,7168]{2,1,0:T(8,128)(2,1)}, u32[]{:S(2)}, u32[]{:S(2)}) collective-permute-start(bf16[2,32,7168]{2,1,0:T(8,128)(2,1)} %get-tuple-element.37), channel_id=1, source_target_pairs={{0,8},{4,12},{8,0},{12,4},{1,9},{5,13},{9,1},{13,5},{2,10},{6,14},... | collective-permute-start | bytes 2752520 | tf_op jit(solution)/shard_map/ppermute | solution.py:165
  188.1 1.4 collective-permute-start.3
  189.5 0.1 select_reduce_fusion.1
  189.7 36.1 %all-to-all-done = bf16[16,2,4,2,16,256]{5,4,3,2,1,0:T(8,128)(2,1)S(1)} async-done(((bf16[16,2,4,2,16,256]{5,4,3,2,1,0:T(8,128)(2,1)}), bf16[16,2,4,2,16,256]{5,4,3,2,1,0:T(8,128)(2,1)S(1)}, u32[]{:S(2)}, u32[]{:S(2)}) %all-to-all-start) | async-done | bytes 2097184 | tf_op jit(solution)/shard_map/all_to_all | solution.py:42
  225.7 1.6 copy.44
  227.3 2.3 gather_fusion.1
  229.6 2.7 %fusion.1 = f32[2,32,7168]{2,1,0:T(8,128)S(1)} fusion(bf16[2,32,7168]{2,1,0:T(8,128)(2,1)} %collective-permute-done.3, bf16[2,32,7168]{2,1,0:T(8,128)(2,1)} %collective-permute-done.2, bf16[2,32,7168]{2,1,0:T(8,128)(2,1)} %collective-permute-done.1, f32[4,2,32,7168]{3,2,1,0:T(8,128)} %copy-done, s32[]{:T(128)S(6)} %select_n.123), kind=kLoop, calls=%fused_computation.10 | loop fusion | flops 2752512 | bytes 6422532 | tf_op jit(solution)/shard_map/add | solution.py:165
  232.4 0.1 fusion.6
  232.4 0.1 collective-permute-start.4
  232.5 0.3 select_bitcast_fusion
  232.8 0.1 slice_bitcast_fusion
  232.9 1.1 copy.45
  234.0 1.1 copy.46
  235.1 9.1 %collective-permute-done.4 = bf16[32,7168]{1,0:T(8,128)(2,1)S(1)} collective-permute-done((bf16[32,7168]{1,0:T(8,128)(2,1)S(1)}, bf16[32,7168]{1,0:T(8,128)(2,1)S(1)}, u32[]{:S(2)}, u32[]{:S(2)}) %collective-permute-start.4) | collective-permute-done | bytes 458784 | tf_op jit(solution)/shard_map/ppermute | solution.py:165
  244.2 0.8 fusion.5
  (19 shorter events, 0.1 us)
Async XLA Ops:
  7.2 4.7 %copy-start.2 = (bf16[4,512,256]{2,1,0:T(8,128)(2,1)S(1)}, bf16[4,512,256]{2,1,0:T(8,128)(2,1)}, u32[]{:S(2)}) copy-start(bf16[4,512,256]{2,1,0:T(8,128)(2,1)} %param.17) | copy-start | bytes 3145732
  7.2 4.7 %copy-start.1 = (bf16[4,512,256]{2,1,0:T(8,128)(2,1)S(1)}, bf16[4,512,256]{2,1,0:T(8,128)(2,1)}, u32[]{:S(2)}) copy-start(bf16[4,512,256]{2,1,0:T(8,128)(2,1)} %param.18) | copy-start | bytes 3145732
  7.2 109.8 %all-gather.3.cloned.1.call-start = ((), (), s32[]{:S(2)}) async-start(), calls=%async_computation.1 | async-start | bytes 8912896 | tf_op jit(solution)/shard_map/all_gather | solution.py:134
  130.9 45.1 %collective-permute-start = (bf16[4,2,32,7168]{3,2,1,0:T(8,128)(2,1)}, bf16[4,2,32,7168]{3,2,1,0:T(8,128)(2,1)}, u32[]{:S(2)}, u32[]{:S(2)}) collective-permute-start(bf16[4,2,32,7168]{3,2,1,0:T(8,128)(2,1)} %bitcast.20), channel_id=1, source_target_pairs={{0,1},{1,0},{2,3},{3,2},{4,5},{5,4},{6,7},{7,6},{8,9},{9,8},{10,11... | collective-permute-start | bytes 11010056 | tf_op jit(solution)/shard_map/ppermute | solution.py:183
  132.6 93.2 %all-to-all-start = ((bf16[16,2,4,2,16,256]{5,4,3,2,1,0:T(8,128)(2,1)}), bf16[16,2,4,2,16,256]{5,4,3,2,1,0:T(8,128)(2,1)S(1)}, u32[]{:S(2)}, u32[]{:S(2)}) async-start(bf16[16,2,4,2,16,256]{5,4,3,2,1,0:T(8,128)(2,1)} %copy.43), calls=%async_computation | async-start | bytes 4194304 | tf_op jit(solution)/shard_map/all_to_all | solution.py:42
  179.4 3.0 %copy-start = (f32[4,2,32,7168]{3,2,1,0:T(8,128)}, f32[4,2,32,7168]{3,2,1,0:T(8,128)S(1)}, u32[]{:S(2)}) copy-start(f32[4,2,32,7168]{3,2,1,0:T(8,128)S(1)} %convert_add_fusion) | copy-start | bytes 22020100
  183.9 45.7 %collective-permute-start.1 = (bf16[2,32,7168]{2,1,0:T(8,128)(2,1)}, bf16[2,32,7168]{2,1,0:T(8,128)(2,1)}, u32[]{:S(2)}, u32[]{:S(2)}) collective-permute-start(bf16[2,32,7168]{2,1,0:T(8,128)(2,1)} %get-tuple-element.35), channel_id=1, source_target_pairs={{0,4},{4,8},{8,12},{12,0},{1,5},{5,9},{9,13},{13,1},{2,6},{6,10},{... | collective-permute-start | bytes 2752520 | tf_op jit(solution)/shard_map/ppermute | solution.py:165
  185.4 44.2 %collective-permute-start.2 = (bf16[2,32,7168]{2,1,0:T(8,128)(2,1)}, bf16[2,32,7168]{2,1,0:T(8,128)(2,1)}, u32[]{:S(2)}, u32[]{:S(2)}) collective-permute-start(bf16[2,32,7168]{2,1,0:T(8,128)(2,1)} %get-tuple-element.37), channel_id=1, source_target_pairs={{0,8},{4,12},{8,0},{12,4},{1,9},{5,13},{9,1},{13,5},{2,10},{6,14},... | collective-permute-start | bytes 2752520 | tf_op jit(solution)/shard_map/ppermute | solution.py:165
  188.1 41.5 %collective-permute-start.3 = (bf16[2,32,7168]{2,1,0:T(8,128)(2,1)S(1)}, bf16[2,32,7168]{2,1,0:T(8,128)(2,1)}, u32[]{:S(2)}, u32[]{:S(2)}) collective-permute-start(bf16[2,32,7168]{2,1,0:T(8,128)(2,1)S(1)} %get-tuple-element.36), channel_id=1, source_target_pairs={{0,12},{4,0},{8,4},{12,8},{1,13},{5,1},{9,5},{13,9},{2,14},{6,2},{... | collective-permute-start | bytes 2752520 | tf_op jit(solution)/shard_map/ppermute | solution.py:165
  232.4 11.8 %collective-permute-start.4 = (bf16[32,7168]{1,0:T(8,128)(2,1)S(1)}, bf16[32,7168]{1,0:T(8,128)(2,1)S(1)}, u32[]{:S(2)}, u32[]{:S(2)}) collective-permute-start(bf16[32,7168]{1,0:T(8,128)(2,1)S(1)} %fusion.6), channel_id=1, source_target_pairs={{0,2},{2,0},{1,3},{3,1},{4,6},{6,4},{5,7},{7,5},{8,10},{10,8},{9,1... | collective-permute-start | bytes 1376264 | tf_op jit(solution)/shard_map/ppermute | solution.py:165
Sparse Core Ops, SparseCore 0:
  11.0 105.9 all-gather.2

commit v15 on v10

--- a/solution.py
+++ b/solution.py
@@ -115,6 +115,25 @@
     )(meta, queries, qseg, kseg, kv, kv)
 
 
+def stack_kernel(k_ref, v_ref, o_ref, sems):
+    copies = [pltpu.make_async_copy(ref, o_ref.at[i], sems.at[i]) for i, ref in enumerate((k_ref, v_ref))]
+    for copy in copies:
+        copy.start()
+    for copy in copies:
+        copy.wait()
+
+
+def stack_pair(first, second):
+    anywhere = pl.BlockSpec(memory_space=pl.ANY)
+    return pl.pallas_call(
+        stack_kernel,
+        in_specs=[anywhere, anywhere],
+        out_specs=anywhere,
+        scratch_shapes=[pltpu.SemaphoreType.DMA((2,))],
+        out_shape=jax.ShapeDtypeStruct((2, *first.shape), first.dtype),
+    )(first, second)
+
+
 def attention(queries, stretch_keys, stretch_values, segment_ids, block_live, moved):
     position = lax.axis_index(SEQ)
     block_count = lax.axis_size(SEQ)
@@ -130,7 +149,7 @@
     meta = jnp.concatenate([flags, position.astype(jnp.int32)[None]])
     qseg = query_seg[:, None]
     kseg = seg_blocks[:, None, :]
-    kv = jnp.stack([stretch_keys, stretch_values])
+    kv = stack_pair(stretch_keys, stretch_values)
     kv_all = lax.all_gather(kv, SEQ, axis=0, tiled=False)
     moved, kv_all = lax.optimization_barrier((moved, kv_all))
     return (attend(meta, queries, qseg, kseg, kv_all), moved)

time: 251 us -> 263 us (1.048)
  Pallas kernels: 7.49 us -> 24.5 us
    pallas_call x0 -> x1, Pallas kernels: none -> 17 us  [stack_pair(): pl.pallas_call(stack_kernel, in_specs=[anywhere, anywhere], out_specs=any...]
  transfers between devices with their start and end apart: 7 -> 7, of which waited for: 3 -> 3; matrix products, arithmetic and copies ran while one was open for 11% -> 10% of each run, Pallas kernels for 0% -> 0%
where the time goes in v15:
time: 263 us
  waiting for transfers between devices  141 us (54%)
  starting transfers between devices  44.3 us (17%)
  Pallas kernels  24.5 us (9%)
  local copies, waits for them, and re-layouts  19.1 us (7%)
  between operations  14.3 us (5%)
  other arithmetic  12.4 us (5%)
  matrix products  8.12 us (3%)
    all_gather x1, waiting for transfers between devices, attention(): kv_all = lax.all_gather(kv, SEQ, axis=0, tiled=False)  95 us
    all_to_all x1, starting transfers between devices, place_pages(): lax.all_to_all(outgoing, SEQ, split_axis=0, concat_axis=0, tiled=True)  38.6 us
    all_to_all x1, waiting for transfers between devices, place_pages(): lax.all_to_all(outgoing, SEQ, split_axis=0, concat_axis=0, tiled=True)  36.3 us
    pallas_call x1, Pallas kernels, stack_pair(): pl.pallas_call(stack_kernel, in_specs=[anywhere, anywhere], out_specs=any...  17 us
    ppermute x4, waiting for transfers between devices, exchange(): total = total + lax.ppermute(sent, name, pairs).astype(jnp.float32)  9.39 us
    dot_general x2, matrix products, reduce_rows(): jnp.dot(rows_for.reshape(-1, width), out_weight, preferred_element_type=j...  8.12 us
    pallas_call x1, Pallas kernels, attend(): pl.pallas_call(kernel, grid_spec=pltpu.PrefetchScalarGridSpec(num_scalar_...  7.5 us
    ppermute x4, starting transfers between devices, exchange(): total = total + lax.ppermute(sent, name, pairs).astype(jnp.float32)  5.67 us
  transfers between devices with their start and end apart: 7, of which 3 were waited for; matrix products, arithmetic and copies ran while one was open for 10% of the time, Pallas kernels for 0%

profile of v15, /device:TPU:8, one launch (start us, length us, event | category | flops | bytes accessed | tf_op | source)
XLA Modules:
  0.0 263.4 jit_solution(7306845690427353473)
XLA Ops:
  7.2 0.0 all-gather.3.cloned.1.call-start
  7.2 17.0 %shard_map.120 = bf16[2,512,256]{2,1,0:T(8,128)(2,1)} custom-call(bf16[512,256]{1,0:T(8,128)(2,1)} %k_ref.1, bf16[512,256]{1,0:T(8,128)(2,1)} %v_ref.1), custom_call_target="tpu_custom_call" | custom-call | tf_op jit(solution)/shard_map/pallas_call | solution.py:128
  24.2 0.0 all-gather.3.cloned.1.call-update
  24.3 0.8 reshape.123
  25.1 0.8 reshape.124
  25.9 0.1 copy.40
  26.0 0.1 select_reduce_fusion.2
  26.1 0.1 iota_add_fusion
  26.2 0.1 add.133
  26.3 0.4 fusion.10
  26.7 0.1 select_reduce_fusion
  26.8 0.1 reduce_sum.31
  26.9 1.6 pad_maximum_fusion
  28.5 2.3 gather_fusion
  30.8 0.3 select_bitcast_fusion.1
  31.0 0.2 copy.41
  31.2 0.9 copy.42.qseg_ref
  32.1 0.6 fusion.16
  32.7 1.4 fusion.11
  34.1 0.7 and_select_fusion.2
  34.8 0.6 pad_add_fusion.meta_ref
  35.4 95.0 %all-gather.3.cloned.1.call-done = bf16[32,512,256]{2,1,0:T(8,128)(2,1)} async-done(((bf16[2,512,256]{2,1,0:T(8,128)(2,1)}), bf16[32,512,256]{2,1,0:T(8,128)(2,1)}) %all-gather.3.cloned.1.call-update) | async-done | bytes 8388624 | tf_op jit(solution)/shard_map/all_gather | solution.py:153
  130.4 7.5 %shard_map.121 = bf16[512,256]{1,0:T(8,128)(2,1)} custom-call(s32[17]{0:T(128)} %pad_add_fusion.meta_ref, bf16[512,256]{1,0:T(8,128)(2,1)} %q_ref.1, s32[512,1]{1,0:T(8,128)} %copy.42.qseg_ref, s32[16,1,512]{2,1,0:T(1,128)} %bitcast.76, bf16[16,2,512,256]{3,2,1,0:T(8,128)(2,1)} %bitcast.65, bf16[16,2,512,256]{3,2,1,0:T(8,128)(2,1)} %bitcast.66), custom_call_target="tpu_custom_call" | custom-call | tf_op jit(solution)/shard_map/pallas_call | solution.py:100
  137.9 1.0 constant_dynamic-slice_fusion.1
  138.9 5.0 %convolution_convert_fusion = bf16[256,7168]{1,0:T(8,128)(2,1)} fusion(bf16[256,256]{1,0:T(8,128)(2,1)S(1)} %bitcast.75, bf16[256,7168]{1,0:T(8,128)(2,1)} %param.16), kind=kOutput, calls=%fused_computation.2 | convolution fusion | flops 941359104 | bytes 7471104 | tf_op jit(solution)/shard_map/dot_general | solution.py:198
  143.8 0.0 collective-permute-start
  143.8 1.6 copy.43
  145.4 38.6 %all-to-all-start = ((bf16[16,2,4,2,16,256]{5,4,3,2,1,0:T(8,128)(2,1)}), bf16[16,2,4,2,16,256]{5,4,3,2,1,0:T(8,128)(2,1)S(1)}, u32[]{:S(2)}, u32[]{:S(2)}) async-start(bf16[16,2,4,2,16,256]{5,4,3,2,1,0:T(8,128)(2,1)} %copy.43), calls=%async_computation | async-start | bytes 4194304 | tf_op jit(solution)/shard_map/all_to_all | solution.py:42
  184.0 3.2 %convolution_convert_fusion.1 = bf16[256,7168]{1,0:T(8,128)(2,1)S(1)} fusion(bf16[256,256]{1,0:T(8,128)(2,1)S(1)} %bitcast.74, bf16[256,7168]{1,0:T(8,128)(2,1)} %param.16), kind=kOutput, calls=%fused_computation.3 | convolution fusion | flops 941359104 | bytes 7471104 | tf_op jit(solution)/shard_map/dot_general | solution.py:198
  187.2 3.3 %convert_add_fusion = f32[4,2,32,7168]{3,2,1,0:T(8,128)S(1)} fusion(bf16[4,2,32,7168]{3,2,1,0:T(8,128)(2,1)S(1)} %bitcast.67, bf16[4,2,32,7168]{3,2,1,0:T(8,128)(2,1)} %collective-permute-done), kind=kLoop, calls=%fused_computation.4 | loop fusion | flops 5505024 | bytes 14680064 | tf_op jit(solution)/shard_map/add | solution.py:202
  190.5 3.0 %copy-done = f32[4,2,32,7168]{3,2,1,0:T(8,128)} copy-done((f32[4,2,32,7168]{3,2,1,0:T(8,128)}, f32[4,2,32,7168]{3,2,1,0:T(8,128)S(1)}, u32[]{:S(2)}) %copy-start) | copy-done | bytes 7340056
  193.4 1.6 fusion.2
  195.0 1.5 collective-permute-start.1
  196.6 2.6 collective-permute-start.2
  199.1 1.5 collective-permute-start.3
  200.6 0.1 select_reduce_fusion.1
  200.7 36.3 %all-to-all-done = bf16[16,2,4,2,16,256]{5,4,3,2,1,0:T(8,128)(2,1)S(1)} async-done(((bf16[16,2,4,2,16,256]{5,4,3,2,1,0:T(8,128)(2,1)}), bf16[16,2,4,2,16,256]{5,4,3,2,1,0:T(8,128)(2,1)S(1)}, u32[]{:S(2)}, u32[]{:S(2)}) %all-to-all-start) | async-done | bytes 2097184 | tf_op jit(solution)/shard_map/all_to_all | solution.py:42
  237.0 1.6 copy.44
  238.6 2.3 gather_fusion.1
  240.9 2.7 %fusion.1 = f32[2,32,7168]{2,1,0:T(8,128)S(1)} fusion(bf16[2,32,7168]{2,1,0:T(8,128)(2,1)} %collective-permute-done.3, bf16[2,32,7168]{2,1,0:T(8,128)(2,1)} %collective-permute-done.2, bf16[2,32,7168]{2,1,0:T(8,128)(2,1)} %collective-permute-done.1, f32[4,2,32,7168]{3,2,1,0:T(8,128)} %copy-done, s32[]{:T(128)S(6)} %select_n.123), kind=kLoop, calls=%fused_computation.10 | loop fusion | flops 2752512 | bytes 6422532 | tf_op jit(solution)/shard_map/add | solution.py:184
  243.6 0.1 fusion.6
  243.7 0.1 collective-permute-start.4
  243.8 0.3 select_bitcast_fusion
  244.1 0.1 slice_bitcast_fusion
  244.2 1.1 copy.45
  245.3 1.1 copy.46
  246.4 9.4 %collective-permute-done.4 = bf16[32,7168]{1,0:T(8,128)(2,1)S(1)} collective-permute-done((bf16[32,7168]{1,0:T(8,128)(2,1)S(1)}, bf16[32,7168]{1,0:T(8,128)(2,1)S(1)}, u32[]{:S(2)}, u32[]{:S(2)}) %collective-permute-start.4) | collective-permute-done | bytes 458784 | tf_op jit(solution)/shard_map/ppermute | solution.py:184
  255.7 0.8 fusion.5
  (19 shorter events, 0.1 us)
Async XLA Ops:
  7.2 19.7 %copy-start.2 = (bf16[4,512,256]{2,1,0:T(8,128)(2,1)S(1)}, bf16[4,512,256]{2,1,0:T(8,128)(2,1)}, u32[]{:S(2)}) copy-start(bf16[4,512,256]{2,1,0:T(8,128)(2,1)} %param.17) | copy-start | bytes 3145732
  7.2 19.7 %copy-start.1 = (bf16[4,512,256]{2,1,0:T(8,128)(2,1)S(1)}, bf16[4,512,256]{2,1,0:T(8,128)(2,1)}, u32[]{:S(2)}) copy-start(bf16[4,512,256]{2,1,0:T(8,128)(2,1)} %param.18) | copy-start | bytes 3145732
  7.2 123.2 %all-gather.3.cloned.1.call-start = ((), (), s32[]{:S(2)}) async-start(), calls=%async_computation.1 | async-start | bytes 8912896 | tf_op jit(solution)/shard_map/all_gather | solution.py:153
  143.8 43.4 %collective-permute-start = (bf16[4,2,32,7168]{3,2,1,0:T(8,128)(2,1)}, bf16[4,2,32,7168]{3,2,1,0:T(8,128)(2,1)}, u32[]{:S(2)}, u32[]{:S(2)}) collective-permute-start(bf16[4,2,32,7168]{3,2,1,0:T(8,128)(2,1)} %bitcast.18), channel_id=1, source_target_pairs={{0,1},{1,0},{2,3},{3,2},{4,5},{5,4},{6,7},{7,6},{8,9},{9,8},{10,11... | collective-permute-start | bytes 11010056 | tf_op jit(solution)/shard_map/ppermute | solution.py:202
  145.4 91.6 %all-to-all-start = ((bf16[16,2,4,2,16,256]{5,4,3,2,1,0:T(8,128)(2,1)}), bf16[16,2,4,2,16,256]{5,4,3,2,1,0:T(8,128)(2,1)S(1)}, u32[]{:S(2)}, u32[]{:S(2)}) async-start(bf16[16,2,4,2,16,256]{5,4,3,2,1,0:T(8,128)(2,1)} %copy.43), calls=%async_computation | async-start | bytes 4194304 | tf_op jit(solution)/shard_map/all_to_all | solution.py:42
  190.5 3.0 %copy-start = (f32[4,2,32,7168]{3,2,1,0:T(8,128)}, f32[4,2,32,7168]{3,2,1,0:T(8,128)S(1)}, u32[]{:S(2)}) copy-start(f32[4,2,32,7168]{3,2,1,0:T(8,128)S(1)} %convert_add_fusion) | copy-start | bytes 22020100
  195.0 45.9 %collective-permute-start.1 = (bf16[2,32,7168]{2,1,0:T(8,128)(2,1)}, bf16[2,32,7168]{2,1,0:T(8,128)(2,1)}, u32[]{:S(2)}, u32[]{:S(2)}) collective-permute-start(bf16[2,32,7168]{2,1,0:T(8,128)(2,1)} %get-tuple-element.35), channel_id=1, source_target_pairs={{0,4},{4,8},{8,12},{12,0},{1,5},{5,9},{9,13},{13,1},{2,6},{6,10},{... | collective-permute-start | bytes 2752520 | tf_op jit(solution)/shard_map/ppermute | solution.py:184
  196.6 44.4 %collective-permute-start.2 = (bf16[2,32,7168]{2,1,0:T(8,128)(2,1)}, bf16[2,32,7168]{2,1,0:T(8,128)(2,1)}, u32[]{:S(2)}, u32[]{:S(2)}) collective-permute-start(bf16[2,32,7168]{2,1,0:T(8,128)(2,1)} %get-tuple-element.37), channel_id=1, source_target_pairs={{0,8},{4,12},{8,0},{12,4},{1,9},{5,13},{9,1},{13,5},{2,10},{6,14},... | collective-permute-start | bytes 2752520 | tf_op jit(solution)/shard_map/ppermute | solution.py:184
  199.1 41.8 %collective-permute-start.3 = (bf16[2,32,7168]{2,1,0:T(8,128)(2,1)S(1)}, bf16[2,32,7168]{2,1,0:T(8,128)(2,1)}, u32[]{:S(2)}, u32[]{:S(2)}) collective-permute-start(bf16[2,32,7168]{2,1,0:T(8,128)(2,1)S(1)} %get-tuple-element.36), channel_id=1, source_target_pairs={{0,12},{4,0},{8,4},{12,8},{1,13},{5,1},{9,5},{13,9},{2,14},{6,2},{... | collective-permute-start | bytes 2752520 | tf_op jit(solution)/shard_map/ppermute | solution.py:184
  243.7 12.0 %collective-permute-start.4 = (bf16[32,7168]{1,0:T(8,128)(2,1)S(1)}, bf16[32,7168]{1,0:T(8,128)(2,1)S(1)}, u32[]{:S(2)}, u32[]{:S(2)}) collective-permute-start(bf16[32,7168]{1,0:T(8,128)(2,1)S(1)} %fusion.6), channel_id=1, source_target_pairs={{0,2},{2,0},{1,3},{3,1},{4,6},{6,4},{5,7},{7,5},{8,10},{10,8},{9,1... | collective-permute-start | bytes 1376264 | tf_op jit(solution)/shard_map/ppermute | solution.py:184
Sparse Core Ops, SparseCore 0:
  24.4 105.9 all-gather.2
